TPU v7x, 512 devices: a whole 4x4x16 slice. The times are simulated.
512 devices in a mesh: phase: 8 (over y, core), ctx: 64 (over z, x).
Axes of the slice: x: 4, y: 4, z: 16, core: 2. Of those that a mesh axis runs over, the one named last changes fastest.
Arguments:
- mixer_input: bfloat16 [8, 8192, 4096], P('phase', 'ctx'), may hold values from -6 to 6
- state_proj: bfloat16 [8, 8192, 2048], P('phase', 'ctx'), may hold values from -6 to 6
- dt_raw: bfloat16 [8, 8192, 64], P('phase', 'ctx'), may hold values from -4 to 4
- decay_rate: float32 [8, 64], P('phase'), may hold values from 0.00048828125 to 0.05
- dt_bias: float32 [8, 64], P('phase'), may hold values from -1 to 1
- skip_gain: float32 [8, 64], P('phase'), may hold values from 0.5 to 1.5
- mamba_gain: float32 [8, 4096], P('phase'), may hold values from 0.5 to 1.5
- keys_values: bfloat16 [8, 8192, 512], P('phase', 'ctx'), may hold values from -160 to 160
- attn_gain: float32 [8, 4096], P('phase'), may hold values from 0.5 to 1.5
- documents: int32 [8, 8192], P('phase'), may hold values from 0 to 31, never falling along the last dimension, each value on 1 to 512 neighbouring positions
- placement_perm: int32 [64], replicated, may hold values from 0 to 63, each once
Outputs:
- handed: bfloat16 [8, 8192, 4096], P('phase', 'ctx')
Inputs may be any that keep to these rules, and one draw needn't show every extreme that they name: Positions 128 placement_perm[d] to 128 placement_perm[d] + 127 lie at index d of ctx; every block once. Each phase's window holds 32 documents in order, each of 1 to 512 positions, one of exactly 512.
All inputs are finite; a program needn't handle non-finite values.
Results may differ from a plain program's by a relative error of at most 0.012.
Values may be sent and summed in bfloat16 or wider, within the bound.
No kernel may reach another device: no remote copies, remote signals or barrier semaphores. Data moves between devices by JAX's collectives and lax.ppermute only.
A program may use at most 128 MiB of HBM per device.

v0:
```python
import math

import jax
import jax.numpy as jnp
from jax import lax
from jax.sharding import PartitionSpec as P

HEADS = 64
HEAD_DIM = 64
GROUPS = 8
STATE = 128
QHEADS = 32
KVHEADS = 2
QDIM = 128


precise = lax.Precision.HIGHEST
epsilon = 1e-05


def passed_along(value, axis, steps):
    count = lax.axis_size(axis)
    pairs = [(source, (source + steps) % count) for source in range(count)]
    return lax.ppermute(value, axis, pairs)


def group_norm(values, gain):
    grouped = values.reshape(values.shape[0], GROUPS, -1)
    normed = grouped * lax.rsqrt(jnp.mean(grouped * grouped, axis=-1, keepdims=True) + epsilon)
    return normed.reshape(values.shape) * gain


def local_terms(values, inject, readout, step_sizes, decay_rates, segs):
    blocks = values.shape[0]
    length = values.shape[1]
    heads_here = values.shape[2]
    groups_here = inject.shape[2]
    within = heads_here // groups_here
    cum_log = jnp.cumsum(-decay_rates * step_sizes, axis=1)
    spread = cum_log[:, :, None, :] - cum_log[:, None, :, :]
    positions = jnp.arange(length)
    allowed = (positions[:, None] >= positions[None, :])[None] & (
        segs[:, :, None] == segs[:, None, :]
    )
    decays = jnp.where(allowed[..., None], jnp.exp(jnp.minimum(spread, 0.0)), 0.0)
    scores = jnp.einsum("nigs,njgs->nijg", readout, inject, preferred_element_type=jnp.float32)
    weights = decays.reshape(blocks, length, length, groups_here, within) * scores[..., None]
    scaled = (values * step_sizes[..., None]).reshape(blocks, length, groups_here, within, HEAD_DIM)
    local_out = jnp.einsum("nijgk,njgkp->nigkp", weights, scaled, precision=precise).reshape(
        values.shape
    )
    ending = cum_log[:, -1]
    last_seg = segs[:, -1]
    to_end = jnp.where(
        (segs == last_seg[:, None])[..., None], jnp.exp(ending[:, None, :] - cum_log), 0.0
    )
    weighted = scaled * to_end.reshape(blocks, length, groups_here, within)[..., None]
    states = jnp.einsum(
        "njgkp,njgs->ngkps", weighted, inject.astype(jnp.float32), precision=precise
    )
    return (local_out, states.reshape(blocks, heads_here, HEAD_DIM, STATE), cum_log, ending)


def combine_blocks(states, ending, seg_end, seg_prev):
    running = jnp.cumsum(ending, axis=0)
    before = jnp.concatenate([jnp.zeros_like(running[:1]), running[:-1]], axis=0)
    positions = jnp.arange(ending.shape[0])
    linked = (positions[None, :] < positions[:, None]) & (seg_end[None, :] == seg_prev[:, None])
    factors = jnp.where(
        linked[..., None], jnp.exp(jnp.minimum(before[:, None, :] - running[None, :, :], 0.0)), 0.0
    )
    return jnp.einsum("cdh,dhps->chps", factors, states, precision=precise)


def inter_terms(readout, entering, cum_log, segs, previous):
    blocks = readout.shape[0]
    length = readout.shape[1]
    groups_here = readout.shape[2]
    heads_here = entering.shape[1]
    within = heads_here // groups_here
    reach_mask = jnp.where((segs == previous[:, None])[..., None], jnp.exp(cum_log), 0.0)
    grouped = entering.reshape(blocks, groups_here, within, HEAD_DIM, STATE)
    read_out = jnp.einsum(
        "nigs,ngkps->nigkp", readout.astype(jnp.float32), grouped, precision=precise
    )
    return read_out.reshape(blocks, length, heads_here, HEAD_DIM) * reach_mask[..., None]


def on_device(
    mixer_input,
    state_proj,
    dt_raw,
    decay_rate,
    dt_bias,
    skip_gain,
    mamba_gain,
    keys_values,
    attn_gain,
    documents,
    placement_perm,
):
    devices = lax.axis_size("ctx")
    myself = lax.axis_index("ctx")
    per_dev = HEADS // devices
    tok_rows = mixer_input.shape[1]
    total_rows = documents.shape[1]
    inverse = (
        jnp.zeros((devices,), jnp.int32)
        .at[placement_perm]
        .set(jnp.arange(devices, dtype=jnp.int32))
    )
    segment = documents[0]
    block_seg = segment.reshape(devices, tok_rows)
    seg_end = block_seg[:, -1]
    seg_prev = jnp.concatenate([jnp.full((1,), -1, jnp.int32), seg_end[:-1]])
    my_block = placement_perm[myself]
    my_seg = lax.dynamic_slice_in_dim(segment, my_block * tok_rows, tok_rows, 0)
    inputs = mixer_input[0]
    projections = state_proj[0]
    raw_steps = dt_raw[0]
    decay_rates = decay_rate[0]
    biases = dt_bias[0]
    skip_terms = skip_gain[0]
    sharers = devices // GROUPS
    copies = jnp.broadcast_to(
        projections.reshape(tok_rows, GROUPS, 1, 2 * STATE), (tok_rows, GROUPS, sharers, 2 * STATE)
    )
    copies = copies.reshape(tok_rows, devices * 2 * STATE)
    head_in, head_proj, head_raw = (
        lax.all_to_all(inputs, "ctx", split_axis=1, concat_axis=0, tiled=True),
        lax.all_to_all(copies, "ctx", split_axis=1, concat_axis=0, tiled=True),
        lax.all_to_all(raw_steps, "ctx", split_axis=1, concat_axis=0, tiled=True),
    )
    head_in = head_in.reshape(devices, tok_rows, per_dev, HEAD_DIM)[inverse]
    paired = head_proj.reshape(devices, tok_rows, 1, 2, STATE)[inverse]
    head_raw = head_raw.reshape(devices, tok_rows, per_dev)[inverse]
    values = head_in.astype(jnp.float32)
    inject = paired[:, :, :, 0]
    readout = paired[:, :, :, 1]
    my_rates = lax.dynamic_slice_in_dim(decay_rates, myself * per_dev, per_dev, 0)
    my_biases = lax.dynamic_slice_in_dim(biases, myself * per_dev, per_dev, 0)
    my_skips = lax.dynamic_slice_in_dim(skip_terms, myself * per_dev, per_dev, 0)
    step_sizes = jax.nn.softplus(head_raw.astype(jnp.float32) + my_biases)
    local_out, states, cum_log, ending = local_terms(
        values, inject, readout, step_sizes, my_rates, block_seg
    )
    entering = combine_blocks(states, ending, seg_end, seg_prev)
    outputs = (
        local_out
        + inter_terms(readout, entering, cum_log, block_seg, seg_prev)
        + my_skips[:, None] * values
    )
    outputs = outputs.astype(jnp.bfloat16).reshape(devices, tok_rows, per_dev * HEAD_DIM)[
        placement_perm
    ]
    outputs = outputs.reshape(total_rows, per_dev * HEAD_DIM)
    mamba_out = lax.all_to_all(outputs, "ctx", split_axis=0, concat_axis=1, tiled=True)
    residual = inputs.astype(jnp.float32) + group_norm(mamba_out.astype(jnp.float32), mamba_gain[0])
    hidden = residual.astype(jnp.bfloat16)
    repeat = QHEADS // KVHEADS
    queries = hidden.reshape(tok_rows, KVHEADS, repeat, QDIM)
    query_pos = my_block * tok_rows + jnp.arange(tok_rows, dtype=jnp.int32)
    score_scale = 1.0 / math.sqrt(QDIM)
    initial = (
        jnp.full((KVHEADS, repeat, tok_rows), -1e30, jnp.float32),
        jnp.zeros((KVHEADS, repeat, tok_rows), jnp.float32),
        jnp.zeros((KVHEADS, repeat, tok_rows, QDIM), jnp.float32),
    )
    piece = lax.all_gather(keys_values[0], "ctx", axis=0, tiled=True)
    blocks = piece.shape[0] // tok_rows
    pieces = piece.reshape(blocks, tok_rows, 2, KVHEADS, QDIM)
    firsts = jnp.arange(blocks, dtype=jnp.int32)

    def one_block(running, element):
        block_kv, source = element
        key_pos = placement_perm[source] * tok_rows + jnp.arange(tok_rows, dtype=jnp.int32)
        key_seg = jnp.take(segment, key_pos)
        allowed = (my_seg[:, None] == key_seg[None, :]) & (key_pos[None, :] <= query_pos[:, None])

        def update(previous):
            best_score, total_weight, accumulated = previous
            logits = (
                jnp.einsum(
                    "tgrd,kgd->grtk", queries, block_kv[:, 0], preferred_element_type=jnp.float32
                )
                * score_scale
            )
            logits = jnp.where(allowed, logits, -1e30)
            new_best = jnp.maximum(best_score, jnp.max(logits, axis=-1))
            shrink = jnp.exp(best_score - new_best)
            probabilities = jnp.where(allowed, jnp.exp(logits - new_best[..., None]), 0.0)
            total_weight = total_weight * shrink + jnp.sum(probabilities, axis=-1)
            blended = jnp.einsum(
                "grtk,kgd->grtd",
                probabilities.astype(jnp.bfloat16),
                block_kv[:, 1],
                preferred_element_type=jnp.float32,
            )
            accumulated = accumulated * shrink[..., None] + blended
            return (new_best, total_weight, accumulated)

        def unchanged(previous):
            return previous

        return (lax.cond(jnp.any(allowed), update, unchanged, running), None)

    best_score, total_weight, accumulated = lax.scan(one_block, initial, (pieces, firsts))[0]
    attended = (
        (accumulated / total_weight[..., None])
        .transpose(2, 0, 1, 3)
        .reshape(tok_rows, QHEADS * QDIM)
    )
    normed = (
        attended
        * lax.rsqrt(jnp.mean(attended * attended, axis=-1, keepdims=True) + epsilon)
        * attn_gain[0]
    )
    result = (hidden.astype(jnp.float32) + normed).astype(jnp.bfloat16)
    return passed_along(result[None], "phase", 1)


def solution(mesh):
    in_specs = (
        P("phase", "ctx", None),
        P("phase", "ctx", None),
        P("phase", "ctx", None),
        P("phase", None),
        P("phase", None),
        P("phase", None),
        P("phase", None),
        P("phase", "ctx", None),
        P("phase", None),
        P("phase", None),
        P(),
    )
    out_specs = P("phase", "ctx", None)
    return jax.shard_map(
        on_device, mesh=mesh, in_specs=in_specs, out_specs=out_specs, check_vma=False
    )
```

profile of v0, /device:TPU:6, one launch (start us, length us, event | category | flops | bytes accessed | tf_op | source)
XLA Modules:
  0.0 888.9 jit_solution(3348212587797685383)
XLA Ops:
  6.5 1.4 copy.106
  7.9 18.6 %all-to-all-start.1 = ((bf16[128,64,1]{0,2,1:T(2,128)(2,1)}), bf16[128,64,1]{0,2,1:T(2,128)(2,1)S(1)}, u32[]{:S(2)}, u32[]{:S(2)}) async-start(bf16[128,64,1]{0,2,1:T(2,128)(2,1)} %copy.106), calls=%async_computation.1 | async-start | bytes 65536 | tf_op jit(solution)/shard_map/all_to_all | solution.py:132
  26.5 2.3 copy.105
  28.8 10.2 %all-to-all-done.1 = bf16[128,64,1]{0,2,1:T(2,128)(2,1)S(1)} async-done(((bf16[128,64,1]{0,2,1:T(2,128)(2,1)}), bf16[128,64,1]{0,2,1:T(2,128)(2,1)S(1)}, u32[]{:S(2)}, u32[]{:S(2)}) %all-to-all-start.1) | async-done | bytes 16416 | tf_op jit(solution)/shard_map/all_to_all | solution.py:132
  39.1 6.8 all-to-all-start
  46.1 53.8 %all-to-all-done = bf16[128,64,64]{0,2,1:T(8,128)(2,1)S(1)} async-done(((bf16[128,64,64]{0,2,1:T(8,128)(2,1)}), bf16[128,64,64]{0,2,1:T(8,128)(2,1)S(1)}, u32[]{:S(2)}, u32[]{:S(2)}) %all-to-all-start) | async-done | bytes 1048608 | tf_op jit(solution)/shard_map/all_to_all | solution.py:130
  100.0 3.0 broadcast_in_dim.45
  103.0 6.3 all-to-all-start.2
  113.2 1.4 fusion.50
  114.6 4.4 copy.108
  119.0 4.5 fusion.81
  123.5 3.7 copy.109
  130.0 196.0 %all-to-all-done.2 = bf16[128,64,256]{0,2,1:T(8,128)(2,1)} async-done(((bf16[128,64,256]{0,2,1:T(8,128)(2,1)}), bf16[128,64,256]{0,2,1:T(8,128)(2,1)}, u32[]{:S(2)}, u32[]{:S(2)}) %all-to-all-start.2) | async-done | bytes 4194336 | tf_op jit(solution)/shard_map/all_to_all | solution.py:131
  326.1 6.4 copy.111
  332.5 5.3 gather_fusion.3
  337.7 2.5 copy.146
  340.3 1.9 fusion.24
  342.2 3.3 fusion.42
  345.5 1.6 fusion.41
  347.0 5.1 fusion.16
  352.4 5.0 fusion.28
  357.4 1.7 gather_fusion.4
  359.0 7.8 all-to-all-start.3
  367.6 1.7 copy.132
  369.9 12.6 %reshape.689 = bf16[64,128,2,2,128]{4,3,2,1,0:T(2,128)(2,1)} reshape(bf16[1,8192,512]{2,1,0:T(8,128)(2,1)} %all-gather.3.cloned.1.call-done) | data formatting | bytes 16777216 | tf_op jit(solution)/shard_map/reshape | solution.py:171
  382.4 9.3 %copy.123 = bf16[64,128,2,2,128]{4,1,3,2,0:T(8,128)(2,1)} copy(bf16[64,128,2,2,128]{4,3,2,1,0:T(2,128)(2,1)} %reshape.689) | data formatting | bytes 16777216
  391.7 27.3 %all-to-all-done.3 = bf16[64,128,64]{1,2,0:T(8,128)(2,1)S(1)} async-done(((bf16[64,128,64]{1,2,0:T(8,128)(2,1)}), bf16[64,128,64]{1,2,0:T(8,128)(2,1)S(1)}, u32[]{:S(2)}, u32[]{:S(2)}) %all-to-all-start.3) | async-done | bytes 1048608 | tf_op jit(solution)/shard_map/all_to_all | solution.py:157
  419.3 2.0 copy.121
  421.7 2.9 fusion.30
  424.9 427.1 %while.15 = (s32[]{:T(128)}, f32[2,16,128]{2,1,0:T(8,128)S(1)}, f32[2,16,128]{2,1,0:T(8,128)S(1)}, f32[2,16,128,128]{3,2,1,0:T(8,128)S(1)}, s32[128]{0:T(128)S(1...) while((s32[]{:T(128)}, f32[2,16,128]{2,1,0:T(8,128)S(1)}, ...), condition=%wide.region_11.12_spmd.clone, body=%wide.region_5.11_spmd.clone.sunk | while | flops 276376192 | bytes 12266329 | solution.py:207
  428.7 1.1 gather_fusion
  435.1 1.1 gather_fusion
  441.5 1.1 gather_fusion
  447.9 1.1 gather_fusion
  450.5 3.5 conditional.3
  452.5 1.5 multiply_add_fusion
  457.7 1.1 gather_fusion
  464.2 1.1 gather_fusion
  470.6 1.1 gather_fusion
  477.0 1.1 gather_fusion
  483.4 1.1 gather_fusion
  489.8 1.1 gather_fusion
  496.2 1.1 gather_fusion
  498.7 3.5 conditional.3
  500.7 1.5 multiply_add_fusion
  506.0 1.1 gather_fusion
  512.4 1.1 gather_fusion
  518.8 1.1 gather_fusion
  531.6 1.1 gather_fusion
  534.2 3.5 conditional.3
  536.2 1.5 multiply_add_fusion
  605.5 1.1 gather_fusion
  727.2 1.1 gather_fusion
  806.6 3.5 conditional.3
  808.6 1.5 multiply_add_fusion
  816.5 3.5 conditional.3
  818.5 1.5 multiply_add_fusion
  852.9 1.2 copy.124
  854.1 1.6 reshape.609
  855.7 1.5 mul.214
  857.2 2.9 mul.215
  860.1 1.9 copy.119
  861.9 3.6 add_convert_fusion
  865.6 15.4 %collective-permute-done = bf16[1,128,4096]{2,1,0:T(8,128)(2,1)S(1)} collective-permute-done((bf16[1,128,4096]{2,1,0:T(8,128)(2,1)S(1)}, bf16[1,128,4096]{2,1,0:T(8,128)(2,1)S(1)}, u32[]{:S(2)}, u32[]{:S(2)}) %collective-permute-start) | collective-permute-done | bytes 1048608 | tf_op jit(solution)/shard_map/ppermute | solution.py:24
  (652 shorter events, 198.8 us)
Async XLA Ops:
  6.5 104.6 %copy-start = (f32[1,64]{1,0:T(1,128)S(1)}, f32[1,64]{1,0:T(1,128)}, u32[]{:S(2)}) copy-start(f32[1,64]{1,0:T(1,128)} %param.20) | copy-start | bytes 772
  7.9 31.2 %all-to-all-start.1 = ((bf16[128,64,1]{0,2,1:T(2,128)(2,1)}), bf16[128,64,1]{0,2,1:T(2,128)(2,1)S(1)}, u32[]{:S(2)}, u32[]{:S(2)}) async-start(bf16[128,64,1]{0,2,1:T(2,128)(2,1)} %copy.106), calls=%async_computation.1 | async-start | bytes 65536 | tf_op jit(solution)/shard_map/all_to_all | solution.py:132
  26.5 19.3 %copy-start.7 = (bf16[1,128,2048]{2,1,0:T(8,128)(2,1)S(1)}, bf16[1,128,2048]{2,1,0:T(8,128)(2,1)}, u32[]{:S(2)}) copy-start(bf16[1,128,2048]{2,1,0:T(8,128)(2,1)} %param.16) | copy-start | bytes 1572868
  39.1 60.9 %all-to-all-start = ((bf16[128,64,64]{0,2,1:T(8,128)(2,1)}), bf16[128,64,64]{0,2,1:T(8,128)(2,1)S(1)}, u32[]{:S(2)}, u32[]{:S(2)}) async-start(bf16[128,64,64]{0,2,1:T(8,128)(2,1)} %bitcast.8), calls=%async_computation | async-start | bytes 2097152 | tf_op jit(solution)/shard_map/all_to_all | solution.py:130
  103.0 7.0 copy-start.2
  103.0 7.2 copy-start.12
  103.0 8.7 copy-start.10
  103.0 8.7 copy-start.11
  103.0 223.0 %all-to-all-start.2 = ((bf16[128,64,256]{0,2,1:T(8,128)(2,1)}), bf16[128,64,256]{0,2,1:T(8,128)(2,1)}, u32[]{:S(2)}, u32[]{:S(2)}) async-start(bf16[128,64,256]{0,2,1:T(8,128)(2,1)} %bitcast.162), calls=%async_computation.2 | async-start | bytes 8388608 | tf_op jit(solution)/shard_map/all_to_all | solution.py:131
  109.3 260.6 %all-gather.3.cloned.1.call-start = ((), (), s32[]{:S(2)}) async-start(), calls=%async_computation.4 | async-start | bytes 8519680 | tf_op jit(solution)/shard_map/all_gather | solution.py:169
  359.0 8.3 copy-start.5
  359.0 60.0 %all-to-all-start.3 = ((bf16[64,128,64]{1,2,0:T(8,128)(2,1)}), bf16[64,128,64]{1,2,0:T(8,128)(2,1)S(1)}, u32[]{:S(2)}, u32[]{:S(2)}) async-start(bf16[64,128,64]{1,2,0:T(8,128)(2,1)} %gather_fusion.4), calls=%async_computation.3 | async-start | bytes 2097152 | tf_op jit(solution)/shard_map/all_to_all | solution.py:157
  419.2 2.0 copy-start.3
  419.3 2.5 copy-start.8
  857.2 2.9 copy-start.4
  860.1 1.9 copy-start.6
  860.1 1.9 copy-start.9
  861.9 20.1 %copy-start.1 = (f32[1,64]{1,0:T(1,128)S(1)}, f32[1,64]{1,0:T(1,128)}, u32[]{:S(2)}) copy-start(f32[1,64]{1,0:T(1,128)} %param.20) | copy-start | bytes 772
  865.6 15.4 %collective-permute-start = (bf16[1,128,4096]{2,1,0:T(8,128)(2,1)S(1)}, bf16[1,128,4096]{2,1,0:T(8,128)(2,1)S(1)}, u32[]{:S(2)}, u32[]{:S(2)}) collective-permute-start(bf16[1,128,4096]{2,1,0:T(8,128)(2,1)S(1)} %add_convert_fusion), channel_id=1, source_target_pairs={{0,64},{64,128},{128,192},{192,256},{256,320},{320,384},{384,448},... | collective-permute-start | bytes 3145736 | tf_op jit(solution)/shard_map/ppermute | solution.py:24
Sparse Core Ops, SparseCore 0:
  113.1 240.6 all-gather.2
where the time goes:
time: 895 us; the launch traced here: 889 us
  waiting for transfers between devices  304 us (34%)
  local copies, waits for them, and re-layouts  225 us (25%)
  loops' own time  213 us (24%)
  other arithmetic  67.4 us (8%)
  starting transfers between devices  39.4 us (4%)
  matrix products  26.4 us (3%)
  between operations  14.6 us (2%)
    another operation x1, loops' own time, on_device(): lax.scan(one_block, initial, (pieces, firsts))[0]  212 us
    all_to_all x1, waiting for transfers between devices, on_device(): lax.all_to_all(copies, 'ctx', split_axis=1, concat_axis=0, tiled=True)  196 us
    gather x64, local copies, waits for them, and re-layouts, one_block(): key_seg = jnp.take(segment, key_pos)  73.5 us
    all_to_all x1, waiting for transfers between devices, on_device(): lax.all_to_all(inputs, 'ctx', split_axis=1, concat_axis=0, tiled=True)  53.8 us
    reduce_or x64, other arithmetic, one_block(): return (lax.cond(jnp.any(allowed), update, unchanged, running), None)  47 us
    dynamic_slice x64, local copies, waits for them, and re-layouts, one_block(): placement_perm[source] * tok_rows + jnp.arange(tok_rows, dtype=jnp.int32)  37.6 us
    dynamic_slice x64, local copies, waits for them, and re-layouts, on_device(): lax.scan(one_block, initial, (pieces, firsts))[0]  37.6 us
    all_to_all x1, waiting for transfers between devices, on_device(): lax.all_to_all(outputs, 'ctx', split_axis=0, concat_axis=1, tiled=True)  27.3 us
  transfers between devices with their start and end apart: 6, of which 5 were waited for; matrix products, arithmetic and copies ran while one was open for 9% of the time, Pallas kernels for 0%

commit v1 on v0

v1 whole, which is shorter than its diff:
```python
import math

import jax
import jax.numpy as jnp
from jax import lax
from jax.sharding import PartitionSpec as P

HEADS = 64
HEAD_DIM = 64
GROUPS = 8
STATE = 128
QHEADS = 32
KVHEADS = 2
QDIM = 128
HALO = 4


precise = lax.Precision.HIGHEST
epsilon = 1e-05


def passed_along(value, axis, steps):
    count = lax.axis_size(axis)
    pairs = [(source, (source + steps) % count) for source in range(count)]
    return lax.ppermute(value, axis, pairs)


def group_norm(values, gain):
    grouped = values.reshape(values.shape[0], GROUPS, -1)
    normed = grouped * lax.rsqrt(jnp.mean(grouped * grouped, axis=-1, keepdims=True) + epsilon)
    return normed.reshape(values.shape) * gain


def block_terms(values, inject, readout, step_sizes, rates, seg):
    length = values.shape[0]
    within = HEADS // GROUPS
    cum_log = jnp.cumsum(-rates * step_sizes, axis=0)
    positions = jnp.arange(length)
    allowed = (positions[:, None] >= positions[None, :]) & (seg[:, None] == seg[None, :])
    spread = cum_log.T[:, :, None] - cum_log.T[:, None, :]
    decays = jnp.where(allowed[None], jnp.exp(jnp.minimum(spread, 0.0)), 0.0)
    scores = jnp.einsum("tgs,ugs->gtu", readout, inject, preferred_element_type=jnp.float32)
    weights = decays.reshape(GROUPS, within, length, length) * scores[:, None]
    scaled = values * step_sizes[..., None]
    local_out = jnp.einsum(
        "gktu,ugkp->tgkp",
        weights,
        scaled.reshape(length, GROUPS, within, HEAD_DIM),
        precision=precise,
    ).reshape(values.shape)
    ending = cum_log[-1]
    to_end = jnp.where((seg == seg[-1])[:, None], jnp.exp(ending[None, :] - cum_log), 0.0)
    weighted = (scaled * to_end[..., None]).reshape(length, GROUPS, within, HEAD_DIM)
    states = jnp.einsum(
        "tgkp,tgs->gkps", weighted, inject.astype(jnp.float32), precision=precise
    ).reshape(HEADS, HEAD_DIM, STATE)
    return local_out, states, cum_log, ending


def on_device(
    mixer_input,
    state_proj,
    dt_raw,
    decay_rate,
    dt_bias,
    skip_gain,
    mamba_gain,
    keys_values,
    attn_gain,
    documents,
    placement_perm,
):
    devices = lax.axis_size("ctx")
    myself = lax.axis_index("ctx")
    tok_rows = mixer_input.shape[1]
    kv_cols = keys_values.shape[2]
    slice_cols = kv_cols // devices
    inverse = (
        jnp.zeros((devices,), jnp.int32)
        .at[placement_perm]
        .set(jnp.arange(devices, dtype=jnp.int32))
    )
    segment = documents[0]
    block_seg = segment.reshape(devices, tok_rows)
    seg_end = block_seg[:, -1]
    seg_prev = jnp.concatenate([jnp.full((1,), -1, jnp.int32), seg_end[:-1]])
    my_block = placement_perm[myself]
    my_seg = lax.dynamic_slice_in_dim(segment, my_block * tok_rows, tok_rows, 0)
    my_prev = seg_prev[my_block]

    inputs = mixer_input[0]
    values = inputs.astype(jnp.float32).reshape(tok_rows, HEADS, HEAD_DIM)
    paired = state_proj[0].reshape(tok_rows, GROUPS, 2, STATE)
    inject = paired[:, :, 0]
    readout = paired[:, :, 1]
    step_sizes = jax.nn.softplus(dt_raw[0].astype(jnp.float32) + dt_bias[0])
    local_out, states, cum_log, ending = block_terms(
        values, inject, readout, step_sizes, decay_rate[0], my_seg
    )

    kv = keys_values[0]
    kv_slices = kv.reshape(tok_rows, devices, slice_cols).transpose(1, 0, 2)
    kv_slices = kv_slices.reshape(devices, tok_rows * slice_cols)
    state_slots = states.astype(jnp.bfloat16).reshape(HEADS, HEAD_DIM * STATE)
    first = jnp.concatenate([state_slots, kv_slices], axis=1)
    got = lax.all_to_all(first, "ctx", split_axis=0, concat_axis=0, tiled=True)
    all_endings = lax.all_gather(ending, "ctx", axis=0, tiled=False)
    got_states = got[:, : HEAD_DIM * STATE].astype(jnp.float32)
    got_kv = got[:, HEAD_DIM * STATE :]

    ending_pos = all_endings[inverse, myself]
    running = jnp.cumsum(ending_pos)
    before = running - ending_pos
    positions = jnp.arange(devices)
    linked = (positions[None, :] < positions[:, None]) & (seg_end[None, :] == seg_prev[:, None])
    factors = jnp.where(
        linked, jnp.exp(jnp.minimum(before[:, None] - running[None, :], 0.0)), 0.0
    )
    by_device = factors[placement_perm][:, placement_perm]
    entering = jnp.dot(by_device, got_states, precision=precise)

    halo_blocks = placement_perm[:, None] - HALO + jnp.arange(HALO)[None, :]
    halo_src = inverse[jnp.clip(halo_blocks, 0, devices - 1)]
    halo = got_kv[halo_src].reshape(devices, HALO * tok_rows * slice_cols)
    second = jnp.concatenate([entering.astype(jnp.bfloat16), halo], axis=1)
    back = lax.all_to_all(second, "ctx", split_axis=0, concat_axis=0, tiled=True)
    enter_here = back[:, : HEAD_DIM * STATE].reshape(GROUPS, HEADS // GROUPS, HEAD_DIM, STATE)
    halo_here = back[:, HEAD_DIM * STATE :].reshape(devices, HALO * tok_rows, slice_cols)
    halo_kv = halo_here.transpose(1, 0, 2).reshape(HALO * tok_rows, kv_cols)

    reach = jnp.where((my_seg == my_prev)[:, None], jnp.exp(cum_log), 0.0)
    read_out = jnp.einsum(
        "tgs,gkps->tgkp", readout, enter_here, preferred_element_type=jnp.float32
    ).reshape(tok_rows, HEADS, HEAD_DIM)
    outputs = local_out + read_out * reach[..., None] + skip_gain[0][:, None] * values
    mamba_out = outputs.astype(jnp.bfloat16).reshape(tok_rows, HEADS * HEAD_DIM)
    residual = inputs.astype(jnp.float32) + group_norm(mamba_out.astype(jnp.float32), mamba_gain[0])
    hidden = residual.astype(jnp.bfloat16)

    repeat = QHEADS // KVHEADS
    queries = hidden.reshape(tok_rows, KVHEADS, repeat, QDIM)
    all_kv = jnp.concatenate([halo_kv, kv], axis=0).reshape(-1, 2, KVHEADS, QDIM)
    keys = all_kv[:, 0]
    vals = all_kv[:, 1]
    query_pos = my_block * tok_rows + jnp.arange(tok_rows, dtype=jnp.int32)
    key_pos = (my_block - HALO) * tok_rows + jnp.arange((HALO + 1) * tok_rows, dtype=jnp.int32)
    key_seg = jnp.take(segment, jnp.maximum(key_pos, 0))
    allowed = (
        (my_seg[:, None] == key_seg[None, :])
        & (key_pos[None, :] <= query_pos[:, None])
        & (key_pos[None, :] >= 0)
    )
    score_scale = 1.0 / math.sqrt(QDIM)
    logits = (
        jnp.einsum("tgrd,kgd->grtk", queries, keys, preferred_element_type=jnp.float32)
        * score_scale
    )
    logits = jnp.where(allowed, logits, -1e30)
    best = jnp.max(logits, axis=-1, keepdims=True)
    weights = jnp.where(allowed, jnp.exp(logits - best), 0.0)
    total_weight = jnp.sum(weights, axis=-1)
    blended = jnp.einsum(
        "grtk,kgd->grtd", weights.astype(jnp.bfloat16), vals, preferred_element_type=jnp.float32
    )
    attended = (
        (blended / total_weight[..., None]).transpose(2, 0, 1, 3).reshape(tok_rows, QHEADS * QDIM)
    )
    normed = (
        attended
        * lax.rsqrt(jnp.mean(attended * attended, axis=-1, keepdims=True) + epsilon)
        * attn_gain[0]
    )
    result = (hidden.astype(jnp.float32) + normed).astype(jnp.bfloat16)
    return passed_along(result[None], "phase", 1)


def solution(mesh):
    in_specs = (
        P("phase", "ctx", None),
        P("phase", "ctx", None),
        P("phase", "ctx", None),
        P("phase", None),
        P("phase", None),
        P("phase", None),
        P("phase", None),
        P("phase", "ctx", None),
        P("phase", None),
        P("phase", None),
        P(),
    )
    out_specs = P("phase", "ctx", None)
    return jax.shard_map(
        on_device, mesh=mesh, in_specs=in_specs, out_specs=out_specs, check_vma=False
    )
```

time: 895 us -> 333 us (0.37)
  waiting for transfers between devices: 304 us -> 57.6 us
  loops' own time: 213 us -> 0 us
  local copies, waits for them, and re-layouts: 225 us -> 71.1 us
  blocking collectives: 0 us -> 118 us
  other arithmetic: 67.4 us -> 20.8 us
  between operations: 14.6 us -> 3.97 us
  starting transfers between devices: 39.4 us -> 30.1 us
    all_to_all x4 -> x2, waiting for transfers between devices: 287 us -> 42.1 us  [the longest x1 42.1 us: on_device(): lax.all_to_all(second, 'ctx', split_axis=0, concat_axis=0, tiled=True)]
    another operation x65 -> x0, loops' own time: 213 us -> none  [the longest x1 212 us: on_device(): lax.scan(one_block, initial, (pieces, firsts))[0]]
    all_gather x0 -> x1, blocking collectives: none -> 118 us  [on_device(): all_endings = lax.all_gather(ending, 'ctx', axis=0, tiled=False)]
    dynamic_slice x130 -> x1, local copies, waits for them, and re-layouts: 75.7 us -> 0.59 us  [on_device(): my_prev = seg_prev[my_block]]
    gather x69 -> x8, local copies, waits for them, and re-layouts: 84.3 us -> 10.5 us  [the longest x1 3.86 us: on_device(): key_seg = jnp.take(segment, jnp.maximum(key_pos, 0))]
    reduce_or x64 -> x0, other arithmetic: 47 us -> none  [one_block(): return (lax.cond(jnp.any(allowed), update, unchanged, running), None)]
    unnamed x30 -> x49, local copies, waits for them, and re-layouts: 14.3 us -> 38.8 us
    reshape x3 -> x2, local copies, waits for them, and re-layouts: 20.5 us -> 3.23 us  [the longest x1 2.17 us: on_device(): halo = got_kv[halo_src].reshape(devices, HALO * tok_rows * slice_cols)]
  transfers between devices with their start and end apart: 6 -> 3, of which waited for: 5 -> 2; matrix products, arithmetic and copies ran while one was open for 9% -> 7% of each run, Pallas kernels for 0% -> 0%
where the time goes in v1:
time: 333 us; the launch traced here: 332 us
  blocking collectives  118 us (35%)
  local copies, waits for them, and re-layouts  71.1 us (21%)
  waiting for transfers between devices  57.6 us (17%)
  starting transfers between devices  30.1 us (9%)
  matrix products  29.9 us (9%)
  other arithmetic  20.8 us (6%)
  between operations  3.97 us (1%)
    all_gather x1, blocking collectives, on_device(): all_endings = lax.all_gather(ending, 'ctx', axis=0, tiled=False)  118 us
    all_to_all x1, waiting for transfers between devices, on_device(): lax.all_to_all(second, 'ctx', split_axis=0, concat_axis=0, tiled=True)  42.1 us
    unnamed x49, local copies, waits for them, and re-layouts  38.8 us
    all_to_all x1, starting transfers between devices, on_device(): got = lax.all_to_all(first, 'ctx', split_axis=0, concat_axis=0, tiled=True)  18.8 us
    ppermute x1, waiting for transfers between devices, passed_along(): return lax.ppermute(value, axis, pairs)  15.4 us
    all_to_all x1, starting transfers between devices, on_device(): lax.all_to_all(second, 'ctx', split_axis=0, concat_axis=0, tiled=True)  11.4 us
    dot_general x1, matrix products, block_terms(): jnp.einsum('gktu,ugkp->tgkp', weights, scaled.reshape(length, GROUPS, wit...  9.61 us
    sub x1, matrix products, on_device(): weights = jnp.where(allowed, jnp.exp(logits - best), 0.0)  8.85 us
  transfers between devices with their start and end apart: 3, of which 2 were waited for; matrix products, arithmetic and copies ran while one was open for 7% of the time, Pallas kernels for 0%

profile of v1, /device:TPU:6, one launch (start us, length us, event | category | flops | bytes accessed | tf_op | source)
XLA Modules:
  0.0 331.9 jit_solution(15197116279320983934)
XLA Ops:
  0.0 1.3 dynamic_slice.9
  2.7 0.7 negate_bitcast_fusion
  3.4 0.8 fusion.77
  4.3 0.2 reduce_window_sum.20
  5.3 0.8 slice.69
  7.0 0.6 dynamic_slice.11
  7.5 1.3 broadcast_compare_fusion
  8.9 0.6 slice.47
  9.4 0.6 broadcast_compare_fusion.1
  10.2 1.6 copy.115
  11.8 0.1 convert_element_type.95
  12.0 2.1 copy.118
  14.0 0.5 broadcast.394
  14.5 0.6 reduce.17
  15.3 0.6 fusion.80
  15.9 2.2 fusion.36
  18.2 1.7 copy.168
  19.9 0.1 copy.126
  20.0 0.9 copy.127
  20.9 1.1 copy.128
  22.0 2.3 maximum_bitcast_fusion.1
  24.3 0.5 broadcast.396
  24.8 3.4 %reduce.19 = bf16[64,9216]{1,0:T(8,128)(2,1)} reduce(bf16[64,1,9216]{2,0,1:T(8,128)(2,1)} %maximum_bitcast_fusion.1, bf16[]{:T(256)} %broadcast.396), dimensions={1}, to_apply=%copy.129.reduce_sub_computation | reduce | bytes 2359298 | tf_op jit(solution)/shard_map/all_to_all | solution.py:106
  28.2 2.8 reshape.606
  31.0 18.8 %all-to-all-start = ((bf16[64,2,4608]{2,1,0:T(2,128)(2,1)}), bf16[64,2,4608]{2,1,0:T(2,128)(2,1)}, u32[]{:S(2)}, u32[]{:S(2)}) async-start(bf16[64,2,4608]{2,1,0:T(2,128)(2,1)} %reshape.606), calls=%async_computation | async-start | bytes 2359296 | tf_op jit(solution)/shard_map/all_to_all | solution.py:106
  49.8 0.8 scatter_custom_fusion
  50.6 118.4 %all-gather = f32[64,1,64]{2,1,0:T(1,128)S(1)} all-gather(f32[1,1,64]{2,1,0:T(1,128)S(1)} %get-tuple-element.7), channel_id=1, replica_groups=mesh['phase'=8,'ctx'=64] {'ctx'}, dimensions={0}, use_global_device_ids=true | all-gather | bytes 16640 | tf_op jit(solution)/shard_map/all_gather | solution.py:107
  169.0 0.8 gather_fusion
  170.0 0.1 reduce.3
  170.3 0.6 gather_fusion.1
  171.0 1.2 gather_fusion.2
  172.3 0.1 reshape.527
  172.4 1.9 gather_fusion.3
  174.4 0.1 reshape.535
  174.5 7.8 %reshape.607 = bf16[64,1,9216]{2,1,0:T(2,128)(2,1)} reshape(bf16[64,2,4608]{2,1,0:T(2,128)(2,1)} %all-to-all-done) | data formatting | bytes 2359296
  182.3 2.1 copy.167
  184.4 2.0 convolution_convert_fusion
  186.4 2.0 gather_fusion.4
  188.4 2.2 reshape.492
  190.5 2.6 maximum_bitcast_fusion
  193.2 3.8 %reduce.20 = bf16[64,12288]{1,0:T(8,128)(2,1)} reduce(bf16[64,1,12288]{2,0,1:T(8,128)(2,1)} %maximum_bitcast_fusion, bf16[]{:T(256)} %broadcast.396), dimensions={1}, to_apply=%copy.130.reduce_sub_computation | reduce | bytes 3145730 | tf_op jit(solution)/shard_map/all_to_all | solution.py:126
  197.0 4.9 %reshape.608 = bf16[64,2,6144]{2,1,0:T(2,128)(2,1)} reshape(bf16[64,12288]{1,0:T(8,128)(2,1)} %reduce.20) | data formatting | bytes 3145728
  201.9 11.4 %all-to-all-start.1 = ((bf16[64,2,6144]{2,1,0:T(2,128)(2,1)}), bf16[64,2,6144]{2,1,0:T(2,128)(2,1)}, u32[]{:S(2)}, u32[]{:S(2)}) async-start(bf16[64,2,6144]{2,1,0:T(2,128)(2,1)} %reshape.608), calls=%async_computation.1 | async-start | bytes 3145728 | tf_op jit(solution)/shard_map/all_to_all | solution.py:126
  213.4 0.6 reduce.18
  214.7 0.8 copy.136
  216.0 3.9 %gather_fusion.5 = s32[640]{0:T(1024)S(1)} fusion(s32[8192]{0:T(1024)S(1)} %bitcast.228, s32[1024]{0:T(1024)S(1)} %pad_clamp_fusion), kind=kCustom, calls=%fused_computation.5 | custom fusion | bytes 7680 | tf_op jit(solution)/shard_map/jit(_take)/gather | solution.py:147
  220.0 0.3 and_and_fusion
  220.3 1.3 fusion.55
  221.7 9.6 %fusion.7 = f32[8,8,64,128]{3,2,1,0:T(8,128)} fusion(f32[8,128,128]{2,1,0:T(8,128)S(1)} %fusion.55, f32[8,8,128]{2,1,0:T(8,128)S(1)} %bitcast.254, pred[128,128]{1,0:T(8,128)(4,1)S(1)} %fusion.62, f32[128,8,8,64]{0,3,2,1:T(8,128)S(1)} %bitcast.230, f32[128,8,8]{0,2,1:T(8,128)S(1)} %copy-done.8), kind=kOutput, calls=%fused_computation.17 | convolution fusion | flops 810024960 | bytes 4800512 | tf_op jit(solution)/shard_map/gktu,ugkp->tgkp/dot_general | solution.py:45
  231.3 42.1 %all-to-all-done.1 = bf16[64,2,6144]{2,1,0:T(2,128)(2,1)} async-done(((bf16[64,2,6144]{2,1,0:T(2,128)(2,1)}), bf16[64,2,6144]{2,1,0:T(2,128)(2,1)}, u32[]{:S(2)}, u32[]{:S(2)}) %all-to-all-start.1) | async-done | bytes 1572896 | tf_op jit(solution)/shard_map/all_to_all | solution.py:126
  273.4 10.4 %reshape.609 = bf16[64,1,12288]{2,1,0:T(2,128)(2,1)} reshape(bf16[64,2,6144]{2,1,0:T(2,128)(2,1)} %all-to-all-done.1) | data formatting | bytes 3145728
  283.8 3.6 %copy.166 = bf16[64,1,12288]{2,0,1:T(8,128)(2,1)S(1)} copy(bf16[64,1,12288]{2,1,0:T(2,128)(2,1)} %reshape.609) | data formatting | bytes 3145728
  287.5 0.8 slice.74
  288.3 0.8 copy-done.1
  289.3 2.0 multiply_reduce_fusion.1
  291.3 2.4 copy.132
  293.7 3.1 copy.133
  296.8 2.0 copy.135
  298.9 1.4 mul.208
  300.3 8.8 %fusion.97 = (f32[2,16,128]{2,1,0:T(8,128)S(1)}, bf16[2,16,128,640]{2,3,1,0:T(8,128)(2,1)}) fusion(pred[128,640]{0,1:T(8,128)(4,1)S(1)} %and_and_fusion, bf16[512,2,2,128]{3,0,2,1:T(8,128)(2,1)} %copy.135, bf16[128,2,2,128]{3,0,2,1:T(8,128)(2,1)S(1)} %copy-done.10, f32[128,2,16,128]{0,3,2,1:T(8,128)S(1)} %bitcast.232, f32[128,2,16,128]{0,3,2,1:T(8,128)} %bitcast.234, ...), kind=kOutput, calls=%fused_computation.146 | convolution fusion | flops 692716160 | bytes 14516224 | tf_op jit(solution)/shard_map/sub | solution.py:160
  309.2 3.9 %multiply_reduce_fusion = (f32[128]{0:T(128)S(1)}, f32[128,2,16,128]{0,3,2,1:T(8,128)S(1)}) fusion(f32[128,2,16]{0,2,1:T(8,128)S(1)} %bitcast.267, bf16[128,2,2,128]{3,0,2,1:T(8,128)(2,1)S(1)} %copy-done.10, bf16[512,2,2,128]{3,0,2,1:T(8,128)(2,1)} %copy.135, bf16[2,16,128,640]{2,3,1,0:T(8,128)(2,1)} %get-tuple-element.16), kind=kOutput, calls=%fused_computation.37 | convolution fusion | flops 673316736 | bytes 8012288 | tf_op jit(solution)/shard_map/grtk,kgd->grtd/dot_general | solution.py:162
  313.1 2.0 add_convert_fusion
  315.1 15.4 %collective-permute-done = bf16[1,128,4096]{1,2,0:T(8,128)(2,1)S(1)} collective-permute-done((bf16[1,128,4096]{1,2,0:T(8,128)(2,1)S(1)}, bf16[1,128,4096]{1,2,0:T(8,128)(2,1)S(1)}, u32[]{:S(2)}, u32[]{:S(2)}) %collective-permute-start) | collective-permute-done | bytes 1048608 | tf_op jit(solution)/shard_map/ppermute | solution.py:25
  330.5 1.3 copy.140
  (78 shorter events, 2.3 us)
Async XLA Ops:
  11.8 2.7 copy-start.15
  11.8 3.4 %copy-start.11 = (bf16[1,128,64]{1,2,0:T(8,128)(2,1)S(1)}, bf16[1,128,64]{1,2,0:T(8,128)(2,1)}, u32[]{:S(2)}) copy-start(bf16[1,128,64]{1,2,0:T(8,128)(2,1)} %param.13) | copy-start | bytes 49156
  15.3 2.9 copy-start.7
  15.9 3.9 %copy-start.9 = (bf16[1,128,512]{2,1,0:T(8,128)(2,1)S(1)}, bf16[1,128,512]{2,1,0:T(8,128)(2,1)}, u32[]{:S(2)}) copy-start(bf16[1,128,512]{2,1,0:T(8,128)(2,1)} %param.18) | copy-start | bytes 393220
  28.2 21.5 %copy-start = (s32[1,8192]{1,0:T(1,128)S(1)}, s32[1,8192]{1,0:T(1,128)}, u32[]{:S(2)}) copy-start(s32[1,8192]{1,0:T(1,128)} %param.20) | copy-start | bytes 98308
  28.2 21.6 %copy-start.16 = (s32[64]{0:T(128)S(1)}, s32[64]{0:T(128)}, u32[]{:S(2)}) copy-start(s32[64]{0:T(128)} %param.21) | copy-start | bytes 772
  31.0 143.5 %all-to-all-start = ((bf16[64,2,4608]{2,1,0:T(2,128)(2,1)}), bf16[64,2,4608]{2,1,0:T(2,128)(2,1)}, u32[]{:S(2)}, u32[]{:S(2)}) async-start(bf16[64,2,4608]{2,1,0:T(2,128)(2,1)} %reshape.606), calls=%async_computation | async-start | bytes 2359296 | tf_op jit(solution)/shard_map/all_to_all | solution.py:106
  182.3 2.1 copy-start.6
  201.9 11.5 %copy-start.14 = (f32[1,64]{1,0:T(1,128)S(1)}, f32[1,64]{1,0:T(1,128)}, u32[]{:S(2)}) copy-start(f32[1,64]{1,0:T(1,128)} %param.16) | copy-start | bytes 772
  201.9 71.5 %all-to-all-start.1 = ((bf16[64,2,6144]{2,1,0:T(2,128)(2,1)}), bf16[64,2,6144]{2,1,0:T(2,128)(2,1)}, u32[]{:S(2)}, u32[]{:S(2)}) async-start(bf16[64,2,6144]{2,1,0:T(2,128)(2,1)} %reshape.608), calls=%async_computation.1 | async-start | bytes 3145728 | tf_op jit(solution)/shard_map/all_to_all | solution.py:126
  216.0 5.7 %copy-start.8 = (f32[128,8,8]{0,2,1:T(8,128)S(1)}, f32[128,8,8]{0,2,1:T(8,128)}, u32[]{:S(2)}) copy-start(f32[128,8,8]{0,2,1:T(8,128)} %copy-done.7) | copy-start | bytes 98308
  287.4 1.8 copy-start.1
  287.4 1.9 copy-start.4
  287.4 1.8 copy-start.5
  293.7 6.6 %copy-start.10 = (bf16[128,2,2,128]{3,0,2,1:T(8,128)(2,1)S(1)}, bf16[128,2,2,128]{3,0,2,1:T(8,128)(2,1)}, u32[]{:S(2)}) copy-start(bf16[128,2,2,128]{3,0,2,1:T(8,128)(2,1)} %copy.136) | copy-start | bytes 393220
  293.7 6.6 %copy-start.12 = (f32[1,4096]{1,0:T(1,128)S(1)}, f32[1,4096]{1,0:T(1,128)}, u32[]{:S(2)}) copy-start(f32[1,4096]{1,0:T(1,128)} %param.17) | copy-start | bytes 49156
  309.2 3.9 %copy-start.2 = (f32[8,8,64,128]{3,2,1,0:T(8,128)S(1)}, f32[8,8,64,128]{3,2,1,0:T(8,128)}, u32[]{:S(2)}) copy-start(f32[8,8,64,128]{3,2,1,0:T(8,128)} %fusion.7) | copy-start | bytes 6291460
  309.2 3.9 %copy-start.3 = (f32[8,8,64,128]{3,2,1,0:T(8,128)S(1)}, f32[8,8,64,128]{3,2,1,0:T(8,128)}, u32[]{:S(2)}) copy-start(f32[8,8,64,128]{3,2,1,0:T(8,128)} %get-tuple-element.14) | copy-start | bytes 6291460
  309.2 3.9 %copy-start.13 = (f32[1,4096]{1,0:T(1,128)S(1)}, f32[1,4096]{1,0:T(1,128)}, u32[]{:S(2)}) copy-start(f32[1,4096]{1,0:T(1,128)} %param.19) | copy-start | bytes 49156
  315.1 15.4 %collective-permute-start = (bf16[1,128,4096]{1,2,0:T(8,128)(2,1)S(1)}, bf16[1,128,4096]{1,2,0:T(8,128)(2,1)S(1)}, u32[]{:S(2)}, u32[]{:S(2)}) collective-permute-start(bf16[1,128,4096]{1,2,0:T(8,128)(2,1)S(1)} %add_convert_fusion), channel_id=1, source_target_pairs={{0,64},{64,128},{128,192},{192,256},{256,320},{320,384},{384,448},... | collective-permute-start | bytes 3145736 | tf_op jit(solution)/shard_map/ppermute | solution.py:25

commit v2 on v1

--- a/solution.py
+++ b/solution.py
@@ -99,16 +99,25 @@
     )
 
     kv = keys_values[0]
+    lanes = 128
+    kv_rows = tok_rows * slice_cols // lanes
     kv_slices = kv.reshape(tok_rows, devices, slice_cols).transpose(1, 0, 2)
-    kv_slices = kv_slices.reshape(devices, tok_rows * slice_cols)
-    state_slots = states.astype(jnp.bfloat16).reshape(HEADS, HEAD_DIM * STATE)
-    first = jnp.concatenate([state_slots, kv_slices], axis=1)
+    kv_slices = kv_slices.reshape(devices, kv_rows, lanes)
+    raw_cols = dt_raw[0].T.reshape(HEADS, 1, tok_rows)
+    state_slots = states.astype(jnp.bfloat16)
+    used = HEAD_DIM + kv_rows + 1
+    padding = jnp.zeros((devices, -used % 8, lanes), jnp.bfloat16)
+    first = jnp.concatenate([state_slots, kv_slices, raw_cols, padding], axis=1)
     got = lax.all_to_all(first, "ctx", split_axis=0, concat_axis=0, tiled=True)
-    all_endings = lax.all_gather(ending, "ctx", axis=0, tiled=False)
-    got_states = got[:, : HEAD_DIM * STATE].astype(jnp.float32)
-    got_kv = got[:, HEAD_DIM * STATE :]
-
-    ending_pos = all_endings[inverse, myself]
+    got_states = got[:, :HEAD_DIM].astype(jnp.float32)
+    got_kv = got[:, HEAD_DIM : HEAD_DIM + kv_rows]
+    got_raw = got[:, HEAD_DIM + kv_rows].astype(jnp.float32)
+
+    my_rate = decay_rate[0][myself]
+    my_bias = dt_bias[0][myself]
+    my_steps = jax.nn.softplus(got_raw + my_bias)
+    endings = jnp.cumsum(-my_rate * my_steps, axis=1)[:, -1]
+    ending_pos = endings[inverse]
     running = jnp.cumsum(ending_pos)
     before = running - ending_pos
     positions = jnp.arange(devices)
@@ -117,15 +126,15 @@
         linked, jnp.exp(jnp.minimum(before[:, None] - running[None, :], 0.0)), 0.0
     )
     by_device = factors[placement_perm][:, placement_perm]
-    entering = jnp.dot(by_device, got_states, precision=precise)
+    entering = jnp.einsum("ds,spn->dpn", by_device, got_states, precision=precise)
 
     halo_blocks = placement_perm[:, None] - HALO + jnp.arange(HALO)[None, :]
     halo_src = inverse[jnp.clip(halo_blocks, 0, devices - 1)]
-    halo = got_kv[halo_src].reshape(devices, HALO * tok_rows * slice_cols)
+    halo = got_kv[halo_src].reshape(devices, HALO * kv_rows, lanes)
     second = jnp.concatenate([entering.astype(jnp.bfloat16), halo], axis=1)
     back = lax.all_to_all(second, "ctx", split_axis=0, concat_axis=0, tiled=True)
-    enter_here = back[:, : HEAD_DIM * STATE].reshape(GROUPS, HEADS // GROUPS, HEAD_DIM, STATE)
-    halo_here = back[:, HEAD_DIM * STATE :].reshape(devices, HALO * tok_rows, slice_cols)
+    enter_here = back[:, :HEAD_DIM].reshape(GROUPS, HEADS // GROUPS, HEAD_DIM, STATE)
+    halo_here = back[:, HEAD_DIM:].reshape(devices, HALO * tok_rows, slice_cols)
     halo_kv = halo_here.transpose(1, 0, 2).reshape(HALO * tok_rows, kv_cols)
 
     reach = jnp.where((my_seg == my_prev)[:, None], jnp.exp(cum_log), 0.0)

time: 333 us -> 257 us (0.77)
  blocking collectives: 118 us -> 0 us
  waiting for transfers between devices: 57.6 us -> 137 us
  local copies, waits for them, and re-layouts: 71.1 us -> 44.8 us
  other arithmetic: 20.8 us -> 15.5 us
  starting transfers between devices: 30.1 us -> 25.1 us
    all_gather x1 -> x0, blocking collectives: 118 us -> none  [on_device(): all_endings = lax.all_gather(ending, 'ctx', axis=0, tiled=False)]
    all_to_all x1, waiting for transfers between devices: 0.01 us -> 62.4 us  [on_device(): got = lax.all_to_all(first, 'ctx', split_axis=0, concat_axis=0, tiled=True)]
    unnamed x49 -> x45, local copies, waits for them, and re-layouts: 38.8 us -> 5.83 us
    all_to_all x1, waiting for transfers between devices: 42.1 us -> 58.7 us  [on_device(): lax.all_to_all(second, 'ctx', split_axis=0, concat_axis=0, tiled=True)]
    all_to_all x4 -> x0, other arithmetic: 12.2 us -> none  [the longest x2 6.47 us: on_device(): lax.all_to_all(second, 'ctx', split_axis=0, concat_axis=0, tiled=True)]
    all_to_all x1, starting transfers between devices: 11.4 us -> 6.24 us  [on_device(): lax.all_to_all(second, 'ctx', split_axis=0, concat_axis=0, tiled=True)]
    slice x3 -> x6, local copies, waits for them, and re-layouts: 3.2 us -> 8.18 us  [the longest x2 4.5 us: on_device(): halo_here = back[:, HEAD_DIM:].reshape(devices, HALO * tok_rows, slice_cols)]
  transfers between devices with their start and end apart: 3 -> 3, of which waited for: 2 -> 3; matrix products, arithmetic and copies ran while one was open for 7% -> 8% of each run, Pallas kernels for 0% -> 0%
where the time goes in v2:
time: 257 us; the launch traced here: 256 us
  waiting for transfers between devices  137 us (53%)
  local copies, waits for them, and re-layouts  44.8 us (17%)
  matrix products  30.4 us (12%)
  starting transfers between devices  25.1 us (10%)
  other arithmetic  15.5 us (6%)
  between operations  3.25 us (1%)
    all_to_all x1, waiting for transfers between devices, on_device(): got = lax.all_to_all(first, 'ctx', split_axis=0, concat_axis=0, tiled=True)  62.4 us
    all_to_all x1, waiting for transfers between devices, on_device(): lax.all_to_all(second, 'ctx', split_axis=0, concat_axis=0, tiled=True)  58.7 us
    all_to_all x1, starting transfers between devices, on_device(): got = lax.all_to_all(first, 'ctx', split_axis=0, concat_axis=0, tiled=True)  18.9 us
    ppermute x1, waiting for transfers between devices, passed_along(): return lax.ppermute(value, axis, pairs)  15.4 us
    dot_general x1, matrix products, block_terms(): jnp.einsum('gktu,ugkp->tgkp', weights, scaled.reshape(length, GROUPS, wit...  9.61 us
    sub x1, matrix products, on_device(): weights = jnp.where(allowed, jnp.exp(logits - best), 0.0)  9.04 us
    all_to_all x1, starting transfers between devices, on_device(): lax.all_to_all(second, 'ctx', split_axis=0, concat_axis=0, tiled=True)  6.24 us
    unnamed x45, local copies, waits for them, and re-layouts  5.83 us
  transfers between devices with their start and end apart: 3, of which 3 were waited for; matrix products, arithmetic and copies ran while one was open for 8% of the time, Pallas kernels for 0%

profile of v2, /device:TPU:6, one launch (start us, length us, event | category | flops | bytes accessed | tf_op | source)
XLA Modules:
  0.0 255.7 jit_solution(17002130859756681429)
XLA Ops:
  0.0 1.2 dynamic_slice.15
  2.3 0.8 copy.67
  3.1 0.7 negate_bitcast_fusion
  3.8 0.7 fusion.57
  4.5 0.2 reduce_window_sum.27
  4.7 0.7 copy.74
  5.9 0.8 slice.79
  7.4 1.2 broadcast_add_fusion
  8.6 0.6 dynamic_slice.19
  9.2 1.3 broadcast_compare_fusion
  10.5 0.6 slice.54
  11.1 1.2 broadcast_compare_fusion.1
  12.4 1.6 copy.66
  14.0 0.1 convert_element_type.95
  14.2 2.0 copy.69
  16.2 0.5 broadcast.369
  16.7 0.6 reduce.18
  17.4 0.7 compare_select_fusion.4
  18.2 0.1 copy.75
  18.3 0.9 copy.76
  19.2 1.1 copy.77
  20.3 0.7 copy.78
  21.1 0.8 fusion.71
  21.9 2.2 fusion.33
  24.2 1.4 maximum_maximum_fusion
  25.6 18.9 %all-to-all-start = ((bf16[64,80,128]{2,1,0:T(8,128)(2,1)}), bf16[64,80,128]{2,1,0:T(8,128)(2,1)}, u32[]{:S(2)}, u32[]{:S(2)}) async-start(bf16[64,80,128]{2,1,0:T(8,128)(2,1)} %maximum_maximum_fusion), calls=%async_computation | async-start | bytes 2621440 | tf_op jit(solution)/shard_map/all_to_all | solution.py:111
  44.9 0.8 scatter_custom_fusion
  45.7 1.9 gather_fusion.3
  47.8 0.6 constant_dynamic-slice_fusion
  48.4 62.4 %all-to-all-done = bf16[64,80,128]{2,1,0:T(8,128)(2,1)} async-done(((bf16[64,80,128]{2,1,0:T(8,128)(2,1)}), bf16[64,80,128]{2,1,0:T(8,128)(2,1)}, u32[]{:S(2)}, u32[]{:S(2)}) %all-to-all-start) | async-done | bytes 1310752 | tf_op jit(solution)/shard_map/all_to_all | solution.py:111
  110.9 1.5 fusion.61
  112.4 0.7 fusion.60
  113.0 0.8 gather_fusion
  114.0 0.1 reduce.5
  114.2 0.6 gather_fusion.1
  114.9 1.2 gather_fusion.2
  116.1 0.9 slice.83
  117.0 1.6 gather_fusion.4
  118.6 1.3 copy.83
  119.9 1.3 slice.82
  121.2 1.4 convolution_convert_fusion
  122.6 0.1 pad_maximum_fusion
  122.8 2.2 copy.84
  124.9 6.2 %all-to-all-start.1 = ((bf16[64,96,128]{2,1,0:T(8,128)(2,1)}), bf16[64,96,128]{2,1,0:T(8,128)(2,1)}, u32[]{:S(2)}, u32[]{:S(2)}) async-start(bf16[64,96,128]{2,1,0:T(8,128)(2,1)} %copy.84), calls=%async_computation.1 | async-start | bytes 3145728 | tf_op jit(solution)/shard_map/all_to_all | solution.py:135
  131.3 0.6 reduce.19
  132.7 0.8 copy.90
  134.0 3.9 %gather_fusion.5 = s32[640]{0:T(1024)S(1)} fusion(s32[8192]{0:T(1024)S(1)} %bitcast.173, s32[1024]{0:T(1024)S(1)} %pad_clamp_fusion), kind=kCustom, calls=%fused_computation.5 | custom fusion | bytes 7680 | tf_op jit(solution)/shard_map/jit(_take)/gather | solution.py:156
  138.0 0.3 and_and_fusion
  138.3 1.3 fusion.50
  139.6 9.6 %fusion.7 = f32[8,8,64,128]{3,2,1,0:T(8,128)} fusion(f32[8,128,128]{2,1,0:T(8,128)S(1)} %fusion.50, f32[8,8,128]{2,1,0:T(8,128)S(1)} %bitcast.198, pred[128,128]{1,0:T(8,128)(4,1)S(1)} %fusion.58, f32[128,8,8,64]{0,3,2,1:T(8,128)S(1)} %bitcast.175, f32[128,8,8]{0,2,1:T(8,128)S(1)} %copy-done.5), kind=kOutput, calls=%fused_computation.16 | convolution fusion | flops 810024960 | bytes 4800512 | tf_op jit(solution)/shard_map/gktu,ugkp->tgkp/dot_general | solution.py:45
  149.2 58.7 %all-to-all-done.1 = bf16[64,96,128]{2,1,0:T(8,128)(2,1)} async-done(((bf16[64,96,128]{2,1,0:T(8,128)(2,1)}), bf16[64,96,128]{2,1,0:T(8,128)(2,1)}, u32[]{:S(2)}, u32[]{:S(2)}) %all-to-all-start.1) | async-done | bytes 1572896 | tf_op jit(solution)/shard_map/all_to_all | solution.py:135
  207.9 1.5 slice.84
  209.4 0.5 copy-done.1
  209.8 2.9 %multiply_reduce_fusion.1 = (f32[128,8]{0,1:T(8,128)S(1)}, f32[8,8,64,128]{3,2,1,0:T(8,128)}) fusion(f32[128,8,8,64]{0,3,2,1:T(8,128)S(1)} %bitcast.176, f32[8,8,64,128]{3,2,1,0:T(8,128)S(1)} %copy-done.1, f32[8,8]{1,0:T(8,128)S(1)} %mul.226, f32[128,8,8]{0,2,1:T(8,128)S(1)} %get-tuple-element.7, bf16[8,8,64,128]{3,2,1,0:T(8,128)(2,1)S(1)} %bitcast.187, ...), kind=kOutput, calls=%fused_computation.39 | convolution fusion | flops 138411008 | bytes 7639296 | tf_op jit(solution)/shard_map/tgs,gkps->tgkp/dot_general | solution.py:141
  212.8 1.9 slice.85
  214.7 2.6 %copy.86 = bf16[64,32,128]{0,2,1:T(8,128)(2,1)} copy(bf16[64,32,128]{2,1,0:T(8,128)(2,1)} %slice.85) | data formatting | bytes 1048576 | tf_op jit(solution)/shard_map/slice | solution.py:137
  217.3 3.1 %copy.87 = bf16[512,64,8]{0,2,1:T(8,128)(2,1)} copy(bf16[512,64,8]{1,2,0:T(8,128)(2,1)} %bitcast.185) | data formatting | bytes 1048576 | tf_op jit(solution)/shard_map/transpose | solution.py:138
  220.4 2.0 copy.89
  222.5 1.4 mul.216
  223.9 9.0 %fusion.86 = (f32[2,16,128]{2,1,0:T(8,128)S(1)}, bf16[2,16,128,640]{2,3,1,0:T(8,128)(2,1)}) fusion(pred[128,640]{0,1:T(8,128)(4,1)S(1)} %and_and_fusion, bf16[512,2,2,128]{3,0,2,1:T(8,128)(2,1)} %copy.89, bf16[128,2,2,128]{3,0,2,1:T(8,128)(2,1)S(1)} %copy-done.8, f32[128,2,16,128]{0,3,2,1:T(8,128)S(1)} %bitcast.177, f32[128,2,16,128]{0,3,2,1:T(8,128)} %bitcast.178, ...), kind=kOutput, calls=%fused_computation.136 | convolution fusion | flops 692716160 | bytes 14516224 | tf_op jit(solution)/shard_map/sub | solution.py:169
  233.0 3.9 %multiply_reduce_fusion = (f32[128]{0:T(128)S(1)}, f32[128,2,16,128]{0,3,2,1:T(8,128)S(1)}) fusion(f32[128,2,16]{0,2,1:T(8,128)S(1)} %bitcast.211, bf16[128,2,2,128]{3,0,2,1:T(8,128)(2,1)S(1)} %copy-done.8, bf16[512,2,2,128]{3,0,2,1:T(8,128)(2,1)} %copy.89, bf16[2,16,128,640]{2,3,1,0:T(8,128)(2,1)} %get-tuple-element.14), kind=kOutput, calls=%fused_computation.36 | convolution fusion | flops 673316736 | bytes 8012288 | tf_op jit(solution)/shard_map/grtk,kgd->grtd/dot_general | solution.py:171
  236.9 2.0 add_convert_fusion
  238.9 15.4 %collective-permute-done = bf16[1,128,4096]{1,2,0:T(8,128)(2,1)S(1)} collective-permute-done((bf16[1,128,4096]{1,2,0:T(8,128)(2,1)S(1)}, bf16[1,128,4096]{1,2,0:T(8,128)(2,1)S(1)}, u32[]{:S(2)}, u32[]{:S(2)}) %collective-permute-start) | collective-permute-done | bytes 1048608 | tf_op jit(solution)/shard_map/ppermute | solution.py:25
  254.4 1.3 copy.94
  (80 shorter events, 2.2 us)
Async XLA Ops:
  8.6 3.8 %copy-start.14 = (s32[64]{0:T(128)}, s32[64]{0:T(128)S(1)}, u32[]{:S(2)}) copy-start(s32[64]{0:T(128)S(1)} %get-tuple-element.17) | copy-start | bytes 772
  14.0 2.7 %copy-start.12 = (f32[1,64]{1,0:T(1,128)S(1)}, f32[1,64]{1,0:T(1,128)}, u32[]{:S(2)}) copy-start(f32[1,64]{1,0:T(1,128)} %param.15) | copy-start | bytes 772
  14.0 3.5 %copy-start.9 = (bf16[1,128,64]{1,2,0:T(8,128)(2,1)S(1)}, bf16[1,128,64]{1,2,0:T(8,128)(2,1)}, u32[]{:S(2)}) copy-start(bf16[1,128,64]{1,2,0:T(8,128)(2,1)} %param.13) | copy-start | bytes 49156
  14.0 4.2 %copy-start.7 = (bf16[1,128,512]{2,1,0:T(8,128)(2,1)S(1)}, bf16[1,128,512]{2,1,0:T(8,128)(2,1)}, u32[]{:S(2)}) copy-start(bf16[1,128,512]{2,1,0:T(8,128)(2,1)} %param.18) | copy-start | bytes 393220
  21.0 3.1 %copy-start.6 = (bf16[64,1,128]{2,1,0:T(2,128)(2,1)S(1)}, bf16[64,1,128]{2,1,0:T(2,128)(2,1)}, u32[]{:S(2)}) copy-start(bf16[64,1,128]{2,1,0:T(2,128)(2,1)} %copy.78) | copy-start | bytes 49156
  24.1 20.4 %copy-start = (s32[1,8192]{1,0:T(1,128)S(1)}, s32[1,8192]{1,0:T(1,128)}, u32[]{:S(2)}) copy-start(s32[1,8192]{1,0:T(1,128)} %param.20) | copy-start | bytes 98308
  24.2 20.5 %copy-start.16 = (s32[64]{0:T(128)S(1)}, s32[64]{0:T(128)}, u32[]{:S(2)}) copy-start(s32[64]{0:T(128)} %get-tuple-element.9) | copy-start | bytes 772
  25.6 19.3 %copy-start.17 = (s32[64]{0:T(128)S(1)}, s32[64]{0:T(128)}, u32[]{:S(2)}) copy-start(s32[64]{0:T(128)} %get-tuple-element.10) | copy-start | bytes 772
  25.6 85.3 %all-to-all-start = ((bf16[64,80,128]{2,1,0:T(8,128)(2,1)}), bf16[64,80,128]{2,1,0:T(8,128)(2,1)}, u32[]{:S(2)}, u32[]{:S(2)}) async-start(bf16[64,80,128]{2,1,0:T(8,128)(2,1)} %maximum_maximum_fusion), calls=%async_computation | async-start | bytes 2621440 | tf_op jit(solution)/shard_map/all_to_all | solution.py:111
  45.7 2.1 copy-start.18
  45.7 68.5 %copy-start.15 = (s32[64]{0:T(128)S(1)}, s32[64]{0:T(128)}, u32[]{:S(2)}) copy-start(s32[64]{0:T(128)} %copy-done.14) | copy-start | bytes 772
  118.6 2.6 %copy-start.4 = (f32[64,64]{1,0:T(8,128)S(1)}, f32[64,64]{1,0:T(8,128)}, u32[]{:S(2)}) copy-start(f32[64,64]{1,0:T(8,128)} %gather_fusion.2) | copy-start | bytes 49156
  124.9 6.3 %copy-start.13 = (f32[1,64]{1,0:T(1,128)S(1)}, f32[1,64]{1,0:T(1,128)}, u32[]{:S(2)}) copy-start(f32[1,64]{1,0:T(1,128)} %param.16) | copy-start | bytes 772
  124.9 83.0 %all-to-all-start.1 = ((bf16[64,96,128]{2,1,0:T(8,128)(2,1)}), bf16[64,96,128]{2,1,0:T(8,128)(2,1)}, u32[]{:S(2)}, u32[]{:S(2)}) async-start(bf16[64,96,128]{2,1,0:T(8,128)(2,1)} %copy.84), calls=%async_computation.1 | async-start | bytes 3145728 | tf_op jit(solution)/shard_map/all_to_all | solution.py:135
  134.0 5.6 %copy-start.5 = (f32[128,8,8]{0,2,1:T(8,128)S(1)}, f32[128,8,8]{0,2,1:T(8,128)}, u32[]{:S(2)}) copy-start(f32[128,8,8]{0,2,1:T(8,128)} %compare_select_fusion.4) | copy-start | bytes 98308
  207.9 1.9 copy-start.1
  217.3 6.6 %copy-start.8 = (bf16[128,2,2,128]{3,0,2,1:T(8,128)(2,1)S(1)}, bf16[128,2,2,128]{3,0,2,1:T(8,128)(2,1)}, u32[]{:S(2)}) copy-start(bf16[128,2,2,128]{3,0,2,1:T(8,128)(2,1)} %copy.90) | copy-start | bytes 393220
  217.3 6.6 %copy-start.10 = (f32[1,4096]{1,0:T(1,128)S(1)}, f32[1,4096]{1,0:T(1,128)}, u32[]{:S(2)}) copy-start(f32[1,4096]{1,0:T(1,128)} %param.17) | copy-start | bytes 49156
  233.0 3.9 %copy-start.2 = (f32[8,8,64,128]{3,2,1,0:T(8,128)S(1)}, f32[8,8,64,128]{3,2,1,0:T(8,128)}, u32[]{:S(2)}) copy-start(f32[8,8,64,128]{3,2,1,0:T(8,128)} %fusion.7) | copy-start | bytes 6291460
  233.0 3.9 %copy-start.3 = (f32[8,8,64,128]{3,2,1,0:T(8,128)S(1)}, f32[8,8,64,128]{3,2,1,0:T(8,128)}, u32[]{:S(2)}) copy-start(f32[8,8,64,128]{3,2,1,0:T(8,128)} %get-tuple-element.12) | copy-start | bytes 6291460
  233.0 3.9 %copy-start.11 = (f32[1,4096]{1,0:T(1,128)S(1)}, f32[1,4096]{1,0:T(1,128)}, u32[]{:S(2)}) copy-start(f32[1,4096]{1,0:T(1,128)} %param.19) | copy-start | bytes 49156
  238.9 15.4 %collective-permute-start = (bf16[1,128,4096]{1,2,0:T(8,128)(2,1)S(1)}, bf16[1,128,4096]{1,2,0:T(8,128)(2,1)S(1)}, u32[]{:S(2)}, u32[]{:S(2)}) collective-permute-start(bf16[1,128,4096]{1,2,0:T(8,128)(2,1)S(1)} %add_convert_fusion), channel_id=1, source_target_pairs={{0,64},{64,128},{128,192},{192,256},{256,320},{320,384},{384,448},... | collective-permute-start | bytes 3145736 | tf_op jit(solution)/shard_map/ppermute | solution.py:25

commit v3 on v1

v3 whole, which is shorter than its diff:
```python
import math

import jax
import jax.numpy as jnp
from jax import lax
from jax.sharding import PartitionSpec as P

HEADS = 64
HEAD_DIM = 64
GROUPS = 8
STATE = 128
QHEADS = 32
KVHEADS = 2
QDIM = 128
HALO = 4
LANES = 128


precise = lax.Precision.HIGHEST
epsilon = 1e-05


def passed_along(value, axis, steps):
    count = lax.axis_size(axis)
    pairs = [(source, (source + steps) % count) for source in range(count)]
    return lax.ppermute(value, axis, pairs)


def group_norm(values, gain):
    grouped = values.reshape(values.shape[0], -1, HEADS // GROUPS * HEAD_DIM)
    normed = grouped * lax.rsqrt(jnp.mean(grouped * grouped, axis=-1, keepdims=True) + epsilon)
    return normed.reshape(values.shape) * gain


def block_terms(values, inject, readout, step_sizes, rates, seg):
    length, heads_here = values.shape[0], values.shape[1]
    groups_here = inject.shape[1]
    within = heads_here // groups_here
    cum_log = jnp.cumsum(-rates * step_sizes, axis=0)
    positions = jnp.arange(length)
    allowed = (positions[:, None] >= positions[None, :]) & (seg[:, None] == seg[None, :])
    spread = cum_log.T[:, :, None] - cum_log.T[:, None, :]
    decays = jnp.where(allowed[None], jnp.exp(jnp.minimum(spread, 0.0)), 0.0)
    scores = jnp.einsum("tgs,ugs->gtu", readout, inject, preferred_element_type=jnp.float32)
    weights = decays.reshape(groups_here, within, length, length) * scores[:, None]
    scaled = values * step_sizes[..., None]
    local_out = jnp.einsum(
        "gktu,ugkp->tgkp",
        weights,
        scaled.reshape(length, groups_here, within, HEAD_DIM),
        precision=precise,
    ).reshape(values.shape)
    ending = cum_log[-1]
    to_end = jnp.where((seg == seg[-1])[:, None], jnp.exp(ending[None, :] - cum_log), 0.0)
    weighted = (scaled * to_end[..., None]).reshape(length, groups_here, within, HEAD_DIM)
    states = jnp.einsum(
        "tgkp,tgs->gkps", weighted, inject.astype(jnp.float32), precision=precise
    ).reshape(heads_here, HEAD_DIM, STATE)
    return local_out, states, cum_log


def on_device(
    mixer_input,
    state_proj,
    dt_raw,
    decay_rate,
    dt_bias,
    skip_gain,
    mamba_gain,
    keys_values,
    attn_gain,
    documents,
    placement_perm,
):
    devices = lax.axis_size("ctx")
    myself = lax.axis_index("ctx")
    tok_rows = mixer_input.shape[1]
    kv_cols = keys_values.shape[2]
    halves = KVHEADS
    half_heads = HEADS // halves
    half_groups = GROUPS // halves
    half_cols = half_heads * HEAD_DIM
    share = devices // half_heads
    slot_rows = HEAD_DIM // share
    kv_half = kv_cols // halves
    slice_cols = kv_half // devices
    kv_rows = tok_rows * slice_cols // LANES

    inverse = (
        jnp.zeros((devices,), jnp.int32)
        .at[placement_perm]
        .set(jnp.arange(devices, dtype=jnp.int32))
    )
    segment = documents[0]
    block_seg = segment.reshape(devices, tok_rows)
    seg_end = block_seg[:, -1]
    seg_prev = jnp.concatenate([jnp.full((1,), -1, jnp.int32), seg_end[:-1]])
    my_block = placement_perm[myself]
    my_seg = lax.dynamic_slice_in_dim(segment, my_block * tok_rows, tok_rows, 0)
    my_prev = seg_prev[my_block]
    positions = jnp.arange(devices)
    linked = (positions[None, :] < positions[:, None]) & (seg_end[None, :] == seg_prev[:, None])
    halo_blocks = placement_perm[:, None] - HALO + jnp.arange(HALO)[None, :]
    halo_src = inverse[jnp.clip(halo_blocks, 0, devices - 1)]

    query_pos = my_block * tok_rows + jnp.arange(tok_rows, dtype=jnp.int32)
    key_pos = (my_block - HALO) * tok_rows + jnp.arange((HALO + 1) * tok_rows, dtype=jnp.int32)
    key_seg = jnp.take(segment, jnp.maximum(key_pos, 0))
    allowed = (
        (my_seg[:, None] == key_seg[None, :])
        & (key_pos[None, :] <= query_pos[:, None])
        & (key_pos[None, :] >= 0)
    )
    score_scale = 1.0 / math.sqrt(QDIM)

    inputs = mixer_input[0]
    projections = state_proj[0]
    raw_all = dt_raw[0]
    kv = keys_values[0]
    my_head = myself // share
    my_part = myself % share

    hidden_parts = []
    attended_parts = []
    for half in range(halves):
        cols = slice(half * half_cols, (half + 1) * half_cols)
        heads = slice(half * half_heads, (half + 1) * half_heads)
        x_half = inputs[:, cols]
        values = x_half.astype(jnp.float32).reshape(tok_rows, half_heads, HEAD_DIM)
        paired = projections[:, half * half_groups * 2 * STATE : (half + 1) * half_groups * 2 * STATE]
        paired = paired.reshape(tok_rows, half_groups, 2, STATE)
        inject = paired[:, :, 0]
        readout = paired[:, :, 1]
        raw_half = raw_all[:, heads]
        step_sizes = jax.nn.softplus(raw_half.astype(jnp.float32) + dt_bias[0][heads])
        local_out, states, cum_log = block_terms(
            values, inject, readout, step_sizes, decay_rate[0][heads], my_seg
        )

        state_slots = states.astype(jnp.bfloat16).reshape(devices, slot_rows, STATE)
        kv_here = jnp.concatenate(
            [
                kv[:, half * QDIM : (half + 1) * QDIM],
                kv[:, kv_half + half * QDIM : kv_half + (half + 1) * QDIM],
            ],
            axis=1,
        )
        kv_slices = kv_here.reshape(tok_rows, devices, slice_cols).transpose(1, 0, 2)
        kv_slices = kv_slices.reshape(devices, kv_rows, LANES)
        raw_cols = jnp.repeat(raw_half.T, share, axis=0).reshape(devices, 1, tok_rows)
        used = slot_rows + kv_rows + 1
        padding = jnp.zeros((devices, -used % 8, LANES), jnp.bfloat16)
        first = jnp.concatenate([state_slots, kv_slices, raw_cols, padding], axis=1)
        got = lax.all_to_all(first, "ctx", split_axis=0, concat_axis=0, tiled=True)
        got_states = got[:, :slot_rows].astype(jnp.float32)
        got_kv = got[:, slot_rows : slot_rows + kv_rows]
        got_raw = got[:, slot_rows + kv_rows].astype(jnp.float32)

        head_id = half * half_heads + my_head
        my_rate = decay_rate[0][head_id]
        my_bias = dt_bias[0][head_id]
        my_steps = jax.nn.softplus(got_raw + my_bias)
        endings = jnp.cumsum(-my_rate * my_steps, axis=1)[:, -1]
        ending_pos = endings[inverse]
        running = jnp.cumsum(ending_pos)
        before = running - ending_pos
        factors = jnp.where(
            linked, jnp.exp(jnp.minimum(before[:, None] - running[None, :], 0.0)), 0.0
        )
        by_device = factors[placement_perm][:, placement_perm]
        entering = jnp.einsum("ds,spn->dpn", by_device, got_states, precision=precise)

        halo = got_kv[halo_src].reshape(devices, HALO * kv_rows, LANES)
        second = jnp.concatenate([entering.astype(jnp.bfloat16), halo], axis=1)
        back = lax.all_to_all(second, "ctx", split_axis=0, concat_axis=0, tiled=True)
        enter_here = back[:, :slot_rows].reshape(
            half_groups, half_heads // half_groups, HEAD_DIM, STATE
        )
        halo_here = back[:, slot_rows:].reshape(devices, HALO * tok_rows, slice_cols)
        halo_kv = halo_here.transpose(1, 0, 2).reshape(HALO * tok_rows, kv_half)

        reach = jnp.where((my_seg == my_prev)[:, None], jnp.exp(cum_log), 0.0)
        read_out = jnp.einsum(
            "tgs,gkps->tgkp", readout, enter_here, preferred_element_type=jnp.float32
        ).reshape(tok_rows, half_heads, HEAD_DIM)
        outputs = local_out + read_out * reach[..., None] + skip_gain[0][heads][:, None] * values
        mamba_out = outputs.astype(jnp.bfloat16).reshape(tok_rows, half_cols)
        residual = x_half.astype(jnp.float32) + group_norm(
            mamba_out.astype(jnp.float32), mamba_gain[0][cols]
        )
        hidden = residual.astype(jnp.bfloat16)
        hidden_parts.append(hidden)

        queries = hidden.reshape(tok_rows, half_cols // QDIM, QDIM)
        all_kv = jnp.concatenate([halo_kv, kv_here], axis=0)
        keys = all_kv[:, :QDIM]
        vals = all_kv[:, QDIM:]
        logits = (
            jnp.einsum("trd,kd->rtk", queries, keys, preferred_element_type=jnp.float32)
            * score_scale
        )
        logits = jnp.where(allowed, logits, -1e30)
        best = jnp.max(logits, axis=-1, keepdims=True)
        weights = jnp.where(allowed, jnp.exp(logits - best), 0.0)
        total_weight = jnp.sum(weights, axis=-1)
        blended = jnp.einsum(
            "rtk,kd->rtd", weights.astype(jnp.bfloat16), vals, preferred_element_type=jnp.float32
        )
        attended = (blended / total_weight[..., None]).transpose(1, 0, 2).reshape(tok_rows, half_cols)
        attended_parts.append(attended)

    hidden = jnp.concatenate(hidden_parts, axis=1)
    attended = jnp.concatenate(attended_parts, axis=1)
    normed = (
        attended
        * lax.rsqrt(jnp.mean(attended * attended, axis=-1, keepdims=True) + epsilon)
        * attn_gain[0]
    )
    result = (hidden.astype(jnp.float32) + normed).astype(jnp.bfloat16)
    return passed_along(result[None], "phase", 1)


def solution(mesh):
    in_specs = (
        P("phase", "ctx", None),
        P("phase", "ctx", None),
        P("phase", "ctx", None),
        P("phase", None),
        P("phase", None),
        P("phase", None),
        P("phase", None),
        P("phase", "ctx", None),
        P("phase", None),
        P("phase", None),
        P(),
    )
    out_specs = P("phase", "ctx", None)
    return jax.shard_map(
        on_device, mesh=mesh, in_specs=in_specs, out_specs=out_specs, check_vma=False
    )
```

time: 333 us -> 282 us (0.85)
  blocking collectives: 118 us -> 56.8 us
  waiting for transfers between devices: 57.6 us -> 85.7 us
  local copies, waits for them, and re-layouts: 71.1 us -> 58 us
  starting transfers between devices: 30.1 us -> 18.3 us
  other arithmetic: 20.8 us -> 26.2 us
    all_gather x1 -> x0, blocking collectives: 118 us -> none  [on_device(): all_endings = lax.all_gather(ending, 'ctx', axis=0, tiled=False)]
    all_to_all x0 -> x1, blocking collectives: none -> 56.8 us  [on_device(): got = lax.all_to_all(first, 'ctx', split_axis=0, concat_axis=0, tiled=True)]
    unnamed x49 -> x91, local copies, waits for them, and re-layouts: 38.8 us -> 4.75 us
    all_to_all x1, waiting for transfers between devices: 0.01 us -> 26.2 us  [on_device(): got = lax.all_to_all(first, 'ctx', split_axis=0, concat_axis=0, tiled=True)]
    all_to_all x1, starting transfers between devices: 18.8 us -> 6.09 us  [on_device(): got = lax.all_to_all(first, 'ctx', split_axis=0, concat_axis=0, tiled=True)]
    all_to_all x4 -> x0, other arithmetic: 12.2 us -> none  [the longest x2 6.47 us: on_device(): lax.all_to_all(second, 'ctx', split_axis=0, concat_axis=0, tiled=True)]
    slice x3 -> x16, local copies, waits for them, and re-layouts: 3.2 us -> 12.6 us  [the longest x4 2.63 us: on_device(): back[:, slot_rows:].reshape(devices, HALO * tok_rows, slice_cols)]
    all_to_all x1 -> x2, waiting for transfers between devices: 42.1 us -> 44 us  [on_device(): lax.all_to_all(second, 'ctx', split_axis=0, concat_axis=0, tiled=True)]
  transfers between devices with their start and end apart: 3 -> 4, of which waited for: 2 -> 4; matrix products, arithmetic and copies ran while one was open for 7% -> 18% of each run, Pallas kernels for 0% -> 0%
where the time goes in v3:
time: 282 us; the launch traced here: 280 us
  waiting for transfers between devices  85.7 us (30%)
  local copies, waits for them, and re-layouts  58 us (21%)
  blocking collectives  56.8 us (20%)
  matrix products  29.1 us (10%)
  other arithmetic  26.2 us (9%)
  starting transfers between devices  18.3 us (6%)
  between operations  5.59 us (2%)
    all_to_all x1, blocking collectives, on_device(): got = lax.all_to_all(first, 'ctx', split_axis=0, concat_axis=0, tiled=True)  56.8 us
    all_to_all x2, waiting for transfers between devices, on_device(): lax.all_to_all(second, 'ctx', split_axis=0, concat_axis=0, tiled=True)  44 us
    all_to_all x1, waiting for transfers between devices, on_device(): got = lax.all_to_all(first, 'ctx', split_axis=0, concat_axis=0, tiled=True)  26.2 us
    ppermute x1, waiting for transfers between devices, passed_along(): return lax.ppermute(value, axis, pairs)  15.4 us
    all_to_all x2, starting transfers between devices, on_device(): lax.all_to_all(second, 'ctx', split_axis=0, concat_axis=0, tiled=True)  12.2 us
    dot_general x2, matrix products, block_terms(): jnp.einsum('gktu,ugkp->tgkp', weights, scaled.reshape(length, groups_here...  10.4 us
    sub x2, matrix products, on_device(): weights = jnp.where(allowed, jnp.exp(logits - best), 0.0)  8.64 us
    all_to_all x1, starting transfers between devices, on_device(): got = lax.all_to_all(first, 'ctx', split_axis=0, concat_axis=0, tiled=True)  6.09 us
  transfers between devices with their start and end apart: 4, of which 4 were waited for; matrix products, arithmetic and copies ran while one was open for 18% of the time, Pallas kernels for 0%

profile of v3, /device:TPU:6, one launch (start us, length us, event | category | flops | bytes accessed | tf_op | source)
XLA Modules:
  0.0 279.7 jit_solution(409057674880032571)
XLA Ops:
  0.0 1.4 dynamic_slice.21
  2.7 0.8 copy.150
  3.6 0.8 negate_bitcast_fusion.1
  7.0 0.8 slice.217
  10.0 1.8 broadcast_compare_fusion
  12.4 1.2 broadcast_compare_fusion.1
  15.0 0.8 fusion.134
  22.2 1.4 maximum_maximum_fusion
  23.6 56.8 %all_to_all.20 = bf16[64,40,128]{2,1,0:T(8,128)(2,1)} all-to-all(bf16[64,40,128]{2,1,0:T(8,128)(2,1)S(1)} %get-tuple-element.39), channel_id=1, replica_groups=mesh['phase'=8,'ctx'=64] {'ctx'}, dimensions={0} | all-to-all | bytes 1310720 | tf_op jit(solution)/shard_map/all_to_all | solution.py:154
  80.4 6.1 %all-to-all-start.2 = ((bf16[64,40,128]{2,1,0:T(8,128)(2,1)}), bf16[64,40,128]{2,1,0:T(8,128)(2,1)}, u32[]{:S(2)}, u32[]{:S(2)}) async-start(bf16[64,40,128]{2,1,0:T(8,128)(2,1)} %get-tuple-element.40), calls=%async_computation.2 | async-start | bytes 1310720 | tf_op jit(solution)/shard_map/all_to_all | solution.py:154
  89.3 0.8 scatter_custom_fusion
  90.1 1.9 gather_fusion.3
  92.7 0.9 reshape.672
  93.6 1.6 fusion.109
  95.3 0.8 gather_fusion
  96.8 1.2 sub.135
  98.0 26.2 %all-to-all-done.2 = bf16[64,40,128]{2,1,0:T(8,128)(2,1)} async-done(((bf16[64,40,128]{2,1,0:T(8,128)(2,1)}), bf16[64,40,128]{2,1,0:T(8,128)(2,1)}, u32[]{:S(2)}, u32[]{:S(2)}) %all-to-all-start.2) | async-done | bytes 655392 | tf_op jit(solution)/shard_map/all_to_all | solution.py:154
  124.3 0.9 slice.233
  125.2 0.8 fusion.108
  126.0 0.8 gather_fusion.5
  128.3 0.8 exponential_select_fusion.5
  129.1 1.2 gather_fusion.6
  130.3 0.8 copy.183
  131.1 1.2 gather_fusion.7
  132.3 1.6 slice.235
  133.8 2.5 gather_fusion.8
  136.3 1.0 copy.186
  137.4 1.1 slice.234
  139.2 1.4 copy.187
  140.6 6.1 %all-to-all-start.3 = ((bf16[64,48,128]{2,1,0:T(8,128)(2,1)}), bf16[64,48,128]{2,1,0:T(8,128)(2,1)}, u32[]{:S(2)}, u32[]{:S(2)}) async-start(bf16[64,48,128]{2,1,0:T(8,128)(2,1)} %copy.187), calls=%async_computation.3 | async-start | bytes 1572864 | tf_op jit(solution)/shard_map/all_to_all | solution.py:175
  148.3 1.5 copy.152
  149.8 1.5 copy.172
  152.0 1.2 gather_fusion.2
  153.2 0.9 slice.223
  154.1 1.7 gather_fusion.4
  155.8 1.0 copy.168
  156.8 1.1 slice.222
  157.9 1.4 convolution_convert_fusion.3
  159.4 1.4 copy.169
  160.8 28.7 %all-to-all-done.3 = bf16[64,48,128]{2,1,0:T(8,128)(2,1)} async-done(((bf16[64,48,128]{2,1,0:T(8,128)(2,1)}), bf16[64,48,128]{2,1,0:T(8,128)(2,1)}, u32[]{:S(2)}, u32[]{:S(2)}) %all-to-all-start.3) | async-done | bytes 786464 | tf_op jit(solution)/shard_map/all_to_all | solution.py:175
  189.5 6.1 %all-to-all-start.1 = ((bf16[64,48,128]{2,1,0:T(8,128)(2,1)}), bf16[64,48,128]{2,1,0:T(8,128)(2,1)}, u32[]{:S(2)}, u32[]{:S(2)}) async-start(bf16[64,48,128]{2,1,0:T(8,128)(2,1)} %copy.169), calls=%async_computation.1 | async-start | bytes 1572864 | tf_op jit(solution)/shard_map/all_to_all | solution.py:175
  195.6 1.6 exponential_select_fusion.3
  197.1 0.9 copy.170
  198.0 0.9 copy.188
  199.6 4.1 %gather_fusion.9 = s32[640]{0:T(1024)S(1)} fusion(s32[8192]{0:T(1024)S(1)} %bitcast.281, s32[1024]{0:T(1024)} %pad_clamp_fusion), kind=kCustom, calls=%fused_computation.9 | custom fusion | bytes 7680 | tf_op jit(solution)/shard_map/jit(_take)/gather | solution.py:108
  203.8 0.8 fusion.104
  204.5 1.6 and_and_fusion
  206.1 1.2 fusion.85
  207.6 5.2 %fusion.18 = f32[4,8,64,128]{3,2,1,0:T(8,128)} fusion(f32[4,128,128]{2,1,0:T(8,128)S(1)} %fusion.85, f32[4,8,128]{2,1,0:T(8,128)S(1)} %bitcast.332, pred[128,128]{1,0:T(8,128)(4,1)S(1)} %fusion.104, f32[128,4,8,64]{0,3,2,1:T(8,128)S(1)} %bitcast.292, f32[128,4,8]{0,2,1:T(8,128)S(1)} %bitcast.325), kind=kOutput, calls=%fused_computation.35 | convolution fusion | flops 405012480 | bytes 2408448 | tf_op jit(solution)/shard_map/gktu,ugkp->tgkp/dot_general | solution.py:47
  212.8 5.2 %fusion.24 = f32[4,8,64,128]{3,2,1,0:T(8,128)} fusion(f32[4,128,128]{2,1,0:T(8,128)S(1)} %fusion.91, f32[4,8,128]{2,1,0:T(8,128)S(1)} %bitcast.331, pred[128,128]{1,0:T(8,128)(4,1)S(1)} %fusion.104, f32[128,4,8,64]{0,3,2,1:T(8,128)S(1)} %bitcast.290, f32[128,4,8]{0,2,1:T(8,128)S(1)} %bitcast.323), kind=kOutput, calls=%fused_computation.41 | convolution fusion | flops 405012480 | bytes 2408448 | tf_op jit(solution)/shard_map/gktu,ugkp->tgkp/dot_general | solution.py:47
  218.6 1.0 slice.240
  220.5 1.1 slice.236
  222.6 15.4 %all-to-all-done.1 = bf16[64,48,128]{2,1,0:T(8,128)(2,1)} async-done(((bf16[64,48,128]{2,1,0:T(8,128)(2,1)}), bf16[64,48,128]{2,1,0:T(8,128)(2,1)}, u32[]{:S(2)}, u32[]{:S(2)}) %all-to-all-start.1) | async-done | bytes 786464 | tf_op jit(solution)/shard_map/all_to_all | solution.py:175
  238.0 1.1 slice.224
  239.4 2.0 bitcast_reduce_fusion.1
  241.4 1.0 slice.237
  243.4 1.6 fusion.44
  245.0 4.8 %fusion.137 = (f32[16,128]{1,0:T(8,128)S(1)}, bf16[16,128,640]{1,2,0:T(8,128)(2,1)}) fusion(pred[128,640]{0,1:T(8,128)(4,1)} %and_and_fusion, bf16[128,16,128]{0,2,1:T(8,128)(2,1)S(1)} %bitcast.301, bf16[640,256]{1,0:T(8,128)(2,1)S(1)} %maximum_maximum_fusion.2), kind=kOutput, calls=%fused_computation.221 | convolution fusion | flops 343409280 | bytes 3481600 | tf_op jit(solution)/shard_map/sub | solution.py:204
  249.9 2.4 fusion.33
  252.3 3.8 %fusion.136 = (f32[16,128]{1,0:T(8,128)S(1)}, bf16[16,128,640]{1,2,0:T(8,128)(2,1)}) fusion(pred[128,640]{0,1:T(8,128)(4,1)S(1)} %copy-done.19, bf16[128,16,128]{0,2,1:T(8,128)(2,1)S(1)} %bitcast.303, bf16[640,256]{1,0:T(8,128)(2,1)S(1)} %copy-done.8), kind=kOutput, calls=%fused_computation.220 | convolution fusion | flops 343409280 | bytes 3481600 | tf_op jit(solution)/shard_map/sub | solution.py:204
  256.1 2.4 fusion.39
  259.2 3.7 %fusion.16 = bf16[1,128,4096]{1,2,0:T(8,128)(2,1)S(1)} fusion(f32[1,128,2048]{1,2,0:T(8,128)S(1)} %bitcast.288, f32[1,128,2048]{1,2,0:T(8,128)S(1)} %bitcast.286, bf16[1,128,2048]{1,2,0:T(8,128)(2,1)S(1)} %bitcast.304, bf16[1,128,2048]{1,2,0:T(8,128)(2,1)S(1)} %bitcast.302, f32[4096]{0:T(1024)S(1)} %bitcast.330, f32[128]{0:T(128)S(1)} %add_rsqrt_fusion.2), kind=kLoop, calls=%fused_computation.32 | loop fusion | flops 4718592 | bytes 4211200 | tf_op jit(solution)/shard_map/convert_element_type | solution.py:219
  263.0 15.4 %collective-permute-done = bf16[1,128,4096]{1,2,0:T(8,128)(2,1)S(1)} collective-permute-done((bf16[1,128,4096]{1,2,0:T(8,128)(2,1)S(1)}, bf16[1,128,4096]{1,2,0:T(8,128)(2,1)S(1)}, u32[]{:S(2)}, u32[]{:S(2)}) %collective-permute-start) | collective-permute-done | bytes 1048608 | tf_op jit(solution)/shard_map/ppermute | solution.py:26
  278.4 1.3 copy.201
  (179 shorter events, 24.0 us)
Async XLA Ops:
  0.0 18.1 %copy-start.7 = (bf16[1,128,2048]{2,1,0:T(8,128)(2,1)S(1)}, bf16[1,128,2048]{2,1,0:T(8,128)(2,1)}, u32[]{:S(2)}) copy-start(bf16[1,128,2048]{2,1,0:T(8,128)(2,1)} %param.12) | copy-start | bytes 1572868
  4.7 13.3 %copy-start.4 = (f32[128,32]{1,0:T(8,128)}, f32[128,32]{1,0:T(8,128)S(1)}, u32[]{:S(2)}) copy-start(f32[128,32]{1,0:T(8,128)S(1)} %reduce_window_sum.39) | copy-start | bytes 49156
  5.6 12.4 %copy-start.6 = (f32[128,32]{1,0:T(8,128)}, f32[128,32]{1,0:T(8,128)S(1)}, u32[]{:S(2)}) copy-start(f32[128,32]{1,0:T(8,128)S(1)} %reduce_window_sum.41) | copy-start | bytes 49156
  7.8 11.3 %copy-start.3 = (bf16[1,128,4096]{2,1,0:T(8,128)(2,1)S(1)}, bf16[1,128,4096]{2,1,0:T(8,128)(2,1)}, u32[]{:S(2)}) copy-start(bf16[1,128,4096]{2,1,0:T(8,128)(2,1)} %param.11) | copy-start | bytes 3145732
  9.4 0.6 copy-start.36
  9.4 79.9 %copy-start.38 = (s32[64]{0:T(128)}, s32[64]{0:T(128)S(1)}, u32[]{:S(2)}) copy-start(s32[64]{0:T(128)S(1)} %get-tuple-element.52) | copy-start | bytes 772
  11.8 1.8 copy-start.32
  15.8 0.6 copy-start.9
  15.9 0.6 copy-start.11
  15.9 0.6 copy-start.13
  17.8 3.6 %copy-start.20 = (f32[128,32]{0,1:T(8,128)}, f32[128,32]{0,1:T(8,128)S(1)}, u32[]{:S(2)}) copy-start(f32[128,32]{0,1:T(8,128)S(1)} %copy.151) | copy-start | bytes 49156
  17.9 2.7 copy-start.22
  19.8 0.7 copy-start.24
  19.8 0.7 copy-start.25
  19.8 0.7 copy-start.42
  19.8 1.0 copy-start.1
  20.0 2.2 copy-start.15
  20.0 2.2 copy-start.16
  20.0 2.2 copy-start.17
  22.2 64.3 %copy-start = (s32[1,8192]{1,0:T(1,128)S(1)}, s32[1,8192]{1,0:T(1,128)}, u32[]{:S(2)}) copy-start(s32[1,8192]{1,0:T(1,128)} %param.20) | copy-start | bytes 98308
  22.2 64.4 %copy-start.33 = (f32[1,64]{1,0:T(1,128)S(1)}, f32[1,64]{1,0:T(1,128)}, u32[]{:S(2)}) copy-start(f32[1,64]{1,0:T(1,128)} %param.14) | copy-start | bytes 772
  22.2 64.4 %copy-start.34 = (f32[1,64]{1,0:T(1,128)S(1)}, f32[1,64]{1,0:T(1,128)}, u32[]{:S(2)}) copy-start(f32[1,64]{1,0:T(1,128)} %param.15) | copy-start | bytes 772
  80.4 43.9 %all-to-all-start.2 = ((bf16[64,40,128]{2,1,0:T(8,128)(2,1)}), bf16[64,40,128]{2,1,0:T(8,128)(2,1)}, u32[]{:S(2)}, u32[]{:S(2)}) async-start(bf16[64,40,128]{2,1,0:T(8,128)(2,1)} %get-tuple-element.40), calls=%async_computation.2 | async-start | bytes 1310720 | tf_op jit(solution)/shard_map/all_to_all | solution.py:154
  90.1 3.5 %copy-start.39 = (s32[64]{0:T(128)S(1)}, s32[64]{0:T(128)}, u32[]{:S(2)}) copy-start(s32[64]{0:T(128)} %copy-done.38) | copy-start | bytes 772
  96.1 0.6 copy-start.41
  126.8 0.5 copy-start.40
  132.3 6.2 %copy-start.18 = (f32[64,64]{1,0:T(8,128)S(1)}, f32[64,64]{1,0:T(8,128)}, u32[]{:S(2)}) copy-start(f32[64,64]{1,0:T(8,128)} %gather_fusion.7) | copy-start | bytes 49156
  139.1 8.3 %copy-start.37 = (f32[1,64]{1,0:T(1,128)S(1)}, f32[1,64]{1,0:T(1,128)}, u32[]{:S(2)}) copy-start(f32[1,64]{1,0:T(1,128)} %param.16) | copy-start | bytes 772
  140.6 48.9 %all-to-all-start.3 = ((bf16[64,48,128]{2,1,0:T(8,128)(2,1)}), bf16[64,48,128]{2,1,0:T(8,128)(2,1)}, u32[]{:S(2)}, u32[]{:S(2)}) async-start(bf16[64,48,128]{2,1,0:T(8,128)(2,1)} %copy.187), calls=%async_computation.3 | async-start | bytes 1572864 | tf_op jit(solution)/shard_map/all_to_all | solution.py:175
  159.3 36.3 %copy-start.5 = (f32[128,32]{1,0:T(8,128)S(1)}, f32[128,32]{1,0:T(8,128)}, u32[]{:S(2)}) copy-start(f32[128,32]{1,0:T(8,128)} %copy-done.4) | copy-start | bytes 49156
  159.3 36.3 %copy-start.35 = (pred[128]{0:T(512)(128)(4,1)S(1)}, pred[128]{0:T(512)(128)(4,1)}, u32[]{:S(2)}) copy-start(pred[128]{0:T(512)(128)(4,1)} %get-tuple-element.9) | copy-start | bytes 388
  189.5 48.5 %all-to-all-start.1 = ((bf16[64,48,128]{2,1,0:T(8,128)(2,1)}), bf16[64,48,128]{2,1,0:T(8,128)(2,1)}, u32[]{:S(2)}, u32[]{:S(2)}) async-start(bf16[64,48,128]{2,1,0:T(8,128)(2,1)} %copy.169), calls=%async_computation.1 | async-start | bytes 1572864 | tf_op jit(solution)/shard_map/all_to_all | solution.py:175
  199.6 8.0 %copy-start.23 = (f32[128,32]{0,1:T(8,128)S(1)}, f32[128,32]{0,1:T(8,128)}, u32[]{:S(2)}) copy-start(f32[128,32]{0,1:T(8,128)} %copy-done.22) | copy-start | bytes 49156
  199.6 8.0 %copy-start.30 = (f32[32,128]{1,0:T(8,128)S(1)}, f32[32,128]{1,0:T(8,128)}, u32[]{:S(2)}) copy-start(f32[32,128]{1,0:T(8,128)} %copy.172) | copy-start | bytes 49156
  207.3 5.5 %copy-start.21 = (f32[128,32]{0,1:T(8,128)S(1)}, f32[128,32]{0,1:T(8,128)}, u32[]{:S(2)}) copy-start(f32[128,32]{0,1:T(8,128)} %copy-done.20) | copy-start | bytes 49156
  207.3 5.5 %copy-start.29 = (f32[32,128]{1,0:T(8,128)S(1)}, f32[32,128]{1,0:T(8,128)}, u32[]{:S(2)}) copy-start(f32[32,128]{1,0:T(8,128)} %copy.152) | copy-start | bytes 49156
  212.8 5.2 %copy-start.31 = (f32[1,4096]{1,0:T(1,128)S(1)}, f32[1,4096]{1,0:T(1,128)}, u32[]{:S(2)}) copy-start(f32[1,4096]{1,0:T(1,128)} %param.17) | copy-start | bytes 49156
  218.6 3.0 %copy-start.12 = (bf16[128,128]{1,0:T(8,128)(2,1)S(1)}, bf16[128,128]{1,0:T(8,128)(2,1)}, u32[]{:S(2)}) copy-start(bf16[128,128]{1,0:T(8,128)(2,1)} %copy-done.11) | copy-start | bytes 98308
  218.6 3.0 %copy-start.14 = (bf16[128,128]{1,0:T(8,128)(2,1)S(1)}, bf16[128,128]{1,0:T(8,128)(2,1)}, u32[]{:S(2)}) copy-start(bf16[128,128]{1,0:T(8,128)(2,1)} %copy-done.13) | copy-start | bytes 98308
  219.5 2.8 %copy-start.2 = (bf16[128,1024]{0,1:T(8,128)(2,1)S(1)}, bf16[128,1024]{0,1:T(8,128)(2,1)}, u32[]{:S(2)}) copy-start(bf16[128,1024]{0,1:T(8,128)(2,1)} %get-tuple-element.18) | copy-start | bytes 786436
  222.3 17.0 %copy-start.26 = (f32[2048]{0:T(1024)S(1)}, f32[2048]{0:T(1024)}, u32[]{:S(2)}) copy-start(f32[2048]{0:T(1024)} %mul.296) | copy-start | bytes 24580
  241.4 2.0 copy-start.10
  241.4 2.0 copy-start.27
  249.9 2.4 copy-start.8
  249.9 2.4 copy-start.19
  258.5 0.7 copy-start.28
  262.9 15.4 %collective-permute-start = (bf16[1,128,4096]{1,2,0:T(8,128)(2,1)S(1)}, bf16[1,128,4096]{1,2,0:T(8,128)(2,1)S(1)}, u32[]{:S(2)}, u32[]{:S(2)}) collective-permute-start(bf16[1,128,4096]{1,2,0:T(8,128)(2,1)S(1)} %fusion.16), channel_id=1, source_target_pairs={{0,64},{64,128},{128,192},{192,256},{256,320},{320,384},{384,448},... | collective-permute-start | bytes 3145736 | tf_op jit(solution)/shard_map/ppermute | solution.py:26

commit v4 on v2

--- a/solution.py
+++ b/solution.py
@@ -100,9 +100,9 @@
 
     kv = keys_values[0]
     lanes = 128
-    kv_rows = tok_rows * slice_cols // lanes
-    kv_slices = kv.reshape(tok_rows, devices, slice_cols).transpose(1, 0, 2)
-    kv_slices = kv_slices.reshape(devices, kv_rows, lanes)
+    share = tok_rows // devices
+    kv_rows = share * kv_cols // lanes
+    kv_slices = kv.reshape(devices, kv_rows, lanes)
     raw_cols = dt_raw[0].T.reshape(HEADS, 1, tok_rows)
     state_slots = states.astype(jnp.bfloat16)
     used = HEAD_DIM + kv_rows + 1
@@ -134,8 +134,12 @@
     second = jnp.concatenate([entering.astype(jnp.bfloat16), halo], axis=1)
     back = lax.all_to_all(second, "ctx", split_axis=0, concat_axis=0, tiled=True)
     enter_here = back[:, :HEAD_DIM].reshape(GROUPS, HEADS // GROUPS, HEAD_DIM, STATE)
-    halo_here = back[:, HEAD_DIM:].reshape(devices, HALO * tok_rows, slice_cols)
-    halo_kv = halo_here.transpose(1, 0, 2).reshape(HALO * tok_rows, kv_cols)
+    halo_kv = back[:, HEAD_DIM:].reshape(devices * HALO * share, kv_cols)
+    halo_pos = (
+        (my_block - HALO + jnp.arange(HALO))[None, :, None] * tok_rows
+        + share * jnp.arange(devices)[:, None, None]
+        + jnp.arange(share)[None, None, :]
+    ).reshape(-1)
 
     reach = jnp.where((my_seg == my_prev)[:, None], jnp.exp(cum_log), 0.0)
     read_out = jnp.einsum(
@@ -147,40 +151,51 @@
     hidden = residual.astype(jnp.bfloat16)
 
     repeat = QHEADS // KVHEADS
-    queries = hidden.reshape(tok_rows, KVHEADS, repeat, QDIM)
     all_kv = jnp.concatenate([halo_kv, kv], axis=0).reshape(-1, 2, KVHEADS, QDIM)
     keys = all_kv[:, 0]
     vals = all_kv[:, 1]
-    query_pos = my_block * tok_rows + jnp.arange(tok_rows, dtype=jnp.int32)
-    key_pos = (my_block - HALO) * tok_rows + jnp.arange((HALO + 1) * tok_rows, dtype=jnp.int32)
+    key_pos = jnp.concatenate(
+        [halo_pos, my_block * tok_rows + jnp.arange(tok_rows, dtype=jnp.int32)]
+    )
     key_seg = jnp.take(segment, jnp.maximum(key_pos, 0))
-    allowed = (
-        (my_seg[:, None] == key_seg[None, :])
-        & (key_pos[None, :] <= query_pos[:, None])
-        & (key_pos[None, :] >= 0)
-    )
     score_scale = 1.0 / math.sqrt(QDIM)
-    logits = (
-        jnp.einsum("tgrd,kgd->grtk", queries, keys, preferred_element_type=jnp.float32)
-        * score_scale
-    )
-    logits = jnp.where(allowed, logits, -1e30)
-    best = jnp.max(logits, axis=-1, keepdims=True)
-    weights = jnp.where(allowed, jnp.exp(logits - best), 0.0)
-    total_weight = jnp.sum(weights, axis=-1)
-    blended = jnp.einsum(
-        "grtk,kgd->grtd", weights.astype(jnp.bfloat16), vals, preferred_element_type=jnp.float32
-    )
-    attended = (
-        (blended / total_weight[..., None]).transpose(2, 0, 1, 3).reshape(tok_rows, QHEADS * QDIM)
-    )
-    normed = (
-        attended
-        * lax.rsqrt(jnp.mean(attended * attended, axis=-1, keepdims=True) + epsilon)
-        * attn_gain[0]
-    )
-    result = (hidden.astype(jnp.float32) + normed).astype(jnp.bfloat16)
-    return passed_along(result[None], "phase", 1)
+    pieces = 2
+    rows = tok_rows // pieces
+    handed = []
+    for piece in range(pieces):
+        part = slice(piece * rows, (piece + 1) * rows)
+        hidden_part = hidden[part]
+        if handed:
+            hidden_part, _ = lax.optimization_barrier((hidden_part, result))
+        queries = hidden_part.reshape(rows, KVHEADS, repeat, QDIM)
+        query_pos = my_block * tok_rows + piece * rows + jnp.arange(rows, dtype=jnp.int32)
+        allowed = (
+            (my_seg[part][:, None] == key_seg[None, :])
+            & (key_pos[None, :] <= query_pos[:, None])
+            & (key_pos[None, :] >= 0)
+        )
+        logits = (
+            jnp.einsum("tgrd,kgd->grtk", queries, keys, preferred_element_type=jnp.float32)
+            * score_scale
+        )
+        logits = jnp.where(allowed, logits, -1e30)
+        best = jnp.max(logits, axis=-1, keepdims=True)
+        weights = jnp.where(allowed, jnp.exp(logits - best), 0.0)
+        total_weight = jnp.sum(weights, axis=-1)
+        blended = jnp.einsum(
+            "grtk,kgd->grtd", weights.astype(jnp.bfloat16), vals, preferred_element_type=jnp.float32
+        )
+        attended = (
+            (blended / total_weight[..., None]).transpose(2, 0, 1, 3).reshape(rows, QHEADS * QDIM)
+        )
+        normed = (
+            attended
+            * lax.rsqrt(jnp.mean(attended * attended, axis=-1, keepdims=True) + epsilon)
+            * attn_gain[0]
+        )
+        result = (hidden_part.astype(jnp.float32) + normed).astype(jnp.bfloat16)
+        handed.append(passed_along(result[None], "phase", 1))
+    return jnp.concatenate(handed, axis=1)
 
 
 def solution(mesh):

time: 257 us -> 245 us (0.953)
  local copies, waits for them, and re-layouts: 44.8 us -> 32.8 us
  other arithmetic: 15.5 us -> 20.5 us
  waiting for transfers between devices: 137 us -> 132 us
    ppermute x1 -> x2, waiting for transfers between devices: 15.4 us -> 8.13 us  [passed_along(): return lax.ppermute(value, axis, pairs)]
    convert_element_type x2 -> x3, other arithmetic: 2.14 us -> 6.54 us  [the longest x2 3.77 us: on_device(): result = (hidden_part.astype(jnp.float32) + normed).astype(jnp.bfloat16)]
    transpose x2 -> x0, local copies, waits for them, and re-layouts: 4.05 us -> none  [the longest x1 3.14 us: on_device(): halo_kv = halo_here.transpose(1, 0, 2).reshape(HALO * tok_rows, kv_cols)]
    reshape x1 -> x2, local copies, waits for them, and re-layouts: 1.09 us -> 3.8 us  [on_device(): (blended / total_weight[..., None]).transpose(2, 0, 1, 3)]
    concatenate x2, local copies, waits for them, and re-layouts: 2.82 us -> 0.22 us  [on_device(): jnp.concatenate([halo_kv, kv], axis=0).reshape(-1, 2, KVHEADS, QDIM)]
    dot_general x1 -> x2, matrix products: 3.87 us -> 6.32 us  [on_device(): jnp.einsum('grtk,kgd->grtd', weights.astype(jnp.bfloat16), vals, preferre...]
    unnamed x45 -> x39, local copies, waits for them, and re-layouts: 5.83 us -> 3.67 us
    sub x1 -> x2, matrix products: 9.04 us -> 10.3 us  [on_device(): weights = jnp.where(allowed, jnp.exp(logits - best), 0.0)]
  transfers between devices with their start and end apart: 3 -> 4, of which waited for: 3 -> 3; matrix products, arithmetic and copies ran while one was open for 8% -> 12% of each run, Pallas kernels for 0% -> 0%
where the time goes in v4:
time: 245 us; the launch traced here: 244 us
  waiting for transfers between devices  132 us (54%)
  local copies, waits for them, and re-layouts  32.8 us (13%)
  matrix products  28.7 us (12%)
  starting transfers between devices  26.5 us (11%)
  other arithmetic  20.5 us (8%)
  between operations  3.82 us (2%)
    all_to_all x1, waiting for transfers between devices, on_device(): got = lax.all_to_all(first, 'ctx', split_axis=0, concat_axis=0, tiled=True)  62.4 us
    all_to_all x1, waiting for transfers between devices, on_device(): lax.all_to_all(second, 'ctx', split_axis=0, concat_axis=0, tiled=True)  61.2 us
    all_to_all x1, starting transfers between devices, on_device(): got = lax.all_to_all(first, 'ctx', split_axis=0, concat_axis=0, tiled=True)  18.6 us
    sub x2, matrix products, on_device(): weights = jnp.where(allowed, jnp.exp(logits - best), 0.0)  10.3 us
    dot_general x1, matrix products, block_terms(): jnp.einsum('gktu,ugkp->tgkp', weights, scaled.reshape(length, GROUPS, wit...  8.36 us
    ppermute x2, waiting for transfers between devices, passed_along(): return lax.ppermute(value, axis, pairs)  8.13 us
    dot_general x2, matrix products, on_device(): jnp.einsum('grtk,kgd->grtd', weights.astype(jnp.bfloat16), vals, preferre...  6.32 us
    all_to_all x1, starting transfers between devices, on_device(): lax.all_to_all(second, 'ctx', split_axis=0, concat_axis=0, tiled=True)  6.24 us
  transfers between devices with their start and end apart: 4, of which 3 were waited for; matrix products, arithmetic and copies ran while one was open for 12% of the time, Pallas kernels for 0%

profile of v4, /device:TPU:6, one launch (start us, length us, event | category | flops | bytes accessed | tf_op | source)
XLA Modules:
  0.0 244.1 jit_solution(16424647703096649767)
XLA Ops:
  0.0 1.4 dynamic_slice.15
  2.6 0.7 negate_bitcast_fusion
  3.3 0.8 copy.61
  4.1 0.7 fusion.80
  4.8 0.2 reduce_window_sum.27
  5.7 0.5 broadcast.402
  6.3 1.3 reduce.17
  7.7 0.8 compare_select_fusion.4
  8.6 0.8 slice.97
  10.1 0.7 broadcast_add_fusion.1
  10.9 0.6 dynamic_slice.19
  11.5 1.3 broadcast_compare_fusion.1
  12.8 0.6 slice.68
  13.3 0.6 broadcast_compare_fusion.2
  14.1 1.0 reshape_squeeze.11
  15.1 1.3 copy.63
  16.4 0.7 copy.60
  17.3 1.3 fusion.44
  18.6 1.4 maximum_maximum_fusion
  20.0 18.6 %all-to-all-start = ((bf16[64,80,128]{2,1,0:T(8,128)(2,1)}), bf16[64,80,128]{2,1,0:T(8,128)(2,1)S(1)}, u32[]{:S(2)}, u32[]{:S(2)}) async-start(bf16[64,80,128]{2,1,0:T(8,128)(2,1)} %maximum_maximum_fusion), calls=%async_computation | async-start | bytes 2621440 | tf_op jit(solution)/shard_map/all_to_all | solution.py:111
  38.9 0.8 scatter_custom_fusion
  39.8 1.9 gather_fusion.3
  41.9 0.7 constant_dynamic-slice_fusion
  42.6 62.4 %all-to-all-done = bf16[64,80,128]{2,1,0:T(8,128)(2,1)S(1)} async-done(((bf16[64,80,128]{2,1,0:T(8,128)(2,1)}), bf16[64,80,128]{2,1,0:T(8,128)(2,1)S(1)}, u32[]{:S(2)}, u32[]{:S(2)}) %all-to-all-start) | async-done | bytes 1310752 | tf_op jit(solution)/shard_map/all_to_all | solution.py:111
  105.0 0.7 fusion.86
  105.7 0.8 fusion.85
  106.5 0.8 gather_fusion
  107.7 0.6 gather_fusion.1
  108.4 0.6 gather_fusion.2
  109.0 1.6 gather_fusion.4
  110.6 1.2 copy.74
  111.8 0.1 slice.100
  111.9 1.4 convolution_convert_fusion
  113.4 0.1 pad_maximum_fusion
  113.5 2.2 copy.75
  115.7 6.2 %all-to-all-start.1 = ((bf16[64,96,128]{2,1,0:T(8,128)(2,1)}), bf16[64,96,128]{2,1,0:T(8,128)(2,1)}, u32[]{:S(2)}, u32[]{:S(2)}) async-start(bf16[64,96,128]{2,1,0:T(8,128)(2,1)} %copy.75), calls=%async_computation.1 | async-start | bytes 3145728 | tf_op jit(solution)/shard_map/all_to_all | solution.py:135
  122.7 0.1 iota_add_fusion
  122.8 0.2 add.292
  123.0 0.2 concatenate.50
  123.3 0.6 reduce.18
  124.4 0.2 copy.79
  124.6 3.9 %gather_fusion.5 = s32[640]{0:T(1024)S(1)} fusion(s32[8192]{0:T(1024)S(1)} %bitcast.214, s32[1024]{0:T(1024)S(1)} %pad_clamp_fusion), kind=kCustom, calls=%fused_computation.5 | custom fusion | bytes 7680 | tf_op jit(solution)/shard_map/jit(_take)/gather | solution.py:160
  128.7 0.1 and_and_fusion.1
  128.9 0.3 fusion.73
  129.1 8.4 %fusion.2 = f32[8,8,64,128]{3,2,1,0:T(8,128)S(1)} fusion(f32[8,128,128]{2,1,0:T(8,128)S(1)} %fusion.73, f32[8,8,128]{2,1,0:T(8,128)S(1)} %bitcast.235, pred[128,128]{1,0:T(8,128)(4,1)S(1)} %fusion.81, f32[128,8,8]{0,2,1:T(8,128)S(1)} %compare_select_fusion.4, bf16[128,8,8,64]{0,3,2,1:T(8,128)(2,1)S(1)} %bitcast.216), kind=kOutput, calls=%fused_computation.13 | convolution fusion | flops 810549248 | bytes 3751936 | tf_op jit(solution)/shard_map/gktu,ugkp->tgkp/dot_general | solution.py:45
  137.5 61.2 %all-to-all-done.1 = bf16[64,96,128]{2,1,0:T(8,128)(2,1)} async-done(((bf16[64,96,128]{2,1,0:T(8,128)(2,1)}), bf16[64,96,128]{2,1,0:T(8,128)(2,1)}, u32[]{:S(2)}, u32[]{:S(2)}) %all-to-all-start.1) | async-done | bytes 1572896 | tf_op jit(solution)/shard_map/all_to_all | solution.py:135
  198.7 1.1 slice.104
  199.9 1.5 slice.102
  201.5 0.7 multiply_reduce_fusion
  202.2 2.8 %fusion.31 = bf16[128,4096]{0,1:T(8,128)(2,1)S(1)} fusion(f32[8,8,64,128]{3,2,1,0:T(8,128)S(1)} %get-tuple-element.22, f32[8,8,64,128]{3,2,1,0:T(8,128)} %copy-done.1, f32[4096]{0:T(1024)S(1)} %bitcast.236, f32[128,8]{0,1:T(8,128)S(1)} %add_rsqrt_fusion, f32[4096]{0:T(1024)S(1)} %mul.204, f32[128,64]{0,1:T(8,128)S(1)} %copy.76, ...), kind=kLoop, calls=%fused_computation.46 | loop fusion | flops 5767168 | bytes 6361088 | tf_op jit(solution)/shard_map/convert_element_type | solution.py:151
  205.0 1.3 fusion.110
  206.4 5.5 %fusion.112 = (f32[2,16,64]{2,1,0:T(8,128)S(1)}, bf16[2,16,64,640]{3,2,1,0:T(8,128)(2,1)}) fusion(pred[64,640]{1,0:T(8,128)(4,1)S(1)} %get-tuple-element.13, bf16[640,2,128,1]{2,0,3,1:T(8,128)(2,1)S(1)} %fusion.68, bf16[64,2,16,128]{0,3,2,1:T(8,128)(2,1)} %bitcast.229), kind=kOutput, calls=%fused_computation.172 | convolution fusion | flops 343409280 | bytes 3522560 | tf_op jit(solution)/shard_map/sub | solution.py:183
  211.9 3.6 %multiply_reduce_fusion.2 = (f32[64]{0:T(128)S(1)}, f32[64,2,16,128]{3,0,2,1:T(8,128)}) fusion(f32[64,2,16]{0,2,1:T(8,128)S(1)} %bitcast.244, bf16[128,2,2,128]{3,0,2,1:T(8,128)(2,1)S(1)} %copy.79, bf16[512,2,2,128]{3,0,2,1:T(8,128)(2,1)S(1)} %copy-done.6, bf16[2,16,64,640]{3,2,1,0:T(8,128)(2,1)} %get-tuple-element.24), kind=kOutput, calls=%fused_computation.73 | convolution fusion | flops 336986048 | bytes 4333824 | tf_op jit(solution)/shard_map/grtk,kgd->grtd/dot_general | solution.py:185
  215.6 3.2 %copy.98 = f32[64,2,16,128]{0,3,2,1:T(8,128)} copy(f32[64,2,16,128]{3,0,2,1:T(8,128)} %get-tuple-element.26) | data formatting | bytes 2097152 | tf_op jit(solution)/shard_map/reshape | solution.py:189
  218.7 1.9 fusion.28
  220.7 1.1 copy.84
  221.8 4.8 %fusion.113 = (f32[2,16,64]{2,1,0:T(8,128)S(1)}, bf16[2,16,64,640]{3,2,1,0:T(8,128)(2,1)}) fusion(pred[64,640]{1,0:T(8,128)(4,1)S(1)} %get-tuple-element.14, bf16[640,2,128,1]{2,0,3,1:T(8,128)(2,1)} %copy-done.10, bf16[64,2,16,128]{0,3,2,1:T(8,128)(2,1)S(1)} %bitcast.225), kind=kOutput, calls=%fused_computation.173 | convolution fusion | flops 343409280 | bytes 3522560 | tf_op jit(solution)/shard_map/sub | solution.py:183
  226.6 2.7 %multiply_reduce_fusion.1 = (f32[64]{0:T(128)S(1)}, f32[64,2,16,128]{3,0,2,1:T(8,128)S(1)}) fusion(f32[64,2,16]{0,2,1:T(8,128)S(1)} %bitcast.243, bf16[128,2,2,128]{3,0,2,1:T(8,128)(2,1)S(1)} %copy.79, bf16[512,2,2,128]{3,0,2,1:T(8,128)(2,1)S(1)} %copy-done.7, bf16[2,16,64,640]{3,2,1,0:T(8,128)(2,1)} %get-tuple-element.28), kind=kOutput, calls=%fused_computation.72 | convolution fusion | flops 336986048 | bytes 4333824 | tf_op jit(solution)/shard_map/grtk,kgd->grtd/dot_general | solution.py:185
  229.3 0.6 copy.99
  230.0 1.8 fusion.25
  231.8 0.3 copy.88
  232.1 1.7 collective-permute-start.1
  233.8 8.1 %collective-permute-done.1 = bf16[1,64,4096]{2,1,0:T(8,128)(2,1)S(1)} collective-permute-done((bf16[1,64,4096]{2,1,0:T(8,128)(2,1)S(1)}, bf16[1,64,4096]{2,1,0:T(8,128)(2,1)S(1)}, u32[]{:S(2)}, u32[]{:S(2)}) %collective-permute-start.1) | collective-permute-done | bytes 524320 | tf_op jit(solution)/shard_map/ppermute | solution.py:25
  242.0 2.1 pad_maximum_fusion.1
  (87 shorter events, 2.7 us)
Async XLA Ops:
  0.0 16.4 %copy-start.8 = (bf16[1,128,4096]{2,1,0:T(8,128)(2,1)S(1)}, bf16[1,128,4096]{2,1,0:T(8,128)(2,1)}, u32[]{:S(2)}) copy-start(bf16[1,128,4096]{2,1,0:T(8,128)(2,1)} %param.11) | copy-start | bytes 3145732
  16.4 112.4 %copy-start.2 = (bf16[1,128,2048]{1,2,0:T(8,128)(2,1)}, bf16[1,128,2048]{1,2,0:T(8,128)(2,1)S(1)}, u32[]{:S(2)}) copy-start(bf16[1,128,2048]{1,2,0:T(8,128)(2,1)S(1)} %copy.63) | copy-start | bytes 1572868
  18.5 20.0 %copy-start = (s32[1,8192]{1,0:T(1,128)S(1)}, s32[1,8192]{1,0:T(1,128)}, u32[]{:S(2)}) copy-start(s32[1,8192]{1,0:T(1,128)} %param.20) | copy-start | bytes 98308
  20.0 85.0 %all-to-all-start = ((bf16[64,80,128]{2,1,0:T(8,128)(2,1)}), bf16[64,80,128]{2,1,0:T(8,128)(2,1)S(1)}, u32[]{:S(2)}, u32[]{:S(2)}) async-start(bf16[64,80,128]{2,1,0:T(8,128)(2,1)} %maximum_maximum_fusion), calls=%async_computation | async-start | bytes 2621440 | tf_op jit(solution)/shard_map/all_to_all | solution.py:111
  39.7 2.1 copy-start.13
  39.7 2.1 copy-start.15
  115.7 7.4 %copy-start.9 = (bf16[1,128,512]{2,1,0:T(8,128)(2,1)S(1)}, bf16[1,128,512]{2,1,0:T(8,128)(2,1)}, u32[]{:S(2)}) copy-start(bf16[1,128,512]{2,1,0:T(8,128)(2,1)} %param.18) | copy-start | bytes 393220
  115.7 7.6 %copy-start.14 = (f32[1,64]{1,0:T(1,128)S(1)}, f32[1,64]{1,0:T(1,128)}, u32[]{:S(2)}) copy-start(f32[1,64]{1,0:T(1,128)} %param.16) | copy-start | bytes 772
  115.7 83.0 %all-to-all-start.1 = ((bf16[64,96,128]{2,1,0:T(8,128)(2,1)}), bf16[64,96,128]{2,1,0:T(8,128)(2,1)}, u32[]{:S(2)}, u32[]{:S(2)}) async-start(bf16[64,96,128]{2,1,0:T(8,128)(2,1)} %copy.75), calls=%async_computation.1 | async-start | bytes 3145728 | tf_op jit(solution)/shard_map/all_to_all | solution.py:135
  137.5 63.9 %copy-start.1 = (f32[8,8,64,128]{3,2,1,0:T(8,128)}, f32[8,8,64,128]{3,2,1,0:T(8,128)S(1)}, u32[]{:S(2)}) copy-start(f32[8,8,64,128]{3,2,1,0:T(8,128)S(1)} %fusion.2) | copy-start | bytes 6291460
  198.7 2.7 %copy-start.3 = (bf16[1,128,2048]{1,2,0:T(8,128)(2,1)S(1)}, bf16[1,128,2048]{1,2,0:T(8,128)(2,1)}, u32[]{:S(2)}) copy-start(bf16[1,128,2048]{1,2,0:T(8,128)(2,1)} %copy-done.2) | copy-start | bytes 1572868
  199.9 6.4 %copy-start.5 = (bf16[512,2,2,128]{3,0,2,1:T(8,128)(2,1)}, bf16[512,2,2,128]{3,0,2,1:T(8,128)(2,1)S(1)}, u32[]{:S(2)}) copy-start(bf16[512,2,2,128]{3,0,2,1:T(8,128)(2,1)S(1)} %copy.78) | copy-start | bytes 1572868
  201.4 0.8 copy-start.12
  206.3 15.5 %copy-start.4 = (bf16[64,4096]{0,1:T(8,128)(2,1)}, bf16[64,4096]{0,1:T(8,128)(2,1)S(1)}, u32[]{:S(2)}) copy-start(bf16[64,4096]{0,1:T(8,128)(2,1)S(1)} %get-tuple-element.6) | copy-start | bytes 1572868
  206.4 5.5 %copy-start.10 = (bf16[640,2,128,1]{2,0,3,1:T(8,128)(2,1)}, bf16[640,2,128,1]{2,0,3,1:T(8,128)(2,1)S(1)}, u32[]{:S(2)}) copy-start(bf16[640,2,128,1]{2,0,3,1:T(8,128)(2,1)S(1)} %fusion.68) | copy-start | bytes 983044
  206.4 5.5 %copy-start.6 = (bf16[512,2,2,128]{3,0,2,1:T(8,128)(2,1)S(1)}, bf16[512,2,2,128]{3,0,2,1:T(8,128)(2,1)}, u32[]{:S(2)}) copy-start(bf16[512,2,2,128]{3,0,2,1:T(8,128)(2,1)} %copy-done.5) | copy-start | bytes 1572868
  215.5 3.2 %copy-start.11 = (f32[1,4096]{1,0:T(1,128)S(1)}, f32[1,4096]{1,0:T(1,128)}, u32[]{:S(2)}) copy-start(f32[1,4096]{1,0:T(1,128)} %param.19) | copy-start | bytes 49156
  221.8 12.0 %collective-permute-start = (bf16[1,64,4096]{2,1,0:T(8,128)(2,1)}, bf16[1,64,4096]{2,1,0:T(8,128)(2,1)}, u32[]{:S(2)}, u32[]{:S(2)}) collective-permute-start(bf16[1,64,4096]{2,1,0:T(8,128)(2,1)} %copy.84), channel_id=1, source_target_pairs={{0,64},{64,128},{128,192},{192,256},{256,320},{320,384},{384,448},... | collective-permute-start | bytes 1572872 | tf_op jit(solution)/shard_map/ppermute | solution.py:25
  221.8 4.8 %copy-start.7 = (bf16[512,2,2,128]{3,0,2,1:T(8,128)(2,1)S(1)}, bf16[512,2,2,128]{3,0,2,1:T(8,128)(2,1)}, u32[]{:S(2)}) copy-start(bf16[512,2,2,128]{3,0,2,1:T(8,128)(2,1)} %copy-done.5) | copy-start | bytes 1572868
  232.1 9.8 %collective-permute-start.1 = (bf16[1,64,4096]{2,1,0:T(8,128)(2,1)S(1)}, bf16[1,64,4096]{2,1,0:T(8,128)(2,1)S(1)}, u32[]{:S(2)}, u32[]{:S(2)}) collective-permute-start(bf16[1,64,4096]{2,1,0:T(8,128)(2,1)S(1)} %copy.88), channel_id=1, source_target_pairs={{0,64},{64,128},{128,192},{192,256},{256,320},{320,384},{384,448},... | collective-permute-start | bytes 1572872 | tf_op jit(solution)/shard_map/ppermute | solution.py:25

commit v5 on v4

--- a/solution.py
+++ b/solution.py
@@ -3,6 +3,8 @@
 import jax
 import jax.numpy as jnp
 from jax import lax
+from jax.experimental import pallas as pl
+from jax.experimental.pallas import tpu as pltpu
 from jax.sharding import PartitionSpec as P
 
 HEADS = 64
@@ -57,6 +59,65 @@
     return local_out, states, cum_log, ending
 
 
+def attention_kernel(q_ref, kv_ref, qpos_ref, qseg_ref, kpos_ref, kseg_ref, gain_ref, out_ref, acc_ref):
+    repeat = QHEADS // KVHEADS
+    kv_width = KVHEADS * QDIM
+    score_scale = 1.0 / math.sqrt(QDIM)
+    allowed = (
+        (qseg_ref[...] == kseg_ref[...])
+        & (kpos_ref[...] <= qpos_ref[...])
+        & (kpos_ref[...] >= 0)
+    )
+
+    def one_head(head, squares):
+        group = head // repeat
+        q = q_ref[:, pl.ds(pl.multiple_of(head * QDIM, QDIM), QDIM)]
+        k = kv_ref[:, pl.ds(pl.multiple_of(group * QDIM, QDIM), QDIM)]
+        v = kv_ref[:, pl.ds(pl.multiple_of(kv_width + group * QDIM, QDIM), QDIM)]
+        logits = (
+            lax.dot_general(q, k, (((1,), (1,)), ((), ())), preferred_element_type=jnp.float32)
+            * score_scale
+        )
+        logits = jnp.where(allowed, logits, -1e30)
+        best = jnp.max(logits, axis=-1, keepdims=True)
+        weights = jnp.where(allowed, jnp.exp(logits - best), 0.0)
+        total = jnp.sum(weights, axis=-1, keepdims=True)
+        blended = jnp.dot(weights.astype(jnp.bfloat16), v, preferred_element_type=jnp.float32)
+        attended = blended / total
+        acc_ref[:, pl.ds(pl.multiple_of(head * QDIM, QDIM), QDIM)] = attended
+        return squares + jnp.sum(attended * attended, axis=-1, keepdims=True)
+
+    squares = lax.fori_loop(0, QHEADS, one_head, jnp.zeros((q_ref.shape[0], 1), jnp.float32))
+    scale = lax.rsqrt(squares / (QHEADS * QDIM) + epsilon)
+    out_ref[...] = (
+        q_ref[...].astype(jnp.float32) + acc_ref[...] * scale * gain_ref[...]
+    ).astype(out_ref.dtype)
+
+
+def attention_block(hidden_part, all_kv, query_pos, query_seg, key_pos, key_seg, gain):
+    rows = hidden_part.shape[0]
+    keys = all_kv.shape[0]
+    flops = 4 * rows * keys * QDIM * QHEADS
+    return pl.pallas_call(
+        attention_kernel,
+        out_shape=jax.ShapeDtypeStruct(hidden_part.shape, jnp.bfloat16),
+        scratch_shapes=[pltpu.VMEM(hidden_part.shape, jnp.float32)],
+        cost_estimate=pl.CostEstimate(
+            flops=flops,
+            transcendentals=rows * keys * QHEADS,
+            bytes_accessed=2 * hidden_part.size * 2 + all_kv.size * 2,
+        ),
+    )(
+        hidden_part,
+        all_kv,
+        query_pos.reshape(rows, 1),
+        query_seg.reshape(rows, 1),
+        key_pos.reshape(1, keys),
+        key_seg.reshape(1, keys),
+        gain.reshape(1, -1),
+    )
+
+
 def on_device(
     mixer_input,
     state_proj,
@@ -150,15 +211,11 @@
     residual = inputs.astype(jnp.float32) + group_norm(mamba_out.astype(jnp.float32), mamba_gain[0])
     hidden = residual.astype(jnp.bfloat16)
 
-    repeat = QHEADS // KVHEADS
-    all_kv = jnp.concatenate([halo_kv, kv], axis=0).reshape(-1, 2, KVHEADS, QDIM)
-    keys = all_kv[:, 0]
-    vals = all_kv[:, 1]
+    all_kv_flat = jnp.concatenate([halo_kv, kv], axis=0)
     key_pos = jnp.concatenate(
         [halo_pos, my_block * tok_rows + jnp.arange(tok_rows, dtype=jnp.int32)]
     )
     key_seg = jnp.take(segment, jnp.maximum(key_pos, 0))
-    score_scale = 1.0 / math.sqrt(QDIM)
     pieces = 2
     rows = tok_rows // pieces
     handed = []
@@ -167,33 +224,10 @@
         hidden_part = hidden[part]
         if handed:
             hidden_part, _ = lax.optimization_barrier((hidden_part, result))
-        queries = hidden_part.reshape(rows, KVHEADS, repeat, QDIM)
         query_pos = my_block * tok_rows + piece * rows + jnp.arange(rows, dtype=jnp.int32)
-        allowed = (
-            (my_seg[part][:, None] == key_seg[None, :])
-            & (key_pos[None, :] <= query_pos[:, None])
-            & (key_pos[None, :] >= 0)
+        result = attention_block(
+            hidden_part, all_kv_flat, query_pos, my_seg[part], key_pos, key_seg, attn_gain[0]
         )
-        logits = (
-            jnp.einsum("tgrd,kgd->grtk", queries, keys, preferred_element_type=jnp.float32)
-            * score_scale
-        )
-        logits = jnp.where(allowed, logits, -1e30)
-        best = jnp.max(logits, axis=-1, keepdims=True)
-        weights = jnp.where(allowed, jnp.exp(logits - best), 0.0)
-        total_weight = jnp.sum(weights, axis=-1)
-        blended = jnp.einsum(
-            "grtk,kgd->grtd", weights.astype(jnp.bfloat16), vals, preferred_element_type=jnp.float32
-        )
-        attended = (
-            (blended / total_weight[..., None]).transpose(2, 0, 1, 3).reshape(rows, QHEADS * QDIM)
-        )
-        normed = (
-            attended
-            * lax.rsqrt(jnp.mean(attended * attended, axis=-1, keepdims=True) + epsilon)
-            * attn_gain[0]
-        )
-        result = (hidden_part.astype(jnp.float32) + normed).astype(jnp.bfloat16)
         handed.append(passed_along(result[None], "phase", 1))
     return jnp.concatenate(handed, axis=1)
 

time: 245 us -> 279 us (1.14)
  Pallas kernels: 0 us -> 38.9 us
  local copies, waits for them, and re-layouts: 32.8 us -> 51.2 us
  matrix products: 28.7 us -> 14.4 us
  waiting for transfers between devices: 132 us -> 121 us
    pallas_call x0 -> x2, Pallas kernels: none -> 38.9 us  [attention_block(): pl.pallas_call(attention_kernel, out_shape=jax.ShapeDtypeStruct(hidden_pa...]
    all_to_all x1, waiting for transfers between devices: 61.2 us -> 49.2 us  [on_device(): lax.all_to_all(second, 'ctx', split_axis=0, concat_axis=0, tiled=True)]
    sub x2 -> x0, matrix products: 10.3 us -> none  [on_device(): weights = jnp.where(allowed, jnp.exp(logits - best), 0.0)]
    dot_general x2 -> x0, matrix products: 6.32 us -> none  [on_device(): jnp.einsum('grtk,kgd->grtd', weights.astype(jnp.bfloat16), vals, preferre...]
    ppermute x2, waiting for transfers between devices: 8.13 us -> 13.9 us  [passed_along(): return lax.ppermute(value, axis, pairs)]
    reshape x2 -> x7, local copies, waits for them, and re-layouts: 3.8 us -> 8.45 us  [the longest x1 2.89 us: block_terms(): local_out = jnp.einsum('gktu,ugkp->tgkp', weights, scaled.reshape(length,...]
    mul x0 -> x3, local copies, waits for them, and re-layouts: none -> 4.59 us  [the longest x2 4.39 us: on_device(): read_out * reach[..., None]]
    all_to_all x1, waiting for transfers between devices: 62.4 us -> 58 us  [on_device(): got = lax.all_to_all(first, 'ctx', split_axis=0, concat_axis=0, tiled=True)]
  transfers between devices with their start and end apart: 4 -> 4, of which waited for: 3 -> 4; matrix products, arithmetic and copies ran while one was open for 12% -> 13% of each run, Pallas kernels for 0% -> 0%
where the time goes in v5:
time: 279 us; the launch traced here: 278 us
  waiting for transfers between devices  121 us (43%)
  local copies, waits for them, and re-layouts  51.2 us (18%)
  Pallas kernels  38.9 us (14%)
  starting transfers between devices  26.5 us (9%)
  other arithmetic  21.8 us (8%)
  matrix products  14.4 us (5%)
  between operations  3.58 us (1%)
    all_to_all x1, waiting for transfers between devices, on_device(): got = lax.all_to_all(first, 'ctx', split_axis=0, concat_axis=0, tiled=True)  58 us
    all_to_all x1, waiting for transfers between devices, on_device(): lax.all_to_all(second, 'ctx', split_axis=0, concat_axis=0, tiled=True)  49.2 us
    pallas_call x2, Pallas kernels, attention_block(): pl.pallas_call(attention_kernel, out_shape=jax.ShapeDtypeStruct(hidden_pa...  38.9 us
    all_to_all x1, starting transfers between devices, on_device(): got = lax.all_to_all(first, 'ctx', split_axis=0, concat_axis=0, tiled=True)  18.6 us
    ppermute x2, waiting for transfers between devices, passed_along(): return lax.ppermute(value, axis, pairs)  13.9 us
    dot_general x1, matrix products, block_terms(): jnp.einsum('gktu,ugkp->tgkp', weights, scaled.reshape(length, GROUPS, wit...  9.57 us
    unnamed x48, local copies, waits for them, and re-layouts  6.79 us
    all_to_all x1, starting transfers between devices, on_device(): lax.all_to_all(second, 'ctx', split_axis=0, concat_axis=0, tiled=True)  6.23 us
  transfers between devices with their start and end apart: 4, of which 4 were waited for; matrix products, arithmetic and copies ran while one was open for 13% of the time, Pallas kernels for 0%

profile of v5, /device:TPU:6, one launch (start us, length us, event | category | flops | bytes accessed | tf_op | source)
XLA Modules:
  0.0 277.6 jit_solution(12253973243402030570)
XLA Ops:
  0.0 1.3 dynamic_slice.15
  2.5 0.7 negate_bitcast_fusion
  3.1 0.8 copy.58
  4.0 0.7 fusion.38
  6.1 1.3 reduce.15
  7.5 0.8 compare_select_fusion.4
  8.4 0.8 slice.89
  10.0 1.2 broadcast_add_fusion.1
  11.7 1.3 broadcast_compare_fusion
  13.6 0.6 broadcast_compare_fusion.1
  14.4 1.0 reshape_squeeze.11
  15.4 1.3 copy.60
  16.7 1.7 copy.57
  19.1 1.2 fusion.21
  20.3 1.4 maximum_maximum_fusion
  21.8 18.6 %all-to-all-start = ((bf16[64,80,128]{2,1,0:T(8,128)(2,1)}), bf16[64,80,128]{2,1,0:T(8,128)(2,1)S(1)}, u32[]{:S(2)}, u32[]{:S(2)}) async-start(bf16[64,80,128]{2,1,0:T(8,128)(2,1)} %maximum_maximum_fusion), calls=%async_computation | async-start | bytes 2621440 | tf_op jit(solution)/shard_map/all_to_all | solution.py:172
  40.4 0.7 copy.86
  41.3 0.9 scatter_custom_fusion
  42.2 1.9 gather_fusion.3
  44.1 0.7 gather.27
  44.8 0.8 compare_select_fusion.1
  45.6 0.7 reshape.538
  46.3 0.7 constant_dynamic-slice_fusion
  48.2 0.7 pad_clamp_fusion.1
  48.8 58.0 %all-to-all-done = bf16[64,80,128]{2,1,0:T(8,128)(2,1)S(1)} async-done(((bf16[64,80,128]{2,1,0:T(8,128)(2,1)}), bf16[64,80,128]{2,1,0:T(8,128)(2,1)S(1)}, u32[]{:S(2)}, u32[]{:S(2)}) %all-to-all-start) | async-done | bytes 1310752 | tf_op jit(solution)/shard_map/all_to_all | solution.py:172
  106.8 0.6 fusion.42
  107.4 0.7 fusion.41
  108.2 0.9 gather_fusion
  109.6 0.7 copy.67
  110.3 0.9 reduce-window.7
  111.9 0.8 exponential_select_fusion.1
  112.6 1.2 gather_fusion.1
  113.8 0.8 copy.68
  114.6 1.2 gather_fusion.2
  115.8 0.7 slice.93
  116.5 2.5 gather_fusion.4
  119.0 1.2 copy.71
  120.4 1.4 convolution_convert_fusion
  121.9 2.2 copy.72
  124.2 6.2 %all-to-all-start.1 = ((bf16[64,96,128]{2,1,0:T(8,128)(2,1)}), bf16[64,96,128]{2,1,0:T(8,128)(2,1)}, u32[]{:S(2)}, u32[]{:S(2)}) async-start(bf16[64,96,128]{2,1,0:T(8,128)(2,1)} %copy.72), calls=%async_computation.1 | async-start | bytes 3145728 | tf_op jit(solution)/shard_map/all_to_all | solution.py:196
  131.7 0.6 reduce.16
  132.7 0.7 copy.79.qseg_ref
  133.4 0.7 copy.78.qseg_ref
  135.0 1.4 mul.147
  136.4 3.0 %copy.75 = f32[128,4096]{1,0:T(8,128)} copy(f32[128,4096]{0,1:T(8,128)} %bitcast.127) | data formatting | bytes 4194304 | tf_op jit(solution)/shard_map/mul | solution.py:209
  139.7 9.6 %fusion = f32[8,8,64,128]{3,2,1,0:T(8,128)} fusion(f32[8,128,128]{2,1,0:T(8,128)S(1)} %fusion.31, f32[8,8,128]{2,1,0:T(8,128)S(1)} %bitcast.139, pred[128,128]{1,0:T(8,128)(4,1)S(1)} %fusion.39, f32[128,8,8,64]{0,3,2,1:T(8,128)S(1)} %bitcast.122, f32[128,8,8]{0,2,1:T(8,128)S(1)} %copy-done.11), kind=kOutput, calls=%fused_computation.7 | convolution fusion | flops 810024960 | bytes 4800512 | tf_op jit(solution)/shard_map/gktu,ugkp->tgkp/dot_general | solution.py:47
  149.3 2.9 %copy.76 = f32[128,4096]{1,0:T(8,128)} copy(f32[128,4096]{0,1:T(8,128)} %bitcast.124) | data formatting | bytes 4194304 | tf_op jit(solution)/shard_map/reshape | solution.py:52
  152.2 3.9 %gather_fusion.5 = s32[640]{0:T(1024)S(1)} fusion(s32[8192]{0:T(1024)S(1)} %bitcast.120, s32[1024]{0:T(1024)S(1)} %pad_clamp_fusion), kind=kCustom, calls=%fused_computation.5 | custom fusion | bytes 7680 | tf_op jit(solution)/shard_map/jit(_take)/gather | solution.py:218
  157.9 49.2 %all-to-all-done.1 = bf16[64,96,128]{2,1,0:T(8,128)(2,1)} async-done(((bf16[64,96,128]{2,1,0:T(8,128)(2,1)}), bf16[64,96,128]{2,1,0:T(8,128)(2,1)}, u32[]{:S(2)}, u32[]{:S(2)}) %all-to-all-start.1) | async-done | bytes 1572896 | tf_op jit(solution)/shard_map/all_to_all | solution.py:196
  207.1 1.9 slice.96
  209.0 1.4 reshape.497
  210.4 1.5 slice.94
  212.3 1.9 multiply_reduce_fusion
  214.2 2.1 copy.74
  216.7 1.7 copy.89
  219.1 0.9 fusion.11
  220.0 1.1 fusion.60
  221.1 0.9 pad_maximum_fusion.2.kv_ref
  222.0 19.4 %shard_map.109 = bf16[64,4096]{1,0:T(8,128)(2,1)} custom-call(bf16[64,4096]{1,0:T(8,128)(2,1)} %get-tuple-element.9.q_ref, bf16[640,512]{1,0:T(8,128)(2,1)} %pad_maximum_fusion.2.kv_ref, s32[64,1]{1,0:T(8,128)} %iota_add_fusion.2.qpos_ref, s32[64,1]{1,0:T(8,128)} %copy.78.qseg_ref, s32[1,640]{1,0:T(1,128)} %reshape.499.kpos_ref, ...), custom_call_target="tpu_custom_call" | custom-call | flops 671088640 | bytes 1703936 | tf_op jit(solution)/shard_map/pallas_call | solution.py:101
  241.4 19.5 %shard_map.110 = bf16[64,4096]{1,0:T(8,128)(2,1)} custom-call(bf16[64,4096]{1,0:T(8,128)(2,1)} %get-tuple-element.6.q_ref, bf16[640,512]{1,0:T(8,128)(2,1)} %pad_maximum_fusion.2.kv_ref, s32[64,1]{1,0:T(8,128)} %iota_add_fusion.1.qpos_ref, s32[64,1]{1,0:T(8,128)} %copy.79.qseg_ref, s32[1,640]{1,0:T(1,128)} %reshape.499.kpos_ref, ...), custom_call_target="tpu_custom_call" | custom-call | flops 671088640 | bytes 1703936 | tf_op jit(solution)/shard_map/pallas_call | solution.py:101
  260.9 1.7 collective-permute-start
  262.6 8.3 %collective-permute-done.1 = bf16[1,64,4096]{2,1,0:T(8,128)(2,1)S(1)} collective-permute-done((bf16[1,64,4096]{2,1,0:T(8,128)(2,1)}, bf16[1,64,4096]{2,1,0:T(8,128)(2,1)S(1)}, u32[]{:S(2)}, u32[]{:S(2)}) %collective-permute-start.1) | collective-permute-done | bytes 524320 | tf_op jit(solution)/shard_map/ppermute | solution.py:27
  270.9 5.6 %collective-permute-done = bf16[1,64,4096]{2,1,0:T(8,128)(2,1)S(1)} collective-permute-done((bf16[1,64,4096]{2,1,0:T(8,128)(2,1)S(1)}, bf16[1,64,4096]{2,1,0:T(8,128)(2,1)S(1)}, u32[]{:S(2)}, u32[]{:S(2)}) %collective-permute-start) | collective-permute-done | bytes 524320 | tf_op jit(solution)/shard_map/ppermute | solution.py:27
  276.5 1.1 pad_maximum_fusion.1
  (97 shorter events, 11.5 us)
Async XLA Ops:
  8.3 10.8 %copy-start.10 = (f32[128,8,8]{0,2,1:T(8,128)}, f32[128,8,8]{0,2,1:T(8,128)S(1)}, u32[]{:S(2)}) copy-start(f32[128,8,8]{0,2,1:T(8,128)S(1)} %compare_select_fusion.4) | copy-start | bytes 98308
  11.2 2.5 copy-start.16
  13.0 5.4 %copy-start.13 = (pred[128]{0:T(512)(128)(4,1)}, pred[128]{0:T(512)(128)(4,1)S(1)}, u32[]{:S(2)}) copy-start(pred[128]{0:T(512)(128)(4,1)S(1)} %get-tuple-element.7) | copy-start | bytes 388
  16.7 3.6 %copy-start.4 = (bf16[1,128,2048]{1,2,0:T(8,128)(2,1)}, bf16[1,128,2048]{1,2,0:T(8,128)(2,1)S(1)}, u32[]{:S(2)}) copy-start(bf16[1,128,2048]{1,2,0:T(8,128)(2,1)S(1)} %copy.60) | copy-start | bytes 1572868
  20.3 20.0 %copy-start = (s32[1,8192]{1,0:T(1,128)S(1)}, s32[1,8192]{1,0:T(1,128)}, u32[]{:S(2)}) copy-start(s32[1,8192]{1,0:T(1,128)} %param.20) | copy-start | bytes 98308
  21.8 85.0 %all-to-all-start = ((bf16[64,80,128]{2,1,0:T(8,128)(2,1)}), bf16[64,80,128]{2,1,0:T(8,128)(2,1)S(1)}, u32[]{:S(2)}, u32[]{:S(2)}) async-start(bf16[64,80,128]{2,1,0:T(8,128)(2,1)} %maximum_maximum_fusion), calls=%async_computation | async-start | bytes 2621440 | tf_op jit(solution)/shard_map/all_to_all | solution.py:172
  42.2 4.1 %copy-start.15 = (f32[1,64]{1,0:T(1,128)S(1)}, f32[1,64]{1,0:T(1,128)}, u32[]{:S(2)}) copy-start(f32[1,64]{1,0:T(1,128)} %param.15) | copy-start | bytes 772
  42.2 4.0 %copy-start.19 = (f32[1,64]{1,0:T(1,128)S(1)}, f32[1,64]{1,0:T(1,128)}, u32[]{:S(2)}) copy-start(f32[1,64]{1,0:T(1,128)} %param.14) | copy-start | bytes 772
  109.1 0.5 copy-start.17
  116.5 3.9 %copy-start.9 = (f32[64,64]{1,0:T(8,128)S(1)}, f32[64,64]{1,0:T(8,128)}, u32[]{:S(2)}) copy-start(f32[64,64]{1,0:T(8,128)} %gather_fusion.2) | copy-start | bytes 49156
  124.2 7.6 %copy-start.18 = (f32[1,64]{1,0:T(1,128)S(1)}, f32[1,64]{1,0:T(1,128)}, u32[]{:S(2)}) copy-start(f32[1,64]{1,0:T(1,128)} %param.16) | copy-start | bytes 772
  124.2 10.0 %copy-start.14 = (pred[128]{0:T(512)(128)(4,1)S(1)}, pred[128]{0:T(512)(128)(4,1)}, u32[]{:S(2)}) copy-start(pred[128]{0:T(512)(128)(4,1)} %copy-done.13) | copy-start | bytes 388
  124.2 83.0 %all-to-all-start.1 = ((bf16[64,96,128]{2,1,0:T(8,128)(2,1)}), bf16[64,96,128]{2,1,0:T(8,128)(2,1)}, u32[]{:S(2)}, u32[]{:S(2)}) async-start(bf16[64,96,128]{2,1,0:T(8,128)(2,1)} %copy.72), calls=%async_computation.1 | async-start | bytes 3145728 | tf_op jit(solution)/shard_map/all_to_all | solution.py:196
  136.4 3.1 %copy-start.5 = (bf16[1,128,2048]{1,2,0:T(8,128)(2,1)S(1)}, bf16[1,128,2048]{1,2,0:T(8,128)(2,1)}, u32[]{:S(2)}) copy-start(bf16[1,128,2048]{1,2,0:T(8,128)(2,1)} %copy-done.4) | copy-start | bytes 1572868
  136.4 3.3 %copy-start.11 = (f32[128,8,8]{0,2,1:T(8,128)S(1)}, f32[128,8,8]{0,2,1:T(8,128)}, u32[]{:S(2)}) copy-start(f32[128,8,8]{0,2,1:T(8,128)} %copy-done.10) | copy-start | bytes 98308
  157.9 53.9 %copy-start.8 = (f32[128,8,8]{0,2,1:T(8,128)S(1)}, f32[128,8,8]{0,2,1:T(8,128)}, u32[]{:S(2)}) copy-start(f32[128,8,8]{0,2,1:T(8,128)} %get-tuple-element.11) | copy-start | bytes 98308
  210.4 1.9 copy-start.3
  216.5 1.9 copy-start.6
  216.5 1.9 copy-start.12
  216.7 1.8 copy-start.1
  216.7 2.4 copy-start.2
  220.0 1.1 copy-start.7
  241.4 19.5 %copy-start.20 = (bf16[64,4096]{1,0:T(8,128)(2,1)S(1)}, bf16[64,4096]{1,0:T(8,128)(2,1)}, u32[]{:S(2)}) copy-start(bf16[64,4096]{1,0:T(8,128)(2,1)} %shard_map.109) | copy-start | bytes 1572868
  260.9 10.0 %collective-permute-start.1 = (bf16[1,64,4096]{2,1,0:T(8,128)(2,1)}, bf16[1,64,4096]{2,1,0:T(8,128)(2,1)S(1)}, u32[]{:S(2)}, u32[]{:S(2)}) collective-permute-start(bf16[1,64,4096]{2,1,0:T(8,128)(2,1)} %bitcast.148), channel_id=1, source_target_pairs={{0,64},{64,128},{128,192},{192,256},{256,320},{320,384},{384,448},... | collective-permute-start | bytes 1572872 | tf_op jit(solution)/shard_map/ppermute | solution.py:27
  260.9 15.6 %collective-permute-start = (bf16[1,64,4096]{2,1,0:T(8,128)(2,1)S(1)}, bf16[1,64,4096]{2,1,0:T(8,128)(2,1)S(1)}, u32[]{:S(2)}, u32[]{:S(2)}) collective-permute-start(bf16[1,64,4096]{2,1,0:T(8,128)(2,1)S(1)} %bitcast.147), channel_id=1, source_target_pairs={{0,64},{64,128},{128,192},{192,256},{256,320},{320,384},{384,448},... | collective-permute-start | bytes 1572872 | tf_op jit(solution)/shard_map/ppermute | solution.py:27

commit v6 on v4

--- a/solution.py
+++ b/solution.py
@@ -159,7 +159,7 @@
     )
     key_seg = jnp.take(segment, jnp.maximum(key_pos, 0))
     score_scale = 1.0 / math.sqrt(QDIM)
-    pieces = 2
+    pieces = 4
     rows = tok_rows // pieces
     handed = []
     for piece in range(pieces):
@@ -180,7 +180,7 @@
         )
         logits = jnp.where(allowed, logits, -1e30)
         best = jnp.max(logits, axis=-1, keepdims=True)
-        weights = jnp.where(allowed, jnp.exp(logits - best), 0.0)
+        weights = jnp.exp(logits - best)
         total_weight = jnp.sum(weights, axis=-1)
         blended = jnp.einsum(
             "grtk,kgd->grtd", weights.astype(jnp.bfloat16), vals, preferred_element_type=jnp.float32

time: 245 us -> 259 us (1.057)
  local copies, waits for them, and re-layouts: 32.8 us -> 45.4 us
  other arithmetic: 20.5 us -> 29.6 us
  matrix products: 28.7 us -> 22.6 us
  waiting for transfers between devices: 132 us -> 128 us
    sub x2 -> x0, matrix products: 10.3 us -> none  [on_device(): weights = jnp.where(allowed, jnp.exp(logits - best), 0.0)]
    reshape x2 -> x4, local copies, waits for them, and re-layouts: 3.8 us -> 9.72 us  [on_device(): (blended / total_weight[..., None]).transpose(2, 0, 1, 3)]
    broadcast_in_dim x2 -> x4, local copies, waits for them, and re-layouts: 1.46 us -> 7.06 us  [on_device(): handed.append(passed_along(result[None], 'phase', 1))]
    convert_element_type x2 -> x4, other arithmetic: 3.77 us -> 9.3 us  [on_device(): result = (hidden_part.astype(jnp.float32) + normed).astype(jnp.bfloat16)]
    dot_general x0 -> x4, matrix products: none -> 4.15 us  [on_device(): jnp.einsum('tgrd,kgd->grtk', queries, keys, preferred_element_type=jnp.fl...]
    reduce_sum x0 -> x4, other arithmetic: none -> 2.96 us  [on_device(): total_weight = jnp.sum(weights, axis=-1)]
    ppermute x2 -> x4, waiting for transfers between devices: 8.13 us -> 5.31 us  [passed_along(): return lax.ppermute(value, axis, pairs)]
    dot_general x2 -> x4, matrix products: 6.32 us -> 6.37 us  [on_device(): jnp.einsum('grtk,kgd->grtd', weights.astype(jnp.bfloat16), vals, preferre...]
  transfers between devices with their start and end apart: 4 -> 6, of which waited for: 3 -> 3; matrix products, arithmetic and copies ran while one was open for 12% -> 19% of each run, Pallas kernels for 0% -> 0%
where the time goes in v6:
time: 259 us; the launch traced here: 257 us
  waiting for transfers between devices  128 us (49%)
  local copies, waits for them, and re-layouts  45.4 us (18%)
  other arithmetic  29.6 us (11%)
  starting transfers between devices  28.2 us (11%)
  matrix products  22.6 us (9%)
  between operations  3.89 us (2%)
    all_to_all x1, waiting for transfers between devices, on_device(): got = lax.all_to_all(first, 'ctx', split_axis=0, concat_axis=0, tiled=True)  62.4 us
    all_to_all x1, waiting for transfers between devices, on_device(): lax.all_to_all(second, 'ctx', split_axis=0, concat_axis=0, tiled=True)  60 us
    all_to_all x1, starting transfers between devices, on_device(): got = lax.all_to_all(first, 'ctx', split_axis=0, concat_axis=0, tiled=True)  18.6 us
    reshape x4, local copies, waits for them, and re-layouts, on_device(): (blended / total_weight[..., None]).transpose(2, 0, 1, 3)  9.72 us
    convert_element_type x4, other arithmetic, on_device(): result = (hidden_part.astype(jnp.float32) + normed).astype(jnp.bfloat16)  9.3 us
    dot_general x1, matrix products, block_terms(): jnp.einsum('gktu,ugkp->tgkp', weights, scaled.reshape(length, GROUPS, wit...  8.37 us
    broadcast_in_dim x4, local copies, waits for them, and re-layouts, on_device(): handed.append(passed_along(result[None], 'phase', 1))  7.06 us
    dot_general x4, matrix products, on_device(): jnp.einsum('grtk,kgd->grtd', weights.astype(jnp.bfloat16), vals, preferre...  6.37 us
  transfers between devices with their start and end apart: 6, of which 3 were waited for; matrix products, arithmetic and copies ran while one was open for 19% of the time, Pallas kernels for 0%

profile of v6, /device:TPU:6, one launch (start us, length us, event | category | flops | bytes accessed | tf_op | source)
XLA Modules:
  0.0 257.4 jit_solution(4708311639923701399)
XLA Ops:
  0.0 1.4 dynamic_slice.15
  2.6 0.7 negate_bitcast_fusion
  3.3 0.8 copy.69
  4.1 0.7 fusion.116
  6.3 1.3 reduce.19
  7.7 0.8 compare_select_fusion.4
  8.6 0.8 slice.115
  10.1 0.7 broadcast_add_fusion.1
  11.5 1.3 broadcast_compare_fusion.1
  14.1 1.0 reshape_squeeze.11
  15.1 1.3 copy.71
  16.4 0.7 copy.68
  17.3 1.3 fusion.48
  18.6 1.4 maximum_maximum_fusion
  20.0 18.6 %all-to-all-start = ((bf16[64,80,128]{2,1,0:T(8,128)(2,1)}), bf16[64,80,128]{2,1,0:T(8,128)(2,1)S(1)}, u32[]{:S(2)}, u32[]{:S(2)}) async-start(bf16[64,80,128]{2,1,0:T(8,128)(2,1)} %maximum_maximum_fusion), calls=%async_computation | async-start | bytes 2621440 | tf_op jit(solution)/shard_map/all_to_all | solution.py:111
  39.0 0.8 scatter_custom_fusion
  39.8 1.9 gather_fusion.3
  42.6 62.4 %all-to-all-done = bf16[64,80,128]{2,1,0:T(8,128)(2,1)S(1)} async-done(((bf16[64,80,128]{2,1,0:T(8,128)(2,1)}), bf16[64,80,128]{2,1,0:T(8,128)(2,1)S(1)}, u32[]{:S(2)}, u32[]{:S(2)}) %all-to-all-start) | async-done | bytes 1310752 | tf_op jit(solution)/shard_map/all_to_all | solution.py:111
  105.0 0.7 fusion.120
  105.7 0.8 fusion.119
  106.5 0.8 gather_fusion
  109.0 1.6 gather_fusion.4
  110.6 1.2 copy.82
  112.0 1.4 convolution_convert_fusion
  113.6 2.2 copy.83
  115.8 6.2 %all-to-all-start.1 = ((bf16[64,96,128]{2,1,0:T(8,128)(2,1)}), bf16[64,96,128]{2,1,0:T(8,128)(2,1)}, u32[]{:S(2)}, u32[]{:S(2)}) async-start(bf16[64,96,128]{2,1,0:T(8,128)(2,1)} %copy.83), calls=%async_computation.1 | async-start | bytes 3145728 | tf_op jit(solution)/shard_map/all_to_all | solution.py:135
  124.4 0.8 copy.87
  125.3 3.9 %gather_fusion.5 = s32[640]{0:T(1024)S(1)} fusion(s32[8192]{0:T(1024)S(1)} %bitcast.282, s32[1024]{0:T(1024)S(1)} %pad_clamp_fusion), kind=kCustom, calls=%fused_computation.5 | custom fusion | bytes 7680 | tf_op jit(solution)/shard_map/jit(_take)/gather | solution.py:160
  129.4 0.7 and_and_fusion
  130.4 8.4 %fusion = f32[8,8,64,128]{3,2,1,0:T(8,128)S(1)} fusion(f32[8,128,128]{2,1,0:T(8,128)S(1)} %fusion.109, f32[8,8,128]{2,1,0:T(8,128)S(1)} %bitcast.309, pred[128,128]{1,0:T(8,128)(4,1)S(1)} %fusion.117, f32[128,8,8]{0,2,1:T(8,128)S(1)} %compare_select_fusion.4, bf16[128,8,8,64]{0,3,2,1:T(8,128)(2,1)S(1)} %bitcast.284), kind=kOutput, calls=%fused_computation.7 | convolution fusion | flops 810549248 | bytes 3751936 | tf_op jit(solution)/shard_map/gktu,ugkp->tgkp/dot_general | solution.py:45
  138.7 60.0 %all-to-all-done.1 = bf16[64,96,128]{2,1,0:T(8,128)(2,1)} async-done(((bf16[64,96,128]{2,1,0:T(8,128)(2,1)}), bf16[64,96,128]{2,1,0:T(8,128)(2,1)}, u32[]{:S(2)}, u32[]{:S(2)}) %all-to-all-start.1) | async-done | bytes 1572896 | tf_op jit(solution)/shard_map/all_to_all | solution.py:135
  198.7 1.1 slice.122
  200.0 1.3 slice.120
  201.3 0.7 multiply_reduce_fusion
  202.1 2.8 %fusion.31 = bf16[128,4096]{0,1:T(8,128)(2,1)S(1)} fusion(f32[8,8,64,128]{3,2,1,0:T(8,128)S(1)} %get-tuple-element.34, f32[8,8,64,128]{3,2,1,0:T(8,128)} %copy-done.2, f32[4096]{0:T(1024)S(1)} %bitcast.311, f32[128,8]{0,1:T(8,128)S(1)} %add_rsqrt_fusion, f32[4096]{0:T(1024)S(1)} %mul.254, f32[128,64]{0,1:T(8,128)S(1)} %copy.84, ...), kind=kLoop, calls=%fused_computation.52 | loop fusion | flops 5767168 | bytes 6361088 | tf_op jit(solution)/shard_map/convert_element_type | solution.py:151
  204.8 1.9 fusion.146
  206.8 0.7 fusion.42
  207.5 0.7 fusion.6
  208.3 1.7 multiply_reduce_fusion.4
  210.0 3.0 %copy.116 = f32[32,2,16,128]{0,3,2,1:T(8,128)} copy(f32[32,2,16,128]{3,0,2,1:T(8,128)} %get-tuple-element.38) | data formatting | bytes 1048576 | tf_op jit(solution)/shard_map/reshape | solution.py:189
  213.0 2.7 %fusion.28 = bf16[32,4096]{0,1:T(8,128)(2,1)} fusion(f32[32,2,16,128]{0,3,2,1:T(8,128)} %copy.116, f32[4096]{0:T(1024)S(1)} %bitcast.304, f32[32]{0:T(128)S(1)} %add_rsqrt_fusion.4, bf16[128,4096]{0,1:T(8,128)(2,1)S(1)} %fusion.31), kind=kLoop, calls=%fused_computation.48 | loop fusion | flops 655360 | bytes 1065088 | tf_op jit(solution)/shard_map/convert_element_type | solution.py:196
  215.7 2.2 copy.92
  218.0 2.0 fusion.43
  220.0 0.7 fusion.8
  220.7 1.7 multiply_reduce_fusion.3
  222.5 3.1 %copy.117 = f32[32,2,16,128]{0,3,2,1:T(8,128)} copy(f32[32,2,16,128]{3,0,2,1:T(8,128)} %get-tuple-element.42) | data formatting | bytes 1048576 | tf_op jit(solution)/shard_map/reshape | solution.py:189
  225.6 2.7 %fusion.25 = bf16[32,4096]{0,1:T(8,128)(2,1)} fusion(f32[32,2,16,128]{0,3,2,1:T(8,128)} %copy.117, bf16[32,4096]{0,1:T(8,128)(2,1)S(1)} %copy-done.1, f32[32]{0:T(128)S(1)} %add_rsqrt_fusion.3, f32[4096]{0:T(1024)S(1)} %bitcast.305), kind=kLoop, calls=%fused_computation.44 | loop fusion | flops 655360 | bytes 1065088 | tf_op jit(solution)/shard_map/convert_element_type | solution.py:196
  228.3 2.3 copy.96
  230.6 1.7 collective-permute-start.1
  232.2 0.7 fusion.44
  233.0 0.7 fusion.10
  233.7 1.3 multiply_reduce_fusion.2
  235.0 2.0 copy.118
  237.0 2.2 fusion.22
  239.2 1.0 copy.100
  240.2 0.7 fusion.45
  240.9 0.7 fusion.12
  241.7 1.7 multiply_reduce_fusion.1
  243.4 1.7 copy.119
  245.0 1.6 fusion.19
  246.7 1.5 copy.104
  248.2 1.7 collective-permute-start.3
  249.9 5.3 %collective-permute-done.3 = bf16[1,32,4096]{2,1,0:T(8,128)(2,1)S(1)} collective-permute-done((bf16[1,32,4096]{2,1,0:T(8,128)(2,1)S(1)}, bf16[1,32,4096]{2,1,0:T(8,128)(2,1)S(1)}, u32[]{:S(2)}, u32[]{:S(2)}) %collective-permute-start.3) | collective-permute-done | bytes 262176 | tf_op jit(solution)/shard_map/ppermute | solution.py:25
  255.3 2.1 pad_maximum_fusion.1
  (112 shorter events, 8.8 us)
Async XLA Ops:
  0.0 16.4 %copy-start.5 = (bf16[1,128,4096]{2,1,0:T(8,128)(2,1)S(1)}, bf16[1,128,4096]{2,1,0:T(8,128)(2,1)}, u32[]{:S(2)}) copy-start(bf16[1,128,4096]{2,1,0:T(8,128)(2,1)} %param.11) | copy-start | bytes 3145732
  16.4 113.7 %copy-start.3 = (bf16[1,128,2048]{1,2,0:T(8,128)(2,1)}, bf16[1,128,2048]{1,2,0:T(8,128)(2,1)S(1)}, u32[]{:S(2)}) copy-start(bf16[1,128,2048]{1,2,0:T(8,128)(2,1)S(1)} %copy.71) | copy-start | bytes 1572868
  18.6 20.0 %copy-start = (s32[1,8192]{1,0:T(1,128)S(1)}, s32[1,8192]{1,0:T(1,128)}, u32[]{:S(2)}) copy-start(s32[1,8192]{1,0:T(1,128)} %param.20) | copy-start | bytes 98308
  20.0 85.0 %all-to-all-start = ((bf16[64,80,128]{2,1,0:T(8,128)(2,1)}), bf16[64,80,128]{2,1,0:T(8,128)(2,1)S(1)}, u32[]{:S(2)}, u32[]{:S(2)}) async-start(bf16[64,80,128]{2,1,0:T(8,128)(2,1)} %maximum_maximum_fusion), calls=%async_computation | async-start | bytes 2621440 | tf_op jit(solution)/shard_map/all_to_all | solution.py:111
  39.8 2.1 copy-start.15
  39.8 2.1 copy-start.17
  113.5 9.6 %copy-start.7 = (bf16[1,128,512]{2,1,0:T(8,128)(2,1)S(1)}, bf16[1,128,512]{2,1,0:T(8,128)(2,1)}, u32[]{:S(2)}) copy-start(bf16[1,128,512]{2,1,0:T(8,128)(2,1)} %param.18) | copy-start | bytes 393220
  115.8 7.6 %copy-start.16 = (f32[1,64]{1,0:T(1,128)S(1)}, f32[1,64]{1,0:T(1,128)}, u32[]{:S(2)}) copy-start(f32[1,64]{1,0:T(1,128)} %param.16) | copy-start | bytes 772
  115.8 83.0 %all-to-all-start.1 = ((bf16[64,96,128]{2,1,0:T(8,128)(2,1)}), bf16[64,96,128]{2,1,0:T(8,128)(2,1)}, u32[]{:S(2)}, u32[]{:S(2)}) async-start(bf16[64,96,128]{2,1,0:T(8,128)(2,1)} %copy.83), calls=%async_computation.1 | async-start | bytes 3145728 | tf_op jit(solution)/shard_map/all_to_all | solution.py:135
  138.7 63.3 %copy-start.2 = (f32[8,8,64,128]{3,2,1,0:T(8,128)}, f32[8,8,64,128]{3,2,1,0:T(8,128)S(1)}, u32[]{:S(2)}) copy-start(f32[8,8,64,128]{3,2,1,0:T(8,128)S(1)} %fusion) | copy-start | bytes 6291460
  198.7 2.5 copy-start.4
  201.3 0.8 copy-start.14
  204.8 1.9 copy-start.6
  204.8 1.9 copy-start.13
  206.8 1.5 copy-start.8
  210.0 3.0 %copy-start.12 = (f32[1,4096]{1,0:T(1,128)S(1)}, f32[1,4096]{1,0:T(1,128)}, u32[]{:S(2)}) copy-start(f32[1,4096]{1,0:T(1,128)} %param.19) | copy-start | bytes 49156
  218.0 32.0 %collective-permute-start = (bf16[1,32,4096]{2,1,0:T(8,128)(2,1)}, bf16[1,32,4096]{2,1,0:T(8,128)(2,1)}, u32[]{:S(2)}, u32[]{:S(2)}) collective-permute-start(bf16[1,32,4096]{2,1,0:T(8,128)(2,1)} %copy.92), channel_id=1, source_target_pairs={{0,64},{64,128},{128,192},{192,256},{256,320},{320,384},{384,448},... | collective-permute-start | bytes 786440 | tf_op jit(solution)/shard_map/ppermute | solution.py:25
  218.0 2.8 %copy-start.9 = (bf16[640,2,128,1]{2,0,3,1:T(8,128)(2,1)S(1)}, bf16[640,2,128,1]{2,0,3,1:T(8,128)(2,1)}, u32[]{:S(2)}) copy-start(bf16[640,2,128,1]{2,0,3,1:T(8,128)(2,1)} %copy-done.8) | copy-start | bytes 983044
  222.5 3.1 %copy-start.1 = (bf16[32,4096]{0,1:T(8,128)(2,1)S(1)}, bf16[32,4096]{0,1:T(8,128)(2,1)}, u32[]{:S(2)}) copy-start(bf16[32,4096]{0,1:T(8,128)(2,1)} %get-tuple-element.8) | copy-start | bytes 786436
  230.6 19.4 %collective-permute-start.1 = (bf16[1,32,4096]{2,1,0:T(8,128)(2,1)}, bf16[1,32,4096]{2,1,0:T(8,128)(2,1)}, u32[]{:S(2)}, u32[]{:S(2)}) collective-permute-start(bf16[1,32,4096]{2,1,0:T(8,128)(2,1)} %copy.96), channel_id=1, source_target_pairs={{0,64},{64,128},{128,192},{192,256},{256,320},{320,384},{384,448},... | collective-permute-start | bytes 786440 | tf_op jit(solution)/shard_map/ppermute | solution.py:25
  232.2 1.5 copy-start.10
  240.2 9.8 %collective-permute-start.2 = (bf16[1,32,4096]{2,1,0:T(8,128)(2,1)}, bf16[1,32,4096]{2,1,0:T(8,128)(2,1)}, u32[]{:S(2)}, u32[]{:S(2)}) collective-permute-start(bf16[1,32,4096]{2,1,0:T(8,128)(2,1)} %copy.100), channel_id=1, source_target_pairs={{0,64},{64,128},{128,192},{192,256},{256,320},{320,384},{384,448},... | collective-permute-start | bytes 786440 | tf_op jit(solution)/shard_map/ppermute | solution.py:25
  240.2 1.5 copy-start.11
  248.2 7.0 %collective-permute-start.3 = (bf16[1,32,4096]{2,1,0:T(8,128)(2,1)S(1)}, bf16[1,32,4096]{2,1,0:T(8,128)(2,1)S(1)}, u32[]{:S(2)}, u32[]{:S(2)}) collective-permute-start(bf16[1,32,4096]{2,1,0:T(8,128)(2,1)S(1)} %copy.104), channel_id=1, source_target_pairs={{0,64},{64,128},{128,192},{192,256},{256,320},{320,384},{384,448},... | collective-permute-start | bytes 786440 | tf_op jit(solution)/shard_map/ppermute | solution.py:25

commit v7 on v6

--- a/solution.py
+++ b/solution.py
@@ -109,7 +109,6 @@
     padding = jnp.zeros((devices, -used % 8, lanes), jnp.bfloat16)
     first = jnp.concatenate([state_slots, kv_slices, raw_cols, padding], axis=1)
     got = lax.all_to_all(first, "ctx", split_axis=0, concat_axis=0, tiled=True)
-    got_states = got[:, :HEAD_DIM].astype(jnp.float32)
     got_kv = got[:, HEAD_DIM : HEAD_DIM + kv_rows]
     got_raw = got[:, HEAD_DIM + kv_rows].astype(jnp.float32)
 
@@ -126,7 +125,13 @@
         linked, jnp.exp(jnp.minimum(before[:, None] - running[None, :], 0.0)), 0.0
     )
     by_device = factors[placement_perm][:, placement_perm]
-    entering = jnp.einsum("ds,spn->dpn", by_device, got_states, precision=precise)
+    flat_states = got[:, :HEAD_DIM].reshape(devices, HEAD_DIM * STATE)
+    high = by_device.astype(jnp.bfloat16)
+    low = (by_device - high.astype(jnp.float32)).astype(jnp.bfloat16)
+    entering = jnp.dot(high, flat_states, preferred_element_type=jnp.float32) + jnp.dot(
+        low, flat_states, preferred_element_type=jnp.float32
+    )
+    entering = entering.reshape(devices, HEAD_DIM, STATE)
 
     halo_blocks = placement_perm[:, None] - HALO + jnp.arange(HALO)[None, :]
     halo_src = inverse[jnp.clip(halo_blocks, 0, devices - 1)]
@@ -159,7 +164,7 @@
     )
     key_seg = jnp.take(segment, jnp.maximum(key_pos, 0))
     score_scale = 1.0 / math.sqrt(QDIM)
-    pieces = 4
+    pieces = 2
     rows = tok_rows // pieces
     handed = []
     for piece in range(pieces):

time: 259 us -> 240 us (0.927)
  local copies, waits for them, and re-layouts: 45.4 us -> 31.4 us
  waiting for transfers between devices: 128 us -> 132 us
  matrix products: 22.6 us -> 19 us
  other arithmetic: 29.6 us -> 26.2 us
    reshape x4 -> x2, local copies, waits for them, and re-layouts: 9.72 us -> 3.8 us  [on_device(): (blended / total_weight[..., None]).transpose(2, 0, 1, 3)]
    convert_element_type x4 -> x2, other arithmetic: 9.3 us -> 4.42 us  [on_device(): result = (hidden_part.astype(jnp.float32) + normed).astype(jnp.bfloat16)]
    broadcast_in_dim x4 -> x2, local copies, waits for them, and re-layouts: 7.06 us -> 3.88 us  [on_device(): handed.append(passed_along(result[None], 'phase', 1))]
    ppermute x4 -> x2, waiting for transfers between devices: 5.31 us -> 8.13 us  [passed_along(): return lax.ppermute(value, axis, pairs)]
    dot_general x4 -> x2, matrix products: 6.37 us -> 4.08 us  [on_device(): jnp.einsum('grtk,kgd->grtd', weights.astype(jnp.bfloat16), vals, preferre...]
  transfers between devices with their start and end apart: 6 -> 4, of which waited for: 3 -> 3; matrix products, arithmetic and copies ran while one was open for 19% -> 12% of each run, Pallas kernels for 0% -> 0%
where the time goes in v7:
time: 240 us; the launch traced here: 239 us
  waiting for transfers between devices  132 us (55%)
  local copies, waits for them, and re-layouts  31.4 us (13%)
  starting transfers between devices  26.5 us (11%)
  other arithmetic  26.2 us (11%)
  matrix products  19 us (8%)
  between operations  3.81 us (2%)
    all_to_all x1, waiting for transfers between devices, on_device(): got = lax.all_to_all(first, 'ctx', split_axis=0, concat_axis=0, tiled=True)  62.4 us
    all_to_all x1, waiting for transfers between devices, on_device(): lax.all_to_all(second, 'ctx', split_axis=0, concat_axis=0, tiled=True)  61.2 us
    all_to_all x1, starting transfers between devices, on_device(): got = lax.all_to_all(first, 'ctx', split_axis=0, concat_axis=0, tiled=True)  18.6 us
    dot_general x1, matrix products, block_terms(): jnp.einsum('gktu,ugkp->tgkp', weights, scaled.reshape(length, GROUPS, wit...  8.36 us
    ppermute x2, waiting for transfers between devices, passed_along(): return lax.ppermute(value, axis, pairs)  8.13 us
    all_to_all x1, starting transfers between devices, on_device(): lax.all_to_all(second, 'ctx', split_axis=0, concat_axis=0, tiled=True)  6.24 us
    unnamed x34, local copies, waits for them, and re-layouts  4.91 us
  transfers between devices with their start and end apart: 4, of which 3 were waited for; matrix products, arithmetic and copies ran while one was open for 12% of the time, Pallas kernels for 0%

profile of v7, /device:TPU:6, one launch (start us, length us, event | category | flops | bytes accessed | tf_op | source)
XLA Modules:
  0.0 238.7 jit_solution(4501093117634698259)
XLA Ops:
  0.0 1.4 dynamic_slice.15
  2.6 0.7 negate_bitcast_fusion
  3.3 0.8 copy.51
  4.1 0.7 fusion.80
  4.8 0.2 reduce_window_sum.27
  5.7 0.5 broadcast.408
  6.3 1.3 reduce.17
  7.7 0.8 compare_select_fusion.4
  8.6 0.8 slice.97
  10.1 0.7 broadcast_add_fusion.1
  10.9 0.6 dynamic_slice.19
  11.5 1.3 broadcast_compare_fusion.1
  12.8 0.6 slice.68
  13.3 0.6 broadcast_compare_fusion.2
  14.1 1.0 reshape_squeeze.11
  15.1 1.3 copy.53
  16.4 0.7 copy.50
  17.3 1.3 fusion.43
  18.6 1.4 maximum_maximum_fusion
  20.0 18.6 %all-to-all-start = ((bf16[64,80,128]{2,1,0:T(8,128)(2,1)}), bf16[64,80,128]{2,1,0:T(8,128)(2,1)S(1)}, u32[]{:S(2)}, u32[]{:S(2)}) async-start(bf16[64,80,128]{2,1,0:T(8,128)(2,1)} %maximum_maximum_fusion), calls=%async_computation | async-start | bytes 2621440 | tf_op jit(solution)/shard_map/all_to_all | solution.py:111
  38.9 0.8 scatter_custom_fusion
  39.8 1.9 gather_fusion.3
  41.9 0.7 constant_dynamic-slice_fusion
  42.6 62.4 %all-to-all-done = bf16[64,80,128]{2,1,0:T(8,128)(2,1)S(1)} async-done(((bf16[64,80,128]{2,1,0:T(8,128)(2,1)}), bf16[64,80,128]{2,1,0:T(8,128)(2,1)S(1)}, u32[]{:S(2)}, u32[]{:S(2)}) %all-to-all-start) | async-done | bytes 1310752 | tf_op jit(solution)/shard_map/all_to_all | solution.py:111
  105.0 0.7 fusion.86
  105.7 0.8 fusion.85
  106.5 0.8 gather_fusion
  107.7 0.6 gather_fusion.1
  108.4 0.6 gather_fusion.2
  109.1 0.9 fusion.54
  110.0 1.0 fusion.52
  110.9 1.3 copy.91
  112.2 0.8 gather_fusion.4
  113.0 2.5 %pad_maximum_fusion = bf16[64,96,128]{2,1,0:T(8,128)(2,1)} fusion(bf16[64,32,128]{2,1,0:T(8,128)(2,1)S(1)} %bitcast.262, bf16[64,64,128]{2,1,0:T(8,128)(2,1)} %bitcast.256), kind=kLoop, calls=%fused_computation.60 | loop fusion | flops 3145728 | bytes 3145728 | tf_op jit(solution)/shard_map/concatenate | solution.py:139
  115.6 6.2 %all-to-all-start.1 = ((bf16[64,96,128]{2,1,0:T(8,128)(2,1)}), bf16[64,96,128]{2,1,0:T(8,128)(2,1)}, u32[]{:S(2)}, u32[]{:S(2)}) async-start(bf16[64,96,128]{2,1,0:T(8,128)(2,1)} %pad_maximum_fusion), calls=%async_computation.1 | async-start | bytes 3145728 | tf_op jit(solution)/shard_map/all_to_all | solution.py:140
  122.7 0.2 add.296
  122.8 0.2 concatenate.50
  123.1 0.6 reduce.18
  124.2 0.2 copy.65
  124.5 3.9 %gather_fusion.5 = s32[640]{0:T(1024)S(1)} fusion(s32[8192]{0:T(1024)S(1)} %bitcast.245, s32[1024]{0:T(1024)S(1)} %pad_clamp_fusion), kind=kCustom, calls=%fused_computation.5 | custom fusion | bytes 7680 | tf_op jit(solution)/shard_map/jit(_take)/gather | solution.py:165
  128.5 0.1 and_and_fusion
  128.7 0.3 fusion.73
  129.0 8.4 %fusion.5 = f32[8,8,64,128]{3,2,1,0:T(8,128)S(1)} fusion(f32[8,128,128]{2,1,0:T(8,128)S(1)} %fusion.73, f32[8,8,128]{2,1,0:T(8,128)S(1)} %bitcast.269, pred[128,128]{1,0:T(8,128)(4,1)S(1)} %fusion.81, f32[128,8,8]{0,2,1:T(8,128)S(1)} %compare_select_fusion.4, bf16[128,8,8,64]{0,3,2,1:T(8,128)(2,1)S(1)} %bitcast.247), kind=kOutput, calls=%fused_computation.17 | convolution fusion | flops 810549248 | bytes 3751936 | tf_op jit(solution)/shard_map/gktu,ugkp->tgkp/dot_general | solution.py:45
  137.4 61.2 %all-to-all-done.1 = bf16[64,96,128]{2,1,0:T(8,128)(2,1)} async-done(((bf16[64,96,128]{2,1,0:T(8,128)(2,1)}), bf16[64,96,128]{2,1,0:T(8,128)(2,1)}, u32[]{:S(2)}, u32[]{:S(2)}) %all-to-all-start.1) | async-done | bytes 1572896 | tf_op jit(solution)/shard_map/all_to_all | solution.py:140
  198.5 1.1 slice.104
  199.8 1.5 slice.102
  201.3 0.7 multiply_reduce_fusion
  202.1 2.5 %fusion.30 = bf16[128,4096]{0,1:T(8,128)(2,1)S(1)} fusion(f32[8,8,64,128]{3,2,1,0:T(8,128)S(1)} %get-tuple-element.22, f32[8,8,64,128]{3,2,1,0:T(8,128)} %copy-done.1, f32[4096]{0:T(1024)S(1)} %bitcast.270, f32[128,8]{0,1:T(8,128)S(1)} %add_rsqrt_fusion, f32[4096]{0:T(1024)S(1)} %mul.204, f32[128,64]{0,1:T(8,128)S(1)} %copy.62, ...), kind=kLoop, calls=%fused_computation.44 | loop fusion | flops 5767168 | bytes 6361088 | tf_op jit(solution)/shard_map/convert_element_type | solution.py:156
  204.6 0.4 fusion.116
  205.0 1.2 fusion.11
  206.2 1.6 fusion.1
  207.9 1.6 multiply_reduce_fusion.2
  209.5 2.0 copy.82
  211.4 2.8 %fusion.27 = bf16[64,4096]{0,1:T(8,128)(2,1)} fusion(f32[64,2,16,128]{0,3,2,1:T(8,128)} %copy.82, f32[4096]{0:T(1024)S(1)} %bitcast.267, f32[64]{0:T(128)S(1)} %add_rsqrt_fusion.2, bf16[128,4096]{0,1:T(8,128)(2,1)S(1)} %fusion.30), kind=kLoop, calls=%fused_computation.40 | loop fusion | flops 1310720 | bytes 2113792 | tf_op jit(solution)/shard_map/convert_element_type | solution.py:201
  214.2 2.3 copy.70
  216.5 1.2 fusion.12
  217.8 1.4 fusion.3
  219.2 2.5 %multiply_reduce_fusion.1 = (f32[64]{0:T(128)S(1)}, f32[64,2,16,128]{3,0,2,1:T(8,128)}) fusion(f32[64,2,16]{0,2,1:T(8,128)S(1)} %bitcast.271, bf16[128,2,2,128]{3,0,2,1:T(8,128)(2,1)S(1)} %copy.65, bf16[512,2,2,128]{3,0,2,1:T(8,128)(2,1)S(1)} %copy-done.3, f32[2,640,64,16]{1,2,3,0:T(8,128)S(1)} %get-tuple-element.28, ...), kind=kOutput, calls=%fused_computation.70 | convolution fusion | flops 342228928 | bytes 7004416 | tf_op jit(solution)/shard_map/grtk,kgd->grtd/dot_general | solution.py:190
  221.7 1.8 copy.83
  223.6 1.6 fusion.24
  225.2 1.5 copy.74
  226.8 1.7 collective-permute-start.1
  228.5 8.1 %collective-permute-done.1 = bf16[1,64,4096]{2,1,0:T(8,128)(2,1)S(1)} collective-permute-done((bf16[1,64,4096]{2,1,0:T(8,128)(2,1)S(1)}, bf16[1,64,4096]{2,1,0:T(8,128)(2,1)S(1)}, u32[]{:S(2)}, u32[]{:S(2)}) %collective-permute-start.1) | collective-permute-done | bytes 524320 | tf_op jit(solution)/shard_map/ppermute | solution.py:25
  236.6 2.1 pad_maximum_fusion.1
  (82 shorter events, 2.9 us)
Async XLA Ops:
  0.0 16.4 %copy-start.6 = (bf16[1,128,4096]{2,1,0:T(8,128)(2,1)S(1)}, bf16[1,128,4096]{2,1,0:T(8,128)(2,1)}, u32[]{:S(2)}) copy-start(bf16[1,128,4096]{2,1,0:T(8,128)(2,1)} %param.11) | copy-start | bytes 3145732
  16.4 112.3 %copy-start.4 = (bf16[1,128,2048]{1,2,0:T(8,128)(2,1)}, bf16[1,128,2048]{1,2,0:T(8,128)(2,1)S(1)}, u32[]{:S(2)}) copy-start(bf16[1,128,2048]{1,2,0:T(8,128)(2,1)S(1)} %copy.53) | copy-start | bytes 1572868
  18.5 20.0 %copy-start = (s32[1,8192]{1,0:T(1,128)S(1)}, s32[1,8192]{1,0:T(1,128)}, u32[]{:S(2)}) copy-start(s32[1,8192]{1,0:T(1,128)} %param.20) | copy-start | bytes 98308
  20.0 85.0 %all-to-all-start = ((bf16[64,80,128]{2,1,0:T(8,128)(2,1)}), bf16[64,80,128]{2,1,0:T(8,128)(2,1)S(1)}, u32[]{:S(2)}, u32[]{:S(2)}) async-start(bf16[64,80,128]{2,1,0:T(8,128)(2,1)} %maximum_maximum_fusion), calls=%async_computation | async-start | bytes 2621440 | tf_op jit(solution)/shard_map/all_to_all | solution.py:111
  39.7 2.1 copy-start.10
  39.7 2.1 copy-start.12
  115.6 7.4 %copy-start.7 = (bf16[1,128,512]{2,1,0:T(8,128)(2,1)S(1)}, bf16[1,128,512]{2,1,0:T(8,128)(2,1)}, u32[]{:S(2)}) copy-start(bf16[1,128,512]{2,1,0:T(8,128)(2,1)} %param.18) | copy-start | bytes 393220
  115.6 7.6 %copy-start.11 = (f32[1,64]{1,0:T(1,128)S(1)}, f32[1,64]{1,0:T(1,128)}, u32[]{:S(2)}) copy-start(f32[1,64]{1,0:T(1,128)} %param.16) | copy-start | bytes 772
  115.6 83.0 %all-to-all-start.1 = ((bf16[64,96,128]{2,1,0:T(8,128)(2,1)}), bf16[64,96,128]{2,1,0:T(8,128)(2,1)}, u32[]{:S(2)}, u32[]{:S(2)}) async-start(bf16[64,96,128]{2,1,0:T(8,128)(2,1)} %pad_maximum_fusion), calls=%async_computation.1 | async-start | bytes 3145728 | tf_op jit(solution)/shard_map/all_to_all | solution.py:140
  137.3 63.9 %copy-start.1 = (f32[8,8,64,128]{3,2,1,0:T(8,128)}, f32[8,8,64,128]{3,2,1,0:T(8,128)S(1)}, u32[]{:S(2)}) copy-start(f32[8,8,64,128]{3,2,1,0:T(8,128)S(1)} %fusion.5) | copy-start | bytes 6291460
  198.5 2.7 %copy-start.5 = (bf16[1,128,2048]{1,2,0:T(8,128)(2,1)S(1)}, bf16[1,128,2048]{1,2,0:T(8,128)(2,1)}, u32[]{:S(2)}) copy-start(bf16[1,128,2048]{1,2,0:T(8,128)(2,1)} %copy-done.4) | copy-start | bytes 1572868
  199.8 8.1 %copy-start.2 = (bf16[512,2,2,128]{3,0,2,1:T(8,128)(2,1)}, bf16[512,2,2,128]{3,0,2,1:T(8,128)(2,1)S(1)}, u32[]{:S(2)}) copy-start(bf16[512,2,2,128]{3,0,2,1:T(8,128)(2,1)S(1)} %copy.64) | copy-start | bytes 1572868
  201.3 0.8 copy-start.9
  209.4 2.0 copy-start.8
  211.4 5.1 %copy-start.3 = (bf16[512,2,2,128]{3,0,2,1:T(8,128)(2,1)S(1)}, bf16[512,2,2,128]{3,0,2,1:T(8,128)(2,1)}, u32[]{:S(2)}) copy-start(bf16[512,2,2,128]{3,0,2,1:T(8,128)(2,1)} %copy-done.2) | copy-start | bytes 1572868
  216.5 11.9 %collective-permute-start = (bf16[1,64,4096]{2,1,0:T(8,128)(2,1)}, bf16[1,64,4096]{2,1,0:T(8,128)(2,1)}, u32[]{:S(2)}, u32[]{:S(2)}) collective-permute-start(bf16[1,64,4096]{2,1,0:T(8,128)(2,1)} %copy.70), channel_id=1, source_target_pairs={{0,64},{64,128},{128,192},{192,256},{256,320},{320,384},{384,448},... | collective-permute-start | bytes 1572872 | tf_op jit(solution)/shard_map/ppermute | solution.py:25
  226.8 9.8 %collective-permute-start.1 = (bf16[1,64,4096]{2,1,0:T(8,128)(2,1)S(1)}, bf16[1,64,4096]{2,1,0:T(8,128)(2,1)S(1)}, u32[]{:S(2)}, u32[]{:S(2)}) collective-permute-start(bf16[1,64,4096]{2,1,0:T(8,128)(2,1)S(1)} %copy.74), channel_id=1, source_target_pairs={{0,64},{64,128},{128,192},{192,256},{256,320},{320,384},{384,448},... | collective-permute-start | bytes 1572872 | tf_op jit(solution)/shard_map/ppermute | solution.py:25

commit v8 on v7

--- a/solution.py
+++ b/solution.py
@@ -3,6 +3,8 @@
 import jax
 import jax.numpy as jnp
 from jax import lax
+from jax.experimental import pallas as pl
+from jax.experimental.pallas import tpu as pltpu
 from jax.sharding import PartitionSpec as P
 
 HEADS = 64
@@ -57,6 +59,64 @@
     return local_out, states, cum_log, ending
 
 
+def states_kernel(xt_ref, bc_ref, raw_ref, bias_ref, rate_ref, seg_ref, tail_ref, out_ref, cum_ref):
+    length = raw_ref.shape[1]
+    within = HEADS // GROUPS
+    shifted = raw_ref[...].astype(jnp.float32) + bias_ref[...]
+    steps = jnp.maximum(shifted, 0.0) + jnp.log1p(jnp.exp(-jnp.abs(shifted)))
+    cum = -rate_ref[...] * steps
+    lane = lax.broadcasted_iota(jnp.int32, cum.shape, 1)
+    reach = 1
+    while reach < length:
+        cum = cum + jnp.where(lane >= reach, pltpu.roll(cum, reach, 1), 0.0)
+        reach *= 2
+    cum_ref[...] = cum
+    ending = cum[:, length - 1 : length]
+    seg = seg_ref[...]
+    same = seg == seg[:, length - 1 : length]
+    weights = jnp.where(same, jnp.exp(ending - cum), 0.0) * steps
+    for group in range(GROUPS):
+        w = weights[group * within : (group + 1) * within]
+        w = jnp.broadcast_to(w[:, None, :], (within, HEAD_DIM, length)).reshape(within * HEAD_DIM, length)
+        rows = slice(group * within * HEAD_DIM, (group + 1) * within * HEAD_DIM)
+        scaled = xt_ref[rows, :].astype(jnp.float32) * w
+        high = scaled.astype(jnp.bfloat16)
+        low = (scaled - high.astype(jnp.float32)).astype(jnp.bfloat16)
+        inject = bc_ref[:, group * 2 * STATE : group * 2 * STATE + STATE]
+        state = jnp.dot(high, inject, preferred_element_type=jnp.float32) + jnp.dot(
+            low, inject, preferred_element_type=jnp.float32
+        )
+        out_ref[group * within : (group + 1) * within, :HEAD_DIM, :] = (
+            state.astype(out_ref.dtype).reshape(within, HEAD_DIM, STATE)
+        )
+    out_ref[:, HEAD_DIM:, :] = tail_ref[...]
+
+
+def block_states(inputs, projections, raw, bias, rate, seg, tail):
+    tokens = inputs.shape[0]
+    rows = HEAD_DIM + tail.shape[1]
+    return pl.pallas_call(
+        states_kernel,
+        out_shape=(
+            jax.ShapeDtypeStruct((HEADS, rows, STATE), jnp.bfloat16),
+            jax.ShapeDtypeStruct((HEADS, tokens), jnp.float32),
+        ),
+        cost_estimate=pl.CostEstimate(
+            flops=4 * HEADS * HEAD_DIM * STATE * tokens,
+            transcendentals=3 * HEADS * tokens,
+            bytes_accessed=inputs.size * 2 + projections.size * 2 + HEADS * rows * STATE * 2,
+        ),
+    )(
+        inputs.T,
+        projections,
+        raw.T,
+        bias.reshape(HEADS, 1),
+        rate.reshape(HEADS, 1),
+        seg.reshape(1, tokens),
+        tail,
+    )
+
+
 def on_device(
     mixer_input,
     state_proj,
@@ -104,10 +164,13 @@
     kv_rows = share * kv_cols // lanes
     kv_slices = kv.reshape(devices, kv_rows, lanes)
     raw_cols = dt_raw[0].T.reshape(HEADS, 1, tok_rows)
-    state_slots = states.astype(jnp.bfloat16)
-    used = HEAD_DIM + kv_rows + 1
+    used = kv_rows + 1
     padding = jnp.zeros((devices, -used % 8, lanes), jnp.bfloat16)
-    first = jnp.concatenate([state_slots, kv_slices, raw_cols, padding], axis=1)
+    tail = jnp.concatenate([kv_slices, raw_cols, padding], axis=1)
+    first, cum_t = block_states(
+        inputs, state_proj[0], dt_raw[0], dt_bias[0], decay_rate[0], my_seg, tail
+    )
+    cum_log = cum_t.T
     got = lax.all_to_all(first, "ctx", split_axis=0, concat_axis=0, tiled=True)
     got_kv = got[:, HEAD_DIM : HEAD_DIM + kv_rows]
     got_raw = got[:, HEAD_DIM + kv_rows].astype(jnp.float32)

time: 240 us -> 238 us (level)
  other arithmetic: 26.2 us -> 18.9 us
  waiting for transfers between devices: 132 us -> 127 us
  local copies, waits for them, and re-layouts: 31.4 us -> 35.7 us
  Pallas kernels: 0 us -> 4.29 us
    div x0 -> x2, local copies, waits for them, and re-layouts: none -> 5.03 us  [on_device(): blended / total_weight[..., None]]
    all_to_all x1, waiting for transfers between devices: 61.2 us -> 56.8 us  [on_device(): lax.all_to_all(second, 'ctx', split_axis=0, concat_axis=0, tiled=True)]
    pallas_call x0 -> x1, Pallas kernels: none -> 4.29 us  [block_states(): pl.pallas_call(states_kernel, out_shape=(jax.ShapeDtypeStruct((HEADS, row...]
    reshape x2 -> x0, local copies, waits for them, and re-layouts: 3.8 us -> none  [on_device(): (blended / total_weight[..., None]).transpose(2, 0, 1, 3)]
    another operation x2 -> x3, local copies, waits for them, and re-layouts: 0.16 us -> 2.79 us  [the longest x1 1.35 us: block_states(): rate.reshape(HEADS, 1)]
    unnamed x34 -> x39, local copies, waits for them, and re-layouts: 4.91 us -> 4.91 us
  transfers between devices with their start and end apart: 4 -> 4, of which waited for: 3 -> 3; matrix products, arithmetic and copies ran while one was open for 12% -> 14% of each run, Pallas kernels for 0% -> 0%
where the time goes in v8:
time: 238 us; the launch traced here: 237 us
  waiting for transfers between devices  127 us (53%)
  local copies, waits for them, and re-layouts  35.7 us (15%)
  starting transfers between devices  26.5 us (11%)
  matrix products  20.1 us (8%)
  other arithmetic  18.9 us (8%)
  Pallas kernels  4.29 us (2%)
  between operations  3.7 us (2%)
    all_to_all x1, waiting for transfers between devices, on_device(): got = lax.all_to_all(first, 'ctx', split_axis=0, concat_axis=0, tiled=True)  62.4 us
    all_to_all x1, waiting for transfers between devices, on_device(): lax.all_to_all(second, 'ctx', split_axis=0, concat_axis=0, tiled=True)  56.8 us
    all_to_all x1, starting transfers between devices, on_device(): got = lax.all_to_all(first, 'ctx', split_axis=0, concat_axis=0, tiled=True)  18.6 us
    dot_general x1, matrix products, block_terms(): jnp.einsum('gktu,ugkp->tgkp', weights, scaled.reshape(length, GROUPS, wit...  9.59 us
    ppermute x2, waiting for transfers between devices, passed_along(): return lax.ppermute(value, axis, pairs)  8.14 us
    all_to_all x1, starting transfers between devices, on_device(): lax.all_to_all(second, 'ctx', split_axis=0, concat_axis=0, tiled=True)  6.24 us
    dot_general x2, matrix products, on_device(): jnp.einsum('grtk,kgd->grtd', weights.astype(jnp.bfloat16), vals, preferre...  5.26 us
    div x2, local copies, waits for them, and re-layouts, on_device(): blended / total_weight[..., None]  5.03 us
  transfers between devices with their start and end apart: 4, of which 3 were waited for; matrix products, arithmetic and copies ran while one was open for 14% of the time, Pallas kernels for 0%

profile of v8, /device:TPU:6, one launch (start us, length us, event | category | flops | bytes accessed | tf_op | source)
XLA Modules:
  0.0 236.6 jit_solution(13439493248120726117)
XLA Ops:
  0.0 1.3 dynamic_slice.15
  3.2 1.3 copy.63.bias_ref
  4.5 0.7 copy.62
  5.3 1.3 copy.64.rate_ref
  6.6 0.8 slice.88
  7.5 1.0 reshape_squeeze.19
  8.5 2.3 copy.53
  11.6 0.7 dynamic_slice.19
  12.3 1.3 broadcast_compare_fusion.1
  13.5 0.8 maximum_maximum_fusion.tail_ref
  14.4 4.3 %shard_map.109 = (bf16[64,80,128]{2,1,0:T(8,128)(2,1)}, f32[64,128]{1,0:T(8,128)}) custom-call(bf16[4096,128]{1,0:T(8,128)(2,1)} %bitcast.246, bf16[128,2048]{1,0:T(8,128)(2,1)} %bitcast.257, bf16[64,128]{1,0:T(8,128)(2,1)} %bitcast.261, f32[64,1]{1,0:T(8,128)} %copy.63.bias_ref, f32[64,1]{1,0:T(8,128)} %copy.64.rate_ref, ...), custom_call_target="tpu_custom_call" | custom-call | flops 268435456 | bytes 2883584 | tf_op jit(solution)/shard_map/pallas_call | solution.py:98
  18.7 18.6 %all-to-all-start = ((bf16[64,80,128]{2,1,0:T(8,128)(2,1)}), bf16[64,80,128]{2,1,0:T(8,128)(2,1)S(1)}, u32[]{:S(2)}, u32[]{:S(2)}) async-start(bf16[64,80,128]{2,1,0:T(8,128)(2,1)} %get-tuple-element.8), calls=%async_computation | async-start | bytes 2621440 | tf_op jit(solution)/shard_map/all_to_all | solution.py:174
  37.6 0.8 scatter_custom_fusion
  38.4 1.9 gather_fusion.3
  40.6 0.7 constant_dynamic-slice_fusion
  41.3 62.4 %all-to-all-done = bf16[64,80,128]{2,1,0:T(8,128)(2,1)S(1)} async-done(((bf16[64,80,128]{2,1,0:T(8,128)(2,1)}), bf16[64,80,128]{2,1,0:T(8,128)(2,1)S(1)}, u32[]{:S(2)}, u32[]{:S(2)}) %all-to-all-start) | async-done | bytes 1310752 | tf_op jit(solution)/shard_map/all_to_all | solution.py:174
  103.7 1.4 fusion.72
  105.1 0.8 gather_fusion
  106.3 0.6 gather_fusion.1
  107.0 0.6 gather_fusion.2
  107.6 0.1 slice.90
  107.7 0.9 fusion.47
  108.6 1.0 fusion.45
  109.6 0.3 copy.88
  109.9 0.8 gather_fusion.4
  110.7 1.3 pad_maximum_fusion
  112.0 6.2 %all-to-all-start.1 = ((bf16[64,96,128]{2,1,0:T(8,128)(2,1)}), bf16[64,96,128]{2,1,0:T(8,128)(2,1)}, u32[]{:S(2)}, u32[]{:S(2)}) async-start(bf16[64,96,128]{2,1,0:T(8,128)(2,1)} %pad_maximum_fusion), calls=%async_computation.1 | async-start | bytes 3145728 | tf_op jit(solution)/shard_map/all_to_all | solution.py:203
  119.0 0.1 iota_add_fusion
  119.1 0.2 add.296
  119.3 0.2 concatenate.50
  119.4 0.1 copy.68
  119.6 1.0 copy.57
  120.6 0.5 copy.54
  121.1 0.5 broadcast.359
  121.6 0.7 reduce.13
  122.3 0.7 reduce.14
  123.3 0.2 reduce_window_sum.25
  123.7 0.1 copy.70
  123.9 3.9 %gather_fusion.5 = s32[640]{0:T(1024)S(1)} fusion(s32[8192]{0:T(1024)S(1)} %bitcast.242, s32[1024]{0:T(1024)S(1)} %pad_clamp_fusion), kind=kCustom, calls=%fused_computation.5 | custom fusion | bytes 7680 | tf_op jit(solution)/shard_map/jit(_take)/gather | solution.py:228
  128.2 0.1 and_and_fusion
  128.3 0.3 fusion.61
  128.6 9.6 %fusion.5 = f32[8,8,64,128]{3,2,1,0:T(8,128)} fusion(f32[8,128,128]{2,1,0:T(8,128)S(1)} %fusion.61, f32[8,8,128]{2,1,0:T(8,128)S(1)} %bitcast.265, f32[128,8,8,64]{0,3,2,1:T(8,128)S(1)} %bitcast.247, pred[128,128]{1,0:T(8,128)(4,1)S(1)} %fusion.67, f32[128,8,8]{0,2,1:T(8,128)S(1)} %compare_select_fusion.4), kind=kOutput, calls=%fused_computation.17 | convolution fusion | flops 810024960 | bytes 4800512 | tf_op jit(solution)/shard_map/gktu,ugkp->tgkp/dot_general | solution.py:47
  138.2 56.8 %all-to-all-done.1 = bf16[64,96,128]{2,1,0:T(8,128)(2,1)} async-done(((bf16[64,96,128]{2,1,0:T(8,128)(2,1)}), bf16[64,96,128]{2,1,0:T(8,128)(2,1)}, u32[]{:S(2)}, u32[]{:S(2)}) %all-to-all-start.1) | async-done | bytes 1572896 | tf_op jit(solution)/shard_map/all_to_all | solution.py:203
  195.0 1.2 slice.94
  196.3 1.3 slice.92
  197.6 0.7 multiply_reduce_fusion
  198.3 0.5 copy-done.1
  198.8 1.6 fusion.21
  200.4 0.4 fusion.105
  200.8 1.2 fusion.11
  202.1 1.4 fusion.1
  203.5 2.7 %multiply_reduce_fusion.2 = (f32[64]{0:T(128)S(1)}, f32[64,2,16,128]{3,0,2,1:T(8,128)}) fusion(f32[64,2,16]{0,2,1:T(8,128)S(1)} %bitcast.269, bf16[128,2,2,128]{3,0,2,1:T(8,128)(2,1)S(1)} %copy.70, bf16[512,2,2,128]{3,0,2,1:T(8,128)(2,1)S(1)} %copy.69, f32[2,640,64,16]{1,2,3,0:T(8,128)S(1)} %get-tuple-element.28, f32[2,16,64]{2,1,0:T(8,128)S(1)} %get-tuple-element.27, ...), kind=kOutput, calls=%fused_computation.66 | convolution fusion | flops 342228928 | bytes 7004416 | tf_op jit(solution)/shard_map/grtk,kgd->grtd/dot_general | solution.py:253
  206.2 3.2 %copy.72 = f32[64,2,16,128]{0,3,2,1:T(8,128)} copy(f32[64,2,16,128]{3,0,2,1:T(8,128)} %get-tuple-element.30) | data formatting | bytes 2097152 | tf_op jit(solution)/shard_map/div | solution.py:257
  209.4 2.7 %fusion.28 = bf16[64,4096]{0,1:T(8,128)(2,1)} fusion(f32[64,2,16,128]{0,3,2,1:T(8,128)} %copy.72, f32[4096]{0:T(1024)S(1)} %bitcast.263, f32[64]{0:T(128)S(1)} %add_rsqrt_fusion.2, bf16[128,4096]{0,1:T(8,128)(2,1)S(1)} %fusion.21), kind=kLoop, calls=%fused_computation.43 | loop fusion | flops 1310720 | bytes 2113792 | tf_op jit(solution)/shard_map/convert_element_type | solution.py:264
  212.1 2.3 copy.73
  214.5 1.2 fusion.12
  215.7 1.4 fusion.3
  217.1 2.5 %multiply_reduce_fusion.1 = (f32[64]{0:T(128)S(1)}, f32[64,2,16,128]{3,0,2,1:T(8,128)}) fusion(f32[64,2,16]{0,2,1:T(8,128)S(1)} %bitcast.268, bf16[128,2,2,128]{3,0,2,1:T(8,128)(2,1)S(1)} %copy.70, bf16[512,2,2,128]{3,0,2,1:T(8,128)(2,1)S(1)} %copy.69, f32[2,640,64,16]{1,2,3,0:T(8,128)S(1)} %get-tuple-element.32, f32[2,16,64]{2,1,0:T(8,128)S(1)} %get-tuple-element.31, ...), kind=kOutput, calls=%fused_computation.65 | convolution fusion | flops 342228928 | bytes 7004416 | tf_op jit(solution)/shard_map/grtk,kgd->grtd/dot_general | solution.py:253
  219.6 1.8 copy.75
  221.5 1.6 fusion.25
  223.1 1.5 copy.76
  224.7 1.7 collective-permute-start.1
  226.4 8.1 %collective-permute-done.1 = bf16[1,64,4096]{2,1,0:T(8,128)(2,1)S(1)} collective-permute-done((bf16[1,64,4096]{2,1,0:T(8,128)(2,1)S(1)}, bf16[1,64,4096]{2,1,0:T(8,128)(2,1)S(1)}, u32[]{:S(2)}, u32[]{:S(2)}) %collective-permute-start.1) | collective-permute-done | bytes 524320 | tf_op jit(solution)/shard_map/ppermute | solution.py:27
  234.5 2.1 pad_maximum_fusion.1
  (84 shorter events, 2.5 us)
Async XLA Ops:
  0.0 11.5 %copy-start.15 = (s32[64]{0:T(128)S(1)}, s32[64]{0:T(128)}, u32[]{:S(2)}) copy-start(s32[64]{0:T(128)} %param.21) | copy-start | bytes 772
  0.0 12.3 %copy-start = (s32[1,8192]{1,0:T(1,128)S(1)}, s32[1,8192]{1,0:T(1,128)}, u32[]{:S(2)}) copy-start(s32[1,8192]{1,0:T(1,128)} %param.20) | copy-start | bytes 98308
  18.7 85.0 %all-to-all-start = ((bf16[64,80,128]{2,1,0:T(8,128)(2,1)}), bf16[64,80,128]{2,1,0:T(8,128)(2,1)S(1)}, u32[]{:S(2)}, u32[]{:S(2)}) async-start(bf16[64,80,128]{2,1,0:T(8,128)(2,1)} %get-tuple-element.8), calls=%async_computation | async-start | bytes 2621440 | tf_op jit(solution)/shard_map/all_to_all | solution.py:174
  38.4 2.1 copy-start.12
  38.4 2.1 copy-start.13
  112.0 7.4 %copy-start.6 = (bf16[1,128,512]{2,1,0:T(8,128)(2,1)S(1)}, bf16[1,128,512]{2,1,0:T(8,128)(2,1)}, u32[]{:S(2)}) copy-start(bf16[1,128,512]{2,1,0:T(8,128)(2,1)} %param.18) | copy-start | bytes 393220
  112.0 7.6 %copy-start.5 = (bf16[1,128,2048]{2,1,0:T(8,128)(2,1)S(1)}, bf16[1,128,2048]{2,1,0:T(8,128)(2,1)}, u32[]{:S(2)}) copy-start(bf16[1,128,2048]{2,1,0:T(8,128)(2,1)} %param.12) | copy-start | bytes 1572868
  112.0 8.6 %copy-start.3 = (bf16[1,128,4096]{2,1,0:T(8,128)(2,1)S(1)}, bf16[1,128,4096]{2,1,0:T(8,128)(2,1)}, u32[]{:S(2)}) copy-start(bf16[1,128,4096]{2,1,0:T(8,128)(2,1)} %param.11) | copy-start | bytes 3145732
  112.0 83.0 %all-to-all-start.1 = ((bf16[64,96,128]{2,1,0:T(8,128)(2,1)}), bf16[64,96,128]{2,1,0:T(8,128)(2,1)}, u32[]{:S(2)}, u32[]{:S(2)}) async-start(bf16[64,96,128]{2,1,0:T(8,128)(2,1)} %pad_maximum_fusion), calls=%async_computation.1 | async-start | bytes 3145728 | tf_op jit(solution)/shard_map/all_to_all | solution.py:203
  119.6 2.7 %copy-start.14 = (f32[1,64]{1,0:T(1,128)S(1)}, f32[1,64]{1,0:T(1,128)}, u32[]{:S(2)}) copy-start(f32[1,64]{1,0:T(1,128)} %param.16) | copy-start | bytes 772
  119.6 3.5 %copy-start.7 = (bf16[1,128,64]{1,2,0:T(8,128)(2,1)S(1)}, bf16[1,128,64]{1,2,0:T(8,128)(2,1)}, u32[]{:S(2)}) copy-start(bf16[1,128,64]{1,2,0:T(8,128)(2,1)} %param.13) | copy-start | bytes 49156
  123.9 3.9 %copy-start.10 = (s32[1,128]{1,0:T(1,128)S(1)}, s32[1,128]{1,0:T(1,128)}, u32[]{:S(2)}) copy-start(s32[1,128]{1,0:T(1,128)} %get-tuple-element.12.seg_ref) | copy-start | bytes 1540
  123.9 4.2 %copy-start.9 = (f32[64,128]{1,0:T(8,128)S(1)}, f32[64,128]{1,0:T(8,128)}, u32[]{:S(2)}) copy-start(f32[64,128]{1,0:T(8,128)} %get-tuple-element.9) | copy-start | bytes 98308
  123.9 4.4 %copy-start.4 = (bf16[1,128,2048]{1,2,0:T(8,128)(2,1)S(1)}, bf16[1,128,2048]{1,2,0:T(8,128)(2,1)}, u32[]{:S(2)}) copy-start(bf16[1,128,2048]{1,2,0:T(8,128)(2,1)} %copy.57) | copy-start | bytes 1572868
  195.0 2.6 %copy-start.2 = (f32[8,8,64,128]{3,2,1,0:T(8,128)S(1)}, f32[8,8,64,128]{3,2,1,0:T(8,128)}, u32[]{:S(2)}) copy-start(f32[8,8,64,128]{3,2,1,0:T(8,128)} %fusion.5) | copy-start | bytes 6291460
  197.6 1.2 copy-start.1
  197.6 1.2 copy-start.11
  206.2 3.2 %copy-start.8 = (f32[1,4096]{1,0:T(1,128)S(1)}, f32[1,4096]{1,0:T(1,128)}, u32[]{:S(2)}) copy-start(f32[1,4096]{1,0:T(1,128)} %param.19) | copy-start | bytes 49156
  214.5 11.9 %collective-permute-start = (bf16[1,64,4096]{2,1,0:T(8,128)(2,1)}, bf16[1,64,4096]{2,1,0:T(8,128)(2,1)}, u32[]{:S(2)}, u32[]{:S(2)}) collective-permute-start(bf16[1,64,4096]{2,1,0:T(8,128)(2,1)} %copy.73), channel_id=1, source_target_pairs={{0,64},{64,128},{128,192},{192,256},{256,320},{320,384},{384,448},... | collective-permute-start | bytes 1572872 | tf_op jit(solution)/shard_map/ppermute | solution.py:27
  224.7 9.8 %collective-permute-start.1 = (bf16[1,64,4096]{2,1,0:T(8,128)(2,1)S(1)}, bf16[1,64,4096]{2,1,0:T(8,128)(2,1)S(1)}, u32[]{:S(2)}, u32[]{:S(2)}) collective-permute-start(bf16[1,64,4096]{2,1,0:T(8,128)(2,1)S(1)} %copy.76), channel_id=1, source_target_pairs={{0,64},{64,128},{128,192},{192,256},{256,320},{320,384},{384,448},... | collective-permute-start | bytes 1572872 | tf_op jit(solution)/shard_map/ppermute | solution.py:27

commit v9 on v8

--- a/solution.py
+++ b/solution.py
@@ -60,21 +60,21 @@
 
 
 def states_kernel(xt_ref, bc_ref, raw_ref, bias_ref, rate_ref, seg_ref, tail_ref, out_ref, cum_ref):
-    length = raw_ref.shape[1]
+    length = raw_ref.shape[0]
     within = HEADS // GROUPS
     shifted = raw_ref[...].astype(jnp.float32) + bias_ref[...]
     steps = jnp.maximum(shifted, 0.0) + jnp.log1p(jnp.exp(-jnp.abs(shifted)))
     cum = -rate_ref[...] * steps
-    lane = lax.broadcasted_iota(jnp.int32, cum.shape, 1)
+    row = lax.broadcasted_iota(jnp.int32, cum.shape, 0)
     reach = 1
     while reach < length:
-        cum = cum + jnp.where(lane >= reach, pltpu.roll(cum, reach, 1), 0.0)
+        cum = cum + jnp.where(row >= reach, pltpu.roll(cum, reach, 0), 0.0)
         reach *= 2
     cum_ref[...] = cum
-    ending = cum[:, length - 1 : length]
+    ending = cum[length - 1 : length, :]
     seg = seg_ref[...]
-    same = seg == seg[:, length - 1 : length]
-    weights = jnp.where(same, jnp.exp(ending - cum), 0.0) * steps
+    same = seg == seg[length - 1 : length, :]
+    weights = (jnp.where(same, jnp.exp(ending - cum), 0.0) * steps).T
     for group in range(GROUPS):
         w = weights[group * within : (group + 1) * within]
         w = jnp.broadcast_to(w[:, None, :], (within, HEAD_DIM, length)).reshape(within * HEAD_DIM, length)
@@ -99,7 +99,7 @@
         states_kernel,
         out_shape=(
             jax.ShapeDtypeStruct((HEADS, rows, STATE), jnp.bfloat16),
-            jax.ShapeDtypeStruct((HEADS, tokens), jnp.float32),
+            jax.ShapeDtypeStruct((tokens, HEADS), jnp.float32),
         ),
         cost_estimate=pl.CostEstimate(
             flops=4 * HEADS * HEAD_DIM * STATE * tokens,
@@ -109,10 +109,10 @@
     )(
         inputs.T,
         projections,
-        raw.T,
-        bias.reshape(HEADS, 1),
-        rate.reshape(HEADS, 1),
-        seg.reshape(1, tokens),
+        raw,
+        bias.reshape(1, HEADS),
+        rate.reshape(1, HEADS),
+        seg.reshape(tokens, 1),
         tail,
     )
 
@@ -167,10 +167,9 @@
     used = kv_rows + 1
     padding = jnp.zeros((devices, -used % 8, lanes), jnp.bfloat16)
     tail = jnp.concatenate([kv_slices, raw_cols, padding], axis=1)
-    first, cum_t = block_states(
+    first, cum_log = block_states(
         inputs, state_proj[0], dt_raw[0], dt_bias[0], decay_rate[0], my_seg, tail
     )
-    cum_log = cum_t.T
     got = lax.all_to_all(first, "ctx", split_axis=0, concat_axis=0, tiled=True)
     got_kv = got[:, HEAD_DIM : HEAD_DIM + kv_rows]
     got_raw = got[:, HEAD_DIM + kv_rows].astype(jnp.float32)

time: 238 us -> 238 us (level)
  waiting for transfers between devices: 127 us -> 124 us
  other arithmetic: 18.9 us -> 21.6 us
    all_to_all x1, waiting for transfers between devices: 56.8 us -> 53.8 us  [on_device(): lax.all_to_all(second, 'ctx', split_axis=0, concat_axis=0, tiled=True)]
    another operation x3 -> x1, local copies, waits for them, and re-layouts: 2.79 us -> 0.1 us  [the longest x1 1.35 us: block_states(): rate.reshape(HEADS, 1)]
    unnamed x39 -> x46, local copies, waits for them, and re-layouts: 4.91 us -> 6.91 us
  transfers between devices with their start and end apart: 4 -> 4, of which waited for: 3 -> 3; matrix products, arithmetic and copies ran while one was open for 14% -> 15% of each run, Pallas kernels for 0% -> 0%
where the time goes in v9:
time: 238 us; the launch traced here: 237 us
  waiting for transfers between devices  124 us (52%)
  local copies, waits for them, and re-layouts  37.3 us (16%)
  starting transfers between devices  26.5 us (11%)
  other arithmetic  21.6 us (9%)
  matrix products  19.9 us (8%)
  between operations  3.81 us (2%)
  Pallas kernels  3.42 us (1%)
    all_to_all x1, waiting for transfers between devices, on_device(): got = lax.all_to_all(first, 'ctx', split_axis=0, concat_axis=0, tiled=True)  62.4 us
    all_to_all x1, waiting for transfers between devices, on_device(): lax.all_to_all(second, 'ctx', split_axis=0, concat_axis=0, tiled=True)  53.8 us
    all_to_all x1, starting transfers between devices, on_device(): got = lax.all_to_all(first, 'ctx', split_axis=0, concat_axis=0, tiled=True)  18.6 us
    dot_general x1, matrix products, block_terms(): jnp.einsum('gktu,ugkp->tgkp', weights, scaled.reshape(length, GROUPS, wit...  9.58 us
    ppermute x2, waiting for transfers between devices, passed_along(): return lax.ppermute(value, axis, pairs)  8.13 us
    unnamed x46, local copies, waits for them, and re-layouts  6.91 us
    all_to_all x1, starting transfers between devices, on_device(): lax.all_to_all(second, 'ctx', split_axis=0, concat_axis=0, tiled=True)  6.22 us
    dot_general x2, matrix products, on_device(): jnp.einsum('grtk,kgd->grtd', weights.astype(jnp.bfloat16), vals, preferre...  5.04 us
  transfers between devices with their start and end apart: 4, of which 3 were waited for; matrix products, arithmetic and copies ran while one was open for 15% of the time, Pallas kernels for 0%

profile of v9, /device:TPU:6, one launch (start us, length us, event | category | flops | bytes accessed | tf_op | source)
XLA Modules:
  0.0 236.8 jit_solution(6646208296802651254)
XLA Ops:
  0.0 1.3 dynamic_slice.15
  3.2 1.4 copy.78
  4.6 0.7 copy.86
  5.3 0.8 slice.88
  6.9 0.7 broadcast_add_fusion.1
  7.7 0.6 dynamic_slice.19
  8.2 1.8 broadcast_compare_fusion.1
  10.0 0.6 copy-done.12
  10.6 0.7 copy.87.seg_ref
  11.3 1.0 reshape_squeeze.11
  12.3 2.3 copy.76
  14.7 0.8 maximum_maximum_fusion.tail_ref
  15.5 3.4 %shard_map.109 = (bf16[64,80,128]{2,1,0:T(8,128)(2,1)}, f32[128,64]{1,0:T(8,128)}) custom-call(bf16[4096,128]{1,0:T(8,128)(2,1)} %bitcast.226, bf16[128,2048]{1,0:T(8,128)(2,1)} %bitcast.236, bf16[128,64]{1,0:T(8,128)(2,1)} %bitcast.241, f32[1,64]{1,0:T(1,128)} %bias_ref.1, f32[1,64]{1,0:T(1,128)} %rate_ref.1, s32[128,1]{1,0:T(8,128)} %copy.87.seg_ref, ...), custom_call_target="tpu_custom_call" | custom-call | flops 268435456 | bytes 2883584 | tf_op jit(solution)/shard_map/pallas_call | solution.py:98
  18.9 18.6 %all-to-all-start = ((bf16[64,80,128]{2,1,0:T(8,128)(2,1)}), bf16[64,80,128]{2,1,0:T(8,128)(2,1)S(1)}, u32[]{:S(2)}, u32[]{:S(2)}) async-start(bf16[64,80,128]{2,1,0:T(8,128)(2,1)} %get-tuple-element.8), calls=%async_computation | async-start | bytes 2621440 | tf_op jit(solution)/shard_map/all_to_all | solution.py:173
  37.9 0.8 scatter_custom_fusion
  38.7 1.9 gather_fusion.3
  40.8 0.7 constant_dynamic-slice_fusion
  41.5 62.4 %all-to-all-done = bf16[64,80,128]{2,1,0:T(8,128)(2,1)S(1)} async-done(((bf16[64,80,128]{2,1,0:T(8,128)(2,1)}), bf16[64,80,128]{2,1,0:T(8,128)(2,1)S(1)}, u32[]{:S(2)}, u32[]{:S(2)}) %all-to-all-start) | async-done | bytes 1310752 | tf_op jit(solution)/shard_map/all_to_all | solution.py:173
  104.0 0.6 fusion.73
  104.5 0.8 fusion.72
  105.3 0.8 gather_fusion
  106.6 0.6 gather_fusion.1
  107.2 0.6 gather_fusion.2
  108.0 0.9 fusion.47
  108.9 1.0 fusion.45
  109.8 0.3 copy.112
  110.1 0.8 gather_fusion.4
  110.9 1.3 pad_maximum_fusion
  112.2 6.2 %all-to-all-start.1 = ((bf16[64,96,128]{2,1,0:T(8,128)(2,1)}), bf16[64,96,128]{2,1,0:T(8,128)(2,1)}, u32[]{:S(2)}, u32[]{:S(2)}) async-start(bf16[64,96,128]{2,1,0:T(8,128)(2,1)} %pad_maximum_fusion), calls=%async_computation.1 | async-start | bytes 3145728 | tf_op jit(solution)/shard_map/all_to_all | solution.py:202
  119.3 0.7 add.296
  120.1 0.8 concatenate.50
  121.0 1.0 copy.80
  122.0 0.5 copy.77
  122.5 0.5 broadcast.356
  123.0 0.6 reduce.13
  123.7 0.6 reduce.14
  124.4 0.7 mul.200
  125.7 0.7 exponential_select_fusion
  126.4 0.7 fusion.84
  127.2 3.9 %gather_fusion.5 = s32[640]{0:T(1024)S(1)} fusion(s32[8192]{0:T(1024)S(1)} %bitcast.222, s32[1024]{0:T(1024)S(1)} %pad_clamp_fusion), kind=kCustom, calls=%fused_computation.5 | custom fusion | bytes 7680 | tf_op jit(solution)/shard_map/jit(_take)/gather | solution.py:227
  131.6 0.3 fusion.61
  131.8 9.6 %fusion.5 = f32[8,8,64,128]{3,2,1,0:T(8,128)} fusion(f32[8,128,128]{2,1,0:T(8,128)S(1)} %fusion.61, f32[8,8,128]{2,1,0:T(8,128)S(1)} %bitcast.247, f32[128,8,8,64]{0,3,2,1:T(8,128)S(1)} %bitcast.227, pred[128,128]{1,0:T(8,128)(4,1)S(1)} %fusion.68, f32[128,8,8]{0,2,1:T(8,128)S(1)} %compare_select_fusion.4), kind=kOutput, calls=%fused_computation.17 | convolution fusion | flops 810024960 | bytes 4800512 | tf_op jit(solution)/shard_map/gktu,ugkp->tgkp/dot_general | solution.py:47
  141.4 53.8 %all-to-all-done.1 = bf16[64,96,128]{2,1,0:T(8,128)(2,1)} async-done(((bf16[64,96,128]{2,1,0:T(8,128)(2,1)}), bf16[64,96,128]{2,1,0:T(8,128)(2,1)}, u32[]{:S(2)}, u32[]{:S(2)}) %all-to-all-start.1) | async-done | bytes 1572896 | tf_op jit(solution)/shard_map/all_to_all | solution.py:202
  195.2 1.2 slice.94
  196.5 1.3 slice.92
  197.9 0.7 multiply_reduce_fusion
  198.6 0.5 copy-done.1
  199.1 1.6 fusion.21
  200.7 0.4 fusion.100
  201.0 1.2 fusion.11
  202.3 1.6 fusion.1
  203.9 2.5 %multiply_reduce_fusion.2 = (f32[64]{0:T(128)S(1)}, f32[64,2,16,128]{3,0,2,1:T(8,128)}) fusion(f32[64,2,16]{0,2,1:T(8,128)S(1)} %bitcast.252, bf16[128,2,2,128]{3,0,2,1:T(8,128)(2,1)S(1)} %copy.94, bf16[512,2,2,128]{3,0,2,1:T(8,128)(2,1)S(1)} %copy.93, f32[2,640,64,16]{1,2,3,0:T(8,128)S(1)} %get-tuple-element.26, f32[2,16,64]{2,1,0:T(8,128)S(1)} %get-tuple-element.25, ...), kind=kOutput, calls=%fused_computation.66 | convolution fusion | flops 342228928 | bytes 7004416 | tf_op jit(solution)/shard_map/grtk,kgd->grtd/dot_general | solution.py:252
  206.5 3.2 %copy.96 = f32[64,2,16,128]{0,3,2,1:T(8,128)} copy(f32[64,2,16,128]{3,0,2,1:T(8,128)} %get-tuple-element.28) | data formatting | bytes 2097152 | tf_op jit(solution)/shard_map/div | solution.py:256
  209.6 2.7 %fusion.28 = bf16[64,4096]{0,1:T(8,128)(2,1)} fusion(f32[64,2,16,128]{0,3,2,1:T(8,128)} %copy.96, f32[4096]{0:T(1024)S(1)} %bitcast.245, f32[64]{0:T(128)S(1)} %add_rsqrt_fusion.2, bf16[128,4096]{0,1:T(8,128)(2,1)S(1)} %fusion.21), kind=kLoop, calls=%fused_computation.43 | loop fusion | flops 1310720 | bytes 2113792 | tf_op jit(solution)/shard_map/convert_element_type | solution.py:263
  212.4 2.3 copy.97
  214.7 1.2 fusion.12
  215.9 1.4 fusion.3
  217.3 2.5 %multiply_reduce_fusion.1 = (f32[64]{0:T(128)S(1)}, f32[64,2,16,128]{3,0,2,1:T(8,128)}) fusion(f32[64,2,16]{0,2,1:T(8,128)S(1)} %bitcast.251, bf16[128,2,2,128]{3,0,2,1:T(8,128)(2,1)S(1)} %copy.94, bf16[512,2,2,128]{3,0,2,1:T(8,128)(2,1)S(1)} %copy.93, f32[2,640,64,16]{1,2,3,0:T(8,128)S(1)} %get-tuple-element.30, f32[2,16,64]{2,1,0:T(8,128)S(1)} %get-tuple-element.29, ...), kind=kOutput, calls=%fused_computation.65 | convolution fusion | flops 342228928 | bytes 7004416 | tf_op jit(solution)/shard_map/grtk,kgd->grtd/dot_general | solution.py:252
  219.9 1.8 copy.99
  221.7 1.6 fusion.25
  223.4 1.5 copy.100
  224.9 1.7 collective-permute-start.1
  226.6 8.1 %collective-permute-done.1 = bf16[1,64,4096]{2,1,0:T(8,128)(2,1)S(1)} collective-permute-done((bf16[1,64,4096]{2,1,0:T(8,128)(2,1)S(1)}, bf16[1,64,4096]{2,1,0:T(8,128)(2,1)S(1)}, u32[]{:S(2)}, u32[]{:S(2)}) %collective-permute-start.1) | collective-permute-done | bytes 524320 | tf_op jit(solution)/shard_map/ppermute | solution.py:27
  234.7 2.1 pad_maximum_fusion.1
  (90 shorter events, 3.0 us)
Async XLA Ops:
  10.0 0.6 copy-start.12
  15.5 22.0 %copy-start = (s32[1,8192]{1,0:T(1,128)S(1)}, s32[1,8192]{1,0:T(1,128)}, u32[]{:S(2)}) copy-start(s32[1,8192]{1,0:T(1,128)} %param.20) | copy-start | bytes 98308
  18.9 85.0 %all-to-all-start = ((bf16[64,80,128]{2,1,0:T(8,128)(2,1)}), bf16[64,80,128]{2,1,0:T(8,128)(2,1)S(1)}, u32[]{:S(2)}, u32[]{:S(2)}) async-start(bf16[64,80,128]{2,1,0:T(8,128)(2,1)} %get-tuple-element.8), calls=%async_computation | async-start | bytes 2621440 | tf_op jit(solution)/shard_map/all_to_all | solution.py:173
  38.7 2.1 copy-start.16
  38.7 2.1 copy-start.17
  112.2 8.6 %copy-start.6 = (bf16[1,128,512]{2,1,0:T(8,128)(2,1)S(1)}, bf16[1,128,512]{2,1,0:T(8,128)(2,1)}, u32[]{:S(2)}) copy-start(bf16[1,128,512]{2,1,0:T(8,128)(2,1)} %param.18) | copy-start | bytes 393220
  112.2 8.7 %copy-start.5 = (bf16[1,128,2048]{2,1,0:T(8,128)(2,1)S(1)}, bf16[1,128,2048]{2,1,0:T(8,128)(2,1)}, u32[]{:S(2)}) copy-start(bf16[1,128,2048]{2,1,0:T(8,128)(2,1)} %param.12) | copy-start | bytes 1572868
  112.2 9.8 %copy-start.3 = (bf16[1,128,4096]{2,1,0:T(8,128)(2,1)S(1)}, bf16[1,128,4096]{2,1,0:T(8,128)(2,1)}, u32[]{:S(2)}) copy-start(bf16[1,128,4096]{2,1,0:T(8,128)(2,1)} %param.11) | copy-start | bytes 3145732
  112.2 83.0 %all-to-all-start.1 = ((bf16[64,96,128]{2,1,0:T(8,128)(2,1)}), bf16[64,96,128]{2,1,0:T(8,128)(2,1)}, u32[]{:S(2)}, u32[]{:S(2)}) async-start(bf16[64,96,128]{2,1,0:T(8,128)(2,1)} %pad_maximum_fusion), calls=%async_computation.1 | async-start | bytes 3145728 | tf_op jit(solution)/shard_map/all_to_all | solution.py:202
  121.0 2.7 %copy-start.18 = (f32[1,64]{1,0:T(1,128)S(1)}, f32[1,64]{1,0:T(1,128)}, u32[]{:S(2)}) copy-start(f32[1,64]{1,0:T(1,128)} %param.16) | copy-start | bytes 772
  121.0 4.2 %copy-start.7 = (bf16[1,128,64]{2,1,0:T(8,128)(2,1)S(1)}, bf16[1,128,64]{2,1,0:T(8,128)(2,1)}, u32[]{:S(2)}) copy-start(bf16[1,128,64]{2,1,0:T(8,128)(2,1)} %copy.78) | copy-start | bytes 49156
  122.0 3.7 %copy-start.10 = (f32[128,64]{1,0:T(8,128)S(1)}, f32[128,64]{1,0:T(8,128)}, u32[]{:S(2)}) copy-start(f32[128,64]{1,0:T(8,128)} %get-tuple-element.9) | copy-start | bytes 98308
  127.2 3.9 %copy-start.11 = (s32[512]{0:T(512)S(1)}, s32[512]{0:T(512)}, u32[]{:S(2)}) copy-start(s32[512]{0:T(512)} %add.296) | copy-start | bytes 6148
  127.2 4.0 %copy-start.13 = (s32[1,128]{1,0:T(1,128)S(1)}, s32[1,128]{1,0:T(1,128)}, u32[]{:S(2)}) copy-start(s32[1,128]{1,0:T(1,128)} %copy-done.12) | copy-start | bytes 1540
  127.2 4.1 %copy-start.8 = (bf16[1,128,64]{1,2,0:T(8,128)(2,1)S(1)}, bf16[1,128,64]{1,2,0:T(8,128)(2,1)}, u32[]{:S(2)}) copy-start(bf16[1,128,64]{1,2,0:T(8,128)(2,1)} %param.13) | copy-start | bytes 49156
  127.2 4.4 %copy-start.4 = (bf16[1,128,2048]{1,2,0:T(8,128)(2,1)S(1)}, bf16[1,128,2048]{1,2,0:T(8,128)(2,1)}, u32[]{:S(2)}) copy-start(bf16[1,128,2048]{1,2,0:T(8,128)(2,1)} %copy.80) | copy-start | bytes 1572868
  141.4 56.4 %copy-start.15 = (f32[8,8]{1,0:T(8,128)S(1)}, f32[8,8]{1,0:T(8,128)}, u32[]{:S(2)}) copy-start(f32[8,8]{1,0:T(8,128)} %mul.200) | copy-start | bytes 772
  195.2 2.6 %copy-start.2 = (f32[8,8,64,128]{3,2,1,0:T(8,128)S(1)}, f32[8,8,64,128]{3,2,1,0:T(8,128)}, u32[]{:S(2)}) copy-start(f32[8,8,64,128]{3,2,1,0:T(8,128)} %fusion.5) | copy-start | bytes 6291460
  197.8 1.2 copy-start.1
  197.9 1.2 copy-start.14
  206.4 3.2 %copy-start.9 = (f32[1,4096]{1,0:T(1,128)S(1)}, f32[1,4096]{1,0:T(1,128)}, u32[]{:S(2)}) copy-start(f32[1,4096]{1,0:T(1,128)} %param.19) | copy-start | bytes 49156
  214.7 11.9 %collective-permute-start = (bf16[1,64,4096]{2,1,0:T(8,128)(2,1)}, bf16[1,64,4096]{2,1,0:T(8,128)(2,1)}, u32[]{:S(2)}, u32[]{:S(2)}) collective-permute-start(bf16[1,64,4096]{2,1,0:T(8,128)(2,1)} %copy.97), channel_id=1, source_target_pairs={{0,64},{64,128},{128,192},{192,256},{256,320},{320,384},{384,448},... | collective-permute-start | bytes 1572872 | tf_op jit(solution)/shard_map/ppermute | solution.py:27
  224.9 9.8 %collective-permute-start.1 = (bf16[1,64,4096]{2,1,0:T(8,128)(2,1)S(1)}, bf16[1,64,4096]{2,1,0:T(8,128)(2,1)S(1)}, u32[]{:S(2)}, u32[]{:S(2)}) collective-permute-start(bf16[1,64,4096]{2,1,0:T(8,128)(2,1)S(1)} %copy.100), channel_id=1, source_target_pairs={{0,64},{64,128},{128,192},{192,256},{256,320},{320,384},{384,448},... | collective-permute-start | bytes 1572872 | tf_op jit(solution)/shard_map/ppermute | solution.py:27

commit v10 on v9

--- a/solution.py
+++ b/solution.py
@@ -59,7 +59,7 @@
     return local_out, states, cum_log, ending
 
 
-def states_kernel(xt_ref, bc_ref, raw_ref, bias_ref, rate_ref, seg_ref, tail_ref, out_ref, cum_ref):
+def states_kernel(x_ref, bc_ref, raw_ref, bias_ref, rate_ref, seg_ref, tail_ref, out_ref, cum_ref):
     length = raw_ref.shape[0]
     within = HEADS // GROUPS
     shifted = raw_ref[...].astype(jnp.float32) + bias_ref[...]
@@ -74,18 +74,25 @@
     ending = cum[length - 1 : length, :]
     seg = seg_ref[...]
     same = seg == seg[length - 1 : length, :]
-    weights = (jnp.where(same, jnp.exp(ending - cum), 0.0) * steps).T
+    weights = jnp.where(same, jnp.exp(ending - cum), 0.0) * steps
+    w_high = weights.astype(jnp.bfloat16)
+    w_low = (weights - w_high.astype(jnp.float32)).astype(jnp.bfloat16)
+    width = within * HEAD_DIM
+    head_of = lax.broadcasted_iota(jnp.int32, (HEADS, width), 0)
+    column = lax.broadcasted_iota(jnp.int32, (HEADS, width), 1)
     for group in range(GROUPS):
-        w = weights[group * within : (group + 1) * within]
-        w = jnp.broadcast_to(w[:, None, :], (within, HEAD_DIM, length)).reshape(within * HEAD_DIM, length)
-        rows = slice(group * within * HEAD_DIM, (group + 1) * within * HEAD_DIM)
-        scaled = xt_ref[rows, :].astype(jnp.float32) * w
+        spread = (column // HEAD_DIM + group * within == head_of).astype(jnp.bfloat16)
+        w = jnp.dot(w_high, spread, preferred_element_type=jnp.float32) + jnp.dot(
+            w_low, spread, preferred_element_type=jnp.float32
+        )
+        scaled = x_ref[:, group * width : (group + 1) * width].astype(jnp.float32) * w
         high = scaled.astype(jnp.bfloat16)
         low = (scaled - high.astype(jnp.float32)).astype(jnp.bfloat16)
         inject = bc_ref[:, group * 2 * STATE : group * 2 * STATE + STATE]
-        state = jnp.dot(high, inject, preferred_element_type=jnp.float32) + jnp.dot(
-            low, inject, preferred_element_type=jnp.float32
-        )
+        over_tokens = (((0,), (0,)), ((), ()))
+        state = lax.dot_general(
+            high, inject, over_tokens, preferred_element_type=jnp.float32
+        ) + lax.dot_general(low, inject, over_tokens, preferred_element_type=jnp.float32)
         out_ref[group * within : (group + 1) * within, :HEAD_DIM, :] = (
             state.astype(out_ref.dtype).reshape(within, HEAD_DIM, STATE)
         )
@@ -107,7 +114,7 @@
             bytes_accessed=inputs.size * 2 + projections.size * 2 + HEADS * rows * STATE * 2,
         ),
     )(
-        inputs.T,
+        inputs,
         projections,
         raw,
         bias.reshape(1, HEADS),

time: 238 us -> 229 us (0.962)
  waiting for transfers between devices: 124 us -> 116 us
  other arithmetic: 21.6 us -> 16.9 us
  local copies, waits for them, and re-layouts: 37.3 us -> 40.8 us
    all_to_all x1, waiting for transfers between devices: 53.8 us -> 45.3 us  [on_device(): lax.all_to_all(second, 'ctx', split_axis=0, concat_axis=0, tiled=True)]
    reshape x0 -> x2, local copies, waits for them, and re-layouts: none -> 5.02 us  [the longest x1 2.87 us: block_terms(): local_out = jnp.einsum('gktu,ugkp->tgkp', weights, scaled.reshape(length,...]
    mul x0 -> x3, local copies, waits for them, and re-layouts: none -> 4.58 us  [the longest x2 4.38 us: on_device(): read_out * reach[..., None]]
    broadcast_in_dim x2 -> x0, local copies, waits for them, and re-layouts: 3.88 us -> none  [on_device(): handed.append(passed_along(result[None], 'phase', 1))]
    div x2, local copies, waits for them, and re-layouts: 5.03 us -> 1.23 us  [on_device(): blended / total_weight[..., None]]
    convert_element_type x2 -> x1, other arithmetic: 4.36 us -> 0.79 us  [on_device(): result = (hidden_part.astype(jnp.float32) + normed).astype(jnp.bfloat16)]
    unnamed x46 -> x55, local copies, waits for them, and re-layouts: 6.91 us -> 7.44 us
  transfers between devices with their start and end apart: 4 -> 4, of which waited for: 3 -> 4; matrix products, arithmetic and copies ran while one was open for 15% -> 18% of each run, Pallas kernels for 0% -> 0%
where the time goes in v10:
time: 229 us; the launch traced here: 228 us
  waiting for transfers between devices  116 us (51%)
  local copies, waits for them, and re-layouts  40.8 us (18%)
  starting transfers between devices  26.5 us (12%)
  matrix products  20.5 us (9%)
  other arithmetic  16.9 us (7%)
  Pallas kernels  4.04 us (2%)
  between operations  3.53 us (2%)
    all_to_all x1, waiting for transfers between devices, on_device(): got = lax.all_to_all(first, 'ctx', split_axis=0, concat_axis=0, tiled=True)  62.5 us
    all_to_all x1, waiting for transfers between devices, on_device(): lax.all_to_all(second, 'ctx', split_axis=0, concat_axis=0, tiled=True)  45.3 us
    all_to_all x1, starting transfers between devices, on_device(): got = lax.all_to_all(first, 'ctx', split_axis=0, concat_axis=0, tiled=True)  18.6 us
    dot_general x1, matrix products, block_terms(): jnp.einsum('gktu,ugkp->tgkp', weights, scaled.reshape(length, GROUPS, wit...  9.58 us
    ppermute x2, waiting for transfers between devices, passed_along(): return lax.ppermute(value, axis, pairs)  8.15 us
    unnamed x55, local copies, waits for them, and re-layouts  7.44 us
    all_to_all x1, starting transfers between devices, on_device(): lax.all_to_all(second, 'ctx', split_axis=0, concat_axis=0, tiled=True)  6.23 us
  transfers between devices with their start and end apart: 4, of which 4 were waited for; matrix products, arithmetic and copies ran while one was open for 18% of the time, Pallas kernels for 0%

profile of v10, /device:TPU:6, one launch (start us, length us, event | category | flops | bytes accessed | tf_op | source)
XLA Modules:
  0.0 228.3 jit_solution(2117299066092355898)
XLA Ops:
  0.0 1.2 dynamic_slice.15
  2.9 1.4 copy.80
  4.4 0.7 copy.88
  5.1 0.8 slice.88
  6.6 0.7 broadcast_add_fusion.1
  7.3 0.6 dynamic_slice.19
  7.9 1.9 broadcast_compare_fusion.1
  10.4 0.7 copy.89.seg_ref
  11.1 1.0 reshape_squeeze.11
  12.2 0.8 maximum_maximum_fusion.tail_ref
  13.0 4.0 %shard_map.109 = (bf16[64,80,128]{2,1,0:T(8,128)(2,1)}, f32[128,64]{1,0:T(8,128)}) custom-call(bf16[128,4096]{1,0:T(8,128)(2,1)} %bitcast.214, bf16[128,2048]{1,0:T(8,128)(2,1)} %bitcast.233, bf16[128,64]{1,0:T(8,128)(2,1)} %bitcast.239, f32[1,64]{1,0:T(1,128)} %bias_ref.1, f32[1,64]{1,0:T(1,128)} %rate_ref.1, s32[128,1]{1,0:T(8,128)} %copy.89.seg_ref, ...), custom_call_target="tpu_custom_call" | custom-call | flops 268435456 | bytes 2883584 | tf_op jit(solution)/shard_map/pallas_call | solution.py:105
  17.1 18.6 %all-to-all-start = ((bf16[64,80,128]{2,1,0:T(8,128)(2,1)}), bf16[64,80,128]{2,1,0:T(8,128)(2,1)S(1)}, u32[]{:S(2)}, u32[]{:S(2)}) async-start(bf16[64,80,128]{2,1,0:T(8,128)(2,1)} %get-tuple-element.8), calls=%async_computation | async-start | bytes 2621440 | tf_op jit(solution)/shard_map/all_to_all | solution.py:180
  36.0 0.8 scatter_custom_fusion
  36.8 1.9 gather_fusion.3
  39.0 0.6 constant_dynamic-slice_fusion
  39.6 62.5 %all-to-all-done = bf16[64,80,128]{2,1,0:T(8,128)(2,1)S(1)} async-done(((bf16[64,80,128]{2,1,0:T(8,128)(2,1)}), bf16[64,80,128]{2,1,0:T(8,128)(2,1)S(1)}, u32[]{:S(2)}, u32[]{:S(2)}) %all-to-all-start) | async-done | bytes 1310752 | tf_op jit(solution)/shard_map/all_to_all | solution.py:180
  102.1 0.7 fusion.76
  102.8 0.8 fusion.75
  103.5 0.8 gather_fusion
  104.7 0.6 gather_fusion.1
  105.4 0.6 gather_fusion.2
  106.1 0.9 fusion.45
  107.0 1.0 fusion.37
  108.3 0.8 gather_fusion.4
  109.1 1.3 pad_maximum_fusion
  110.5 6.2 %all-to-all-start.1 = ((bf16[64,96,128]{2,1,0:T(8,128)(2,1)}), bf16[64,96,128]{2,1,0:T(8,128)(2,1)}, u32[]{:S(2)}, u32[]{:S(2)}) async-start(bf16[64,96,128]{2,1,0:T(8,128)(2,1)} %pad_maximum_fusion), calls=%async_computation.1 | async-start | bytes 3145728 | tf_op jit(solution)/shard_map/all_to_all | solution.py:209
  117.5 0.7 add.296
  118.3 0.7 concatenate.50
  119.2 1.0 copy.82
  120.7 0.6 broadcast.356
  121.2 0.6 reduce.13
  121.9 0.6 reduce.14
  122.5 0.7 add.258
  123.2 0.7 mul.200
  124.5 0.9 exponential_select_fusion
  125.5 1.5 mul.189
  127.0 2.9 %copy.94 = f32[128,4096]{1,0:T(8,128)} copy(f32[128,4096]{0,1:T(8,128)} %bitcast.223) | data formatting | bytes 4194304 | tf_op jit(solution)/shard_map/mul | solution.py:222
  130.1 1.3 fusion.64
  131.4 9.6 %fusion.5 = f32[8,8,64,128]{3,2,1,0:T(8,128)} fusion(f32[8,128,128]{2,1,0:T(8,128)S(1)} %fusion.64, f32[8,8,128]{2,1,0:T(8,128)S(1)} %bitcast.245, f32[128,8,8,64]{0,3,2,1:T(8,128)S(1)} %bitcast.217, pred[128,128]{1,0:T(8,128)(4,1)S(1)} %fusion.71, f32[128,8,8]{0,2,1:T(8,128)S(1)} %compare_select_fusion.4), kind=kOutput, calls=%fused_computation.17 | convolution fusion | flops 810024960 | bytes 4800512 | tf_op jit(solution)/shard_map/gktu,ugkp->tgkp/dot_general | solution.py:47
  141.0 2.9 %copy.95 = f32[128,4096]{1,0:T(8,128)} copy(f32[128,4096]{0,1:T(8,128)} %bitcast.219) | data formatting | bytes 4194304 | tf_op jit(solution)/shard_map/reshape | solution.py:52
  143.9 3.9 %gather_fusion.5 = s32[640]{0:T(1024)S(1)} fusion(s32[8192]{0:T(1024)S(1)} %bitcast.213, s32[1024]{0:T(1024)S(1)} %pad_clamp_fusion), kind=kCustom, calls=%fused_computation.5 | custom fusion | bytes 7680 | tf_op jit(solution)/shard_map/jit(_take)/gather | solution.py:234
  148.1 45.3 %all-to-all-done.1 = bf16[64,96,128]{2,1,0:T(8,128)(2,1)} async-done(((bf16[64,96,128]{2,1,0:T(8,128)(2,1)}), bf16[64,96,128]{2,1,0:T(8,128)(2,1)}, u32[]{:S(2)}, u32[]{:S(2)}) %all-to-all-start.1) | async-done | bytes 1572896 | tf_op jit(solution)/shard_map/all_to_all | solution.py:209
  193.4 1.2 slice.94
  194.7 0.9 copy.99
  195.6 1.3 slice.92
  196.9 1.9 multiply_reduce_fusion
  198.8 2.1 copy.93
  201.3 1.7 copy.115
  203.5 0.9 fusion.21
  204.6 0.9 copy-done.5
  205.5 1.3 fusion.11
  206.8 1.4 fusion.1
  208.2 1.7 multiply_reduce_fusion.2
  209.9 0.6 copy.102
  210.6 0.8 fusion.43
  211.5 1.3 fusion.12
  212.8 1.6 fusion.3
  214.4 1.6 multiply_reduce_fusion.1
  216.0 0.6 copy.104
  216.6 0.8 fusion.56
  217.4 1.7 collective-permute-start.1
  219.1 2.2 collective-permute-done
  221.3 6.0 %collective-permute-done.1 = bf16[1,64,4096]{2,1,0:T(8,128)(2,1)S(1)} collective-permute-done((bf16[1,64,4096]{2,1,0:T(8,128)(2,1)S(1)}, bf16[1,64,4096]{2,1,0:T(8,128)(2,1)S(1)}, u32[]{:S(2)}, u32[]{:S(2)}) %collective-permute-start.1) | collective-permute-done | bytes 524320 | tf_op jit(solution)/shard_map/ppermute | solution.py:27
  227.2 1.1 pad_maximum_fusion.1
  (102 shorter events, 5.3 us)
Async XLA Ops:
  9.8 0.5 copy-start.13
  11.1 24.6 %copy-start = (s32[1,8192]{1,0:T(1,128)S(1)}, s32[1,8192]{1,0:T(1,128)}, u32[]{:S(2)}) copy-start(s32[1,8192]{1,0:T(1,128)} %param.20) | copy-start | bytes 98308
  17.1 85.0 %all-to-all-start = ((bf16[64,80,128]{2,1,0:T(8,128)(2,1)}), bf16[64,80,128]{2,1,0:T(8,128)(2,1)S(1)}, u32[]{:S(2)}, u32[]{:S(2)}) async-start(bf16[64,80,128]{2,1,0:T(8,128)(2,1)} %get-tuple-element.8), calls=%async_computation | async-start | bytes 2621440 | tf_op jit(solution)/shard_map/all_to_all | solution.py:180
  36.8 2.1 copy-start.19
  36.8 2.1 copy-start.20
  109.1 9.9 %copy-start.8 = (bf16[1,128,512]{2,1,0:T(8,128)(2,1)S(1)}, bf16[1,128,512]{2,1,0:T(8,128)(2,1)}, u32[]{:S(2)}) copy-start(bf16[1,128,512]{2,1,0:T(8,128)(2,1)} %param.18) | copy-start | bytes 393220
  110.5 8.7 %copy-start.7 = (bf16[1,128,2048]{2,1,0:T(8,128)(2,1)S(1)}, bf16[1,128,2048]{2,1,0:T(8,128)(2,1)}, u32[]{:S(2)}) copy-start(bf16[1,128,2048]{2,1,0:T(8,128)(2,1)} %param.12) | copy-start | bytes 1572868
  110.5 9.7 %copy-start.1 = (bf16[1,128,4096]{2,1,0:T(8,128)(2,1)S(1)}, bf16[1,128,4096]{2,1,0:T(8,128)(2,1)}, u32[]{:S(2)}) copy-start(bf16[1,128,4096]{2,1,0:T(8,128)(2,1)} %param.11) | copy-start | bytes 3145732
  110.5 83.0 %all-to-all-start.1 = ((bf16[64,96,128]{2,1,0:T(8,128)(2,1)}), bf16[64,96,128]{2,1,0:T(8,128)(2,1)}, u32[]{:S(2)}, u32[]{:S(2)}) async-start(bf16[64,96,128]{2,1,0:T(8,128)(2,1)} %pad_maximum_fusion), calls=%async_computation.1 | async-start | bytes 3145728 | tf_op jit(solution)/shard_map/all_to_all | solution.py:209
  116.7 5.2 %copy-start.21 = (f32[1,64]{1,0:T(1,128)S(1)}, f32[1,64]{1,0:T(1,128)}, u32[]{:S(2)}) copy-start(f32[1,64]{1,0:T(1,128)} %param.16) | copy-start | bytes 772
  116.7 7.3 %copy-start.9 = (bf16[1,128,64]{2,1,0:T(8,128)(2,1)S(1)}, bf16[1,128,64]{2,1,0:T(8,128)(2,1)}, u32[]{:S(2)}) copy-start(bf16[1,128,64]{2,1,0:T(8,128)(2,1)} %copy.80) | copy-start | bytes 49156
  126.9 2.9 %copy-start.14 = (s32[1,128]{1,0:T(1,128)S(1)}, s32[1,128]{1,0:T(1,128)}, u32[]{:S(2)}) copy-start(s32[1,128]{1,0:T(1,128)} %copy-done.13) | copy-start | bytes 1540
  126.9 3.0 %copy-start.10 = (bf16[1,128,64]{1,2,0:T(8,128)(2,1)S(1)}, bf16[1,128,64]{1,2,0:T(8,128)(2,1)}, u32[]{:S(2)}) copy-start(bf16[1,128,64]{1,2,0:T(8,128)(2,1)} %param.13) | copy-start | bytes 49156
  127.0 3.0 %copy-start.17 = (f32[8,8]{1,0:T(8,128)S(1)}, f32[8,8]{1,0:T(8,128)}, u32[]{:S(2)}) copy-start(f32[8,8]{1,0:T(8,128)} %add.258) | copy-start | bytes 772
  141.0 2.9 %copy-start.18 = (s32[512,1]{0,1:T(1,128)S(1)}, s32[512,1]{0,1:T(1,128)}, u32[]{:S(2)}) copy-start(s32[512,1]{0,1:T(1,128)} %concatenate.50) | copy-start | bytes 6148
  143.9 4.0 %copy-start.12 = (s32[512]{0:T(512)S(1)}, s32[512]{0:T(512)}, u32[]{:S(2)}) copy-start(s32[512]{0:T(512)} %add.296) | copy-start | bytes 6148
  147.8 49.1 %copy-start.16 = (f32[8,8]{1,0:T(8,128)S(1)}, f32[8,8]{1,0:T(8,128)}, u32[]{:S(2)}) copy-start(f32[8,8]{1,0:T(8,128)} %mul.200) | copy-start | bytes 772
  193.4 3.4 %copy-start.4 = (f32[8,8,64,128]{3,2,1,0:T(8,128)S(1)}, f32[8,8,64,128]{3,2,1,0:T(8,128)}, u32[]{:S(2)}) copy-start(f32[8,8,64,128]{3,2,1,0:T(8,128)} %fusion.5) | copy-start | bytes 6291460
  193.4 3.4 %copy-start.6 = (bf16[1,128,2048]{1,2,0:T(8,128)(2,1)S(1)}, bf16[1,128,2048]{1,2,0:T(8,128)(2,1)}, u32[]{:S(2)}) copy-start(bf16[1,128,2048]{1,2,0:T(8,128)(2,1)} %copy.82) | copy-start | bytes 1572868
  201.1 1.9 copy-start.15
  201.3 1.7 copy-start.2
  201.3 2.2 copy-start.3
  204.4 1.0 copy-start.5
  208.2 2.3 %copy-start.11 = (f32[1,4096]{1,0:T(1,128)S(1)}, f32[1,4096]{1,0:T(1,128)}, u32[]{:S(2)}) copy-start(f32[1,4096]{1,0:T(1,128)} %param.19) | copy-start | bytes 49156
  211.4 9.8 %collective-permute-start = (bf16[1,64,4096]{2,1,0:T(8,128)(2,1)S(1)}, bf16[1,64,4096]{2,1,0:T(8,128)(2,1)S(1)}, u32[]{:S(2)}, u32[]{:S(2)}) collective-permute-start(bf16[1,64,4096]{2,1,0:T(8,128)(2,1)S(1)} %bitcast.236), channel_id=1, source_target_pairs={{0,64},{64,128},{128,192},{192,256},{256,320},{320,384},{384,448},... | collective-permute-start | bytes 1572872 | tf_op jit(solution)/shard_map/ppermute | solution.py:27
  217.4 9.8 %collective-permute-start.1 = (bf16[1,64,4096]{2,1,0:T(8,128)(2,1)S(1)}, bf16[1,64,4096]{2,1,0:T(8,128)(2,1)S(1)}, u32[]{:S(2)}, u32[]{:S(2)}) collective-permute-start(bf16[1,64,4096]{2,1,0:T(8,128)(2,1)S(1)} %fusion.56), channel_id=1, source_target_pairs={{0,64},{64,128},{128,192},{192,256},{256,320},{320,384},{384,448},... | collective-permute-start | bytes 1572872 | tf_op jit(solution)/shard_map/ppermute | solution.py:27

commit v11 on v10

--- a/solution.py
+++ b/solution.py
@@ -33,10 +33,9 @@
     return normed.reshape(values.shape) * gain
 
 
-def block_terms(values, inject, readout, step_sizes, rates, seg):
+def block_terms(values, inject, readout, step_sizes, cum_log, seg):
     length = values.shape[0]
     within = HEADS // GROUPS
-    cum_log = jnp.cumsum(-rates * step_sizes, axis=0)
     positions = jnp.arange(length)
     allowed = (positions[:, None] >= positions[None, :]) & (seg[:, None] == seg[None, :])
     spread = cum_log.T[:, :, None] - cum_log.T[:, None, :]
@@ -161,10 +160,6 @@
     inject = paired[:, :, 0]
     readout = paired[:, :, 1]
     step_sizes = jax.nn.softplus(dt_raw[0].astype(jnp.float32) + dt_bias[0])
-    local_out, states, cum_log, ending = block_terms(
-        values, inject, readout, step_sizes, decay_rate[0], my_seg
-    )
-
     kv = keys_values[0]
     lanes = 128
     share = tok_rows // devices
@@ -177,6 +172,7 @@
     first, cum_log = block_states(
         inputs, state_proj[0], dt_raw[0], dt_bias[0], decay_rate[0], my_seg, tail
     )
+    local_out = block_terms(values, inject, readout, step_sizes, cum_log, my_seg)[0]
     got = lax.all_to_all(first, "ctx", split_axis=0, concat_axis=0, tiled=True)
     got_kv = got[:, HEAD_DIM : HEAD_DIM + kv_rows]
     got_raw = got[:, HEAD_DIM + kv_rows].astype(jnp.float32)

time: 229 us -> 229 us (level)
  transfers between devices with their start and end apart: 4 -> 4, of which waited for: 4 -> 4; matrix products, arithmetic and copies ran while one was open for 18% -> 17% of each run, Pallas kernels for 0% -> 0%
where the time goes in v11:
time: 229 us
  waiting for transfers between devices  116 us (51%)
  local copies, waits for them, and re-layouts  40.9 us (18%)
  starting transfers between devices  26.5 us (12%)
  matrix products  20.5 us (9%)
  other arithmetic  16.3 us (7%)
  between operations  4.08 us (2%)
  Pallas kernels  4.05 us (2%)
    all_to_all x1, waiting for transfers between devices, on_device(): got = lax.all_to_all(first, 'ctx', split_axis=0, concat_axis=0, tiled=True)  62.5 us
    all_to_all x1, waiting for transfers between devices, on_device(): lax.all_to_all(second, 'ctx', split_axis=0, concat_axis=0, tiled=True)  45.7 us
    all_to_all x1, starting transfers between devices, on_device(): got = lax.all_to_all(first, 'ctx', split_axis=0, concat_axis=0, tiled=True)  18.6 us
    dot_general x1, matrix products, block_terms(): jnp.einsum('gktu,ugkp->tgkp', weights, scaled.reshape(length, GROUPS, wit...  9.57 us
    ppermute x2, waiting for transfers between devices, passed_along(): return lax.ppermute(value, axis, pairs)  8.13 us
    unnamed x55, local copies, waits for them, and re-layouts  7.42 us
    all_to_all x1, starting transfers between devices, on_device(): lax.all_to_all(second, 'ctx', split_axis=0, concat_axis=0, tiled=True)  6.23 us
  transfers between devices with their start and end apart: 4, of which 4 were waited for; matrix products, arithmetic and copies ran while one was open for 17% of the time, Pallas kernels for 0%

profile of v11, /device:TPU:6, one launch (start us, length us, event | category | flops | bytes accessed | tf_op | source)
XLA Modules:
  0.0 228.6 jit_solution(14532460491162529916)
XLA Ops:
  0.0 1.3 dynamic_slice.15
  3.3 1.4 copy.53
  4.8 0.7 copy.55
  5.5 0.8 slice.88
  7.1 0.7 broadcast_add_fusion.1
  7.9 0.6 dynamic_slice.19
  8.5 1.8 broadcast_compare_fusion.1
  10.8 0.7 copy.56.seg_ref
  11.5 1.0 reshape_squeeze.9
  12.6 0.8 maximum_maximum_fusion.tail_ref
  13.4 4.1 %shard_map.109 = (bf16[64,80,128]{2,1,0:T(8,128)(2,1)}, f32[128,64]{1,0:T(8,128)}) custom-call(bf16[128,4096]{1,0:T(8,128)(2,1)} %bitcast.210, bf16[128,2048]{1,0:T(8,128)(2,1)} %bitcast.229, bf16[128,64]{1,0:T(8,128)(2,1)} %bitcast.237, f32[1,64]{1,0:T(1,128)} %bias_ref.1, f32[1,64]{1,0:T(1,128)} %rate_ref.1, s32[128,1]{1,0:T(8,128)} %copy.56.seg_ref, ...), custom_call_target="tpu_custom_call" | custom-call | flops 268435456 | bytes 2883584 | tf_op jit(solution)/shard_map/pallas_call | solution.py:104
  17.5 18.6 %all-to-all-start = ((bf16[64,80,128]{2,1,0:T(8,128)(2,1)}), bf16[64,80,128]{2,1,0:T(8,128)(2,1)S(1)}, u32[]{:S(2)}, u32[]{:S(2)}) async-start(bf16[64,80,128]{2,1,0:T(8,128)(2,1)} %get-tuple-element.9), calls=%async_computation | async-start | bytes 2621440 | tf_op jit(solution)/shard_map/all_to_all | solution.py:176
  36.4 0.8 scatter_custom_fusion
  37.3 1.9 gather_fusion.3
  39.4 0.6 constant_dynamic-slice_fusion
  40.0 62.5 %all-to-all-done = bf16[64,80,128]{2,1,0:T(8,128)(2,1)S(1)} async-done(((bf16[64,80,128]{2,1,0:T(8,128)(2,1)}), bf16[64,80,128]{2,1,0:T(8,128)(2,1)S(1)}, u32[]{:S(2)}, u32[]{:S(2)}) %all-to-all-start) | async-done | bytes 1310752 | tf_op jit(solution)/shard_map/all_to_all | solution.py:176
  102.5 0.7 fusion.75
  103.2 0.7 fusion.74
  103.8 0.8 gather_fusion
  105.0 0.6 gather_fusion.1
  105.7 0.6 gather_fusion.2
  106.5 0.9 fusion.45
  107.4 1.0 fusion.37
  108.6 0.8 gather_fusion.4
  109.4 1.3 pad_maximum_fusion
  110.8 6.2 %all-to-all-start.1 = ((bf16[64,96,128]{2,1,0:T(8,128)(2,1)}), bf16[64,96,128]{2,1,0:T(8,128)(2,1)}, u32[]{:S(2)}, u32[]{:S(2)}) async-start(bf16[64,96,128]{2,1,0:T(8,128)(2,1)} %pad_maximum_fusion), calls=%async_computation.1 | async-start | bytes 3145728 | tf_op jit(solution)/shard_map/all_to_all | solution.py:205
  118.0 0.7 add.284
  118.7 0.8 concatenate.50
  119.6 1.0 copy.58
  121.1 0.6 broadcast.356
  121.7 0.7 reduce.13
  122.3 0.7 reduce.14
  123.0 0.7 add.250
  123.7 0.7 mul.187
  124.7 0.7 exponential_select_fusion
  125.5 1.5 mul.176
  126.9 2.9 %copy.67 = f32[128,4096]{1,0:T(8,128)} copy(f32[128,4096]{0,1:T(8,128)} %bitcast.219) | data formatting | bytes 4194304 | tf_op jit(solution)/shard_map/mul | solution.py:218
  130.1 1.3 fusion.64
  131.4 9.6 %fusion.5 = f32[8,8,64,128]{3,2,1,0:T(8,128)} fusion(f32[8,128,128]{2,1,0:T(8,128)S(1)} %fusion.64, f32[8,8,128]{2,1,0:T(8,128)S(1)} %bitcast.241, f32[128,8,8,64]{0,3,2,1:T(8,128)S(1)} %bitcast.213, pred[128,128]{1,0:T(8,128)(4,1)S(1)} %fusion.70, f32[128,8,8]{0,2,1:T(8,128)S(1)} %compare_select_fusion.3), kind=kOutput, calls=%fused_computation.17 | convolution fusion | flops 810024960 | bytes 4800512 | tf_op jit(solution)/shard_map/gktu,ugkp->tgkp/dot_general | solution.py:46
  141.0 2.9 %copy.68 = f32[128,4096]{1,0:T(8,128)} copy(f32[128,4096]{0,1:T(8,128)} %bitcast.215) | data formatting | bytes 4194304 | tf_op jit(solution)/shard_map/reshape | solution.py:51
  143.9 3.9 %gather_fusion.5 = s32[640]{0:T(1024)S(1)} fusion(s32[8192]{0:T(1024)S(1)} %bitcast.209, s32[1024]{0:T(1024)S(1)} %pad_clamp_fusion), kind=kCustom, calls=%fused_computation.5 | custom fusion | bytes 7680 | tf_op jit(solution)/shard_map/jit(_take)/gather | solution.py:230
  148.1 45.7 %all-to-all-done.1 = bf16[64,96,128]{2,1,0:T(8,128)(2,1)} async-done(((bf16[64,96,128]{2,1,0:T(8,128)(2,1)}), bf16[64,96,128]{2,1,0:T(8,128)(2,1)}, u32[]{:S(2)}, u32[]{:S(2)}) %all-to-all-start.1) | async-done | bytes 1572896 | tf_op jit(solution)/shard_map/all_to_all | solution.py:205
  193.7 1.2 slice.94
  195.0 0.9 copy.72
  195.9 1.3 slice.92
  197.2 1.9 multiply_reduce_fusion
  199.1 2.1 copy.66
  201.6 1.7 copy.88
  203.8 0.9 fusion.21
  204.9 0.9 copy-done.5
  205.8 1.3 fusion.11
  207.1 1.4 fusion.1
  208.6 1.7 multiply_reduce_fusion.2
  210.2 0.6 copy.75
  210.9 0.8 fusion.43
  211.8 1.3 fusion.12
  213.1 1.6 fusion.3
  214.7 1.6 multiply_reduce_fusion.1
  216.3 0.6 copy.77
  216.9 0.8 fusion.56
  217.7 1.7 collective-permute-start.1
  219.4 2.2 collective-permute-done
  221.6 6.0 %collective-permute-done.1 = bf16[1,64,4096]{2,1,0:T(8,128)(2,1)S(1)} collective-permute-done((bf16[1,64,4096]{2,1,0:T(8,128)(2,1)S(1)}, bf16[1,64,4096]{2,1,0:T(8,128)(2,1)S(1)}, u32[]{:S(2)}, u32[]{:S(2)}) %collective-permute-start.1) | collective-permute-done | bytes 524320 | tf_op jit(solution)/shard_map/ppermute | solution.py:27
  227.6 1.1 pad_maximum_fusion.1
  (99 shorter events, 5.0 us)
Async XLA Ops:
  10.3 0.5 copy-start.13
  11.5 24.6 %copy-start = (s32[1,8192]{1,0:T(1,128)S(1)}, s32[1,8192]{1,0:T(1,128)}, u32[]{:S(2)}) copy-start(s32[1,8192]{1,0:T(1,128)} %param.20) | copy-start | bytes 98308
  17.5 85.0 %all-to-all-start = ((bf16[64,80,128]{2,1,0:T(8,128)(2,1)}), bf16[64,80,128]{2,1,0:T(8,128)(2,1)S(1)}, u32[]{:S(2)}, u32[]{:S(2)}) async-start(bf16[64,80,128]{2,1,0:T(8,128)(2,1)} %get-tuple-element.9), calls=%async_computation | async-start | bytes 2621440 | tf_op jit(solution)/shard_map/all_to_all | solution.py:176
  37.2 2.1 copy-start.19
  37.2 2.1 copy-start.20
  109.4 10.0 %copy-start.8 = (bf16[1,128,512]{2,1,0:T(8,128)(2,1)S(1)}, bf16[1,128,512]{2,1,0:T(8,128)(2,1)}, u32[]{:S(2)}) copy-start(bf16[1,128,512]{2,1,0:T(8,128)(2,1)} %param.18) | copy-start | bytes 393220
  110.8 8.8 %copy-start.7 = (bf16[1,128,2048]{2,1,0:T(8,128)(2,1)S(1)}, bf16[1,128,2048]{2,1,0:T(8,128)(2,1)}, u32[]{:S(2)}) copy-start(bf16[1,128,2048]{2,1,0:T(8,128)(2,1)} %param.12) | copy-start | bytes 1572868
  110.8 9.8 %copy-start.1 = (bf16[1,128,4096]{2,1,0:T(8,128)(2,1)S(1)}, bf16[1,128,4096]{2,1,0:T(8,128)(2,1)}, u32[]{:S(2)}) copy-start(bf16[1,128,4096]{2,1,0:T(8,128)(2,1)} %param.11) | copy-start | bytes 3145732
  110.8 83.0 %all-to-all-start.1 = ((bf16[64,96,128]{2,1,0:T(8,128)(2,1)}), bf16[64,96,128]{2,1,0:T(8,128)(2,1)}, u32[]{:S(2)}, u32[]{:S(2)}) async-start(bf16[64,96,128]{2,1,0:T(8,128)(2,1)} %pad_maximum_fusion), calls=%async_computation.1 | async-start | bytes 3145728 | tf_op jit(solution)/shard_map/all_to_all | solution.py:205
  117.0 5.3 %copy-start.21 = (f32[1,64]{1,0:T(1,128)S(1)}, f32[1,64]{1,0:T(1,128)}, u32[]{:S(2)}) copy-start(f32[1,64]{1,0:T(1,128)} %param.16) | copy-start | bytes 772
  117.8 6.8 %copy-start.9 = (f32[128,64]{1,0:T(8,128)S(1)}, f32[128,64]{1,0:T(8,128)}, u32[]{:S(2)}) copy-start(f32[128,64]{1,0:T(8,128)} %get-tuple-element.8) | copy-start | bytes 98308
  126.9 2.9 %copy-start.14 = (s32[1,128]{1,0:T(1,128)S(1)}, s32[1,128]{1,0:T(1,128)}, u32[]{:S(2)}) copy-start(s32[1,128]{1,0:T(1,128)} %copy-done.13) | copy-start | bytes 1540
  126.9 3.0 %copy-start.10 = (bf16[1,128,64]{1,2,0:T(8,128)(2,1)S(1)}, bf16[1,128,64]{1,2,0:T(8,128)(2,1)}, u32[]{:S(2)}) copy-start(bf16[1,128,64]{1,2,0:T(8,128)(2,1)} %param.13) | copy-start | bytes 49156
  126.9 3.0 %copy-start.17 = (f32[8,8]{1,0:T(8,128)S(1)}, f32[8,8]{1,0:T(8,128)}, u32[]{:S(2)}) copy-start(f32[8,8]{1,0:T(8,128)} %add.250) | copy-start | bytes 772
  141.0 2.9 %copy-start.18 = (s32[512,1]{0,1:T(1,128)S(1)}, s32[512,1]{0,1:T(1,128)}, u32[]{:S(2)}) copy-start(s32[512,1]{0,1:T(1,128)} %concatenate.50) | copy-start | bytes 6148
  143.9 4.0 %copy-start.12 = (s32[512]{0:T(512)S(1)}, s32[512]{0:T(512)}, u32[]{:S(2)}) copy-start(s32[512]{0:T(512)} %add.284) | copy-start | bytes 6148
  147.8 49.4 %copy-start.16 = (f32[8,8]{1,0:T(8,128)S(1)}, f32[8,8]{1,0:T(8,128)}, u32[]{:S(2)}) copy-start(f32[8,8]{1,0:T(8,128)} %mul.187) | copy-start | bytes 772
  193.7 3.5 %copy-start.4 = (f32[8,8,64,128]{3,2,1,0:T(8,128)S(1)}, f32[8,8,64,128]{3,2,1,0:T(8,128)}, u32[]{:S(2)}) copy-start(f32[8,8,64,128]{3,2,1,0:T(8,128)} %fusion.5) | copy-start | bytes 6291460
  193.7 3.5 %copy-start.6 = (bf16[1,128,2048]{1,2,0:T(8,128)(2,1)S(1)}, bf16[1,128,2048]{1,2,0:T(8,128)(2,1)}, u32[]{:S(2)}) copy-start(bf16[1,128,2048]{1,2,0:T(8,128)(2,1)} %copy.58) | copy-start | bytes 1572868
  201.4 1.9 copy-start.15
  201.6 1.7 copy-start.2
  201.6 2.2 copy-start.3
  204.8 1.0 copy-start.5
  208.5 2.3 %copy-start.11 = (f32[1,4096]{1,0:T(1,128)S(1)}, f32[1,4096]{1,0:T(1,128)}, u32[]{:S(2)}) copy-start(f32[1,4096]{1,0:T(1,128)} %param.19) | copy-start | bytes 49156
  211.8 9.8 %collective-permute-start = (bf16[1,64,4096]{2,1,0:T(8,128)(2,1)S(1)}, bf16[1,64,4096]{2,1,0:T(8,128)(2,1)S(1)}, u32[]{:S(2)}, u32[]{:S(2)}) collective-permute-start(bf16[1,64,4096]{2,1,0:T(8,128)(2,1)S(1)} %bitcast.232), channel_id=1, source_target_pairs={{0,64},{64,128},{128,192},{192,256},{256,320},{320,384},{384,448},... | collective-permute-start | bytes 1572872 | tf_op jit(solution)/shard_map/ppermute | solution.py:27
  217.7 9.8 %collective-permute-start.1 = (bf16[1,64,4096]{2,1,0:T(8,128)(2,1)S(1)}, bf16[1,64,4096]{2,1,0:T(8,128)(2,1)S(1)}, u32[]{:S(2)}, u32[]{:S(2)}) collective-permute-start(bf16[1,64,4096]{2,1,0:T(8,128)(2,1)S(1)} %fusion.56), channel_id=1, source_target_pairs={{0,64},{64,128},{128,192},{192,256},{256,320},{320,384},{384,448},... | collective-permute-start | bytes 1572872 | tf_op jit(solution)/shard_map/ppermute | solution.py:27

commit v12 on v10

--- a/solution.py
+++ b/solution.py
@@ -188,12 +188,11 @@
     ending_pos = endings[inverse]
     running = jnp.cumsum(ending_pos)
     before = running - ending_pos
-    positions = jnp.arange(devices)
-    linked = (positions[None, :] < positions[:, None]) & (seg_end[None, :] == seg_prev[:, None])
-    factors = jnp.where(
-        linked, jnp.exp(jnp.minimum(before[:, None] - running[None, :], 0.0)), 0.0
-    )
-    by_device = factors[placement_perm][:, placement_perm]
+    at = placement_perm
+    linked = (at[None, :] < at[:, None]) & (seg_end[at][None, :] == seg_prev[at][:, None])
+    by_device = jnp.where(
+        linked, jnp.exp(jnp.minimum(before[at][:, None] - running[at][None, :], 0.0)), 0.0
+    )
     flat_states = got[:, :HEAD_DIM].reshape(devices, HEAD_DIM * STATE)
     high = by_device.astype(jnp.bfloat16)
     low = (by_device - high.astype(jnp.float32)).astype(jnp.bfloat16)

time: 229 us -> 229 us (level)
    unnamed x55 -> x57, local copies, waits for them, and re-layouts: 7.44 us -> 7.44 us
where the time goes in v12:
time: 229 us; the launch traced here: 228 us
  waiting for transfers between devices  114 us (50%)
  local copies, waits for them, and re-layouts  42.7 us (19%)
  starting transfers between devices  26.5 us (12%)
  matrix products  20.5 us (9%)
  other arithmetic  16.8 us (7%)
  Pallas kernels  4.04 us (2%)
  between operations  3.53 us (2%)
    all_to_all x1, waiting for transfers between devices, on_device(): got = lax.all_to_all(first, 'ctx', split_axis=0, concat_axis=0, tiled=True)  60.9 us
    all_to_all x1, waiting for transfers between devices, on_device(): lax.all_to_all(second, 'ctx', split_axis=0, concat_axis=0, tiled=True)  45.3 us
    all_to_all x1, starting transfers between devices, on_device(): got = lax.all_to_all(first, 'ctx', split_axis=0, concat_axis=0, tiled=True)  18.6 us
    dot_general x1, matrix products, block_terms(): jnp.einsum('gktu,ugkp->tgkp', weights, scaled.reshape(length, GROUPS, wit...  9.58 us
    ppermute x2, waiting for transfers between devices, passed_along(): return lax.ppermute(value, axis, pairs)  8.16 us
    unnamed x57, local copies, waits for them, and re-layouts  7.44 us
    all_to_all x1, starting transfers between devices, on_device(): lax.all_to_all(second, 'ctx', split_axis=0, concat_axis=0, tiled=True)  6.23 us
  transfers between devices with their start and end apart: 4, of which 4 were waited for; matrix products, arithmetic and copies ran while one was open for 18% of the time, Pallas kernels for 0%

profile of v12, /device:TPU:6, one launch (start us, length us, event | category | flops | bytes accessed | tf_op | source)
XLA Modules:
  0.0 228.5 jit_solution(7949003829603601335)
XLA Ops:
  0.0 1.2 dynamic_slice.15
  2.9 1.4 copy.77
  4.4 0.7 copy.85
  5.1 0.8 slice.92
  6.6 0.7 broadcast_add_fusion.1
  7.9 1.9 broadcast_compare_fusion.1
  10.4 0.7 copy.86.seg_ref
  11.1 1.0 reshape_squeeze.11
  12.2 0.8 maximum_maximum_fusion.tail_ref
  13.0 4.0 %shard_map.109 = (bf16[64,80,128]{2,1,0:T(8,128)(2,1)}, f32[128,64]{1,0:T(8,128)}) custom-call(bf16[128,4096]{1,0:T(8,128)(2,1)} %bitcast.196, bf16[128,2048]{1,0:T(8,128)(2,1)} %bitcast.215, bf16[128,64]{1,0:T(8,128)(2,1)} %bitcast.221, f32[1,64]{1,0:T(1,128)} %bias_ref.1, f32[1,64]{1,0:T(1,128)} %rate_ref.1, s32[128,1]{1,0:T(8,128)} %copy.86.seg_ref, ...), custom_call_target="tpu_custom_call" | custom-call | flops 268435456 | bytes 2883584 | tf_op jit(solution)/shard_map/pallas_call | solution.py:105
  17.1 18.6 %all-to-all-start = ((bf16[64,80,128]{2,1,0:T(8,128)(2,1)}), bf16[64,80,128]{2,1,0:T(8,128)(2,1)S(1)}, u32[]{:S(2)}, u32[]{:S(2)}) async-start(bf16[64,80,128]{2,1,0:T(8,128)(2,1)} %get-tuple-element.8), calls=%async_computation | async-start | bytes 2621440 | tf_op jit(solution)/shard_map/all_to_all | solution.py:180
  35.8 0.8 scatter_custom_fusion
  36.6 0.8 gather_fusion.1
  37.4 0.8 gather_fusion
  38.4 1.9 gather_fusion.5
  40.5 0.6 constant_dynamic-slice_fusion
  41.2 60.9 %all-to-all-done = bf16[64,80,128]{2,1,0:T(8,128)(2,1)S(1)} async-done(((bf16[64,80,128]{2,1,0:T(8,128)(2,1)}), bf16[64,80,128]{2,1,0:T(8,128)(2,1)S(1)}, u32[]{:S(2)}, u32[]{:S(2)}) %all-to-all-start) | async-done | bytes 1310752 | tf_op jit(solution)/shard_map/all_to_all | solution.py:180
  102.1 0.7 fusion.76
  102.8 0.8 fusion.75
  103.5 0.8 gather_fusion.2
  104.6 0.8 gather_fusion.4
  105.4 0.8 gather_fusion.3
  106.3 0.9 fusion.45
  107.2 1.0 fusion.37
  108.5 0.8 gather_fusion.6
  109.3 1.3 pad_maximum_fusion
  110.6 6.2 %all-to-all-start.1 = ((bf16[64,96,128]{2,1,0:T(8,128)(2,1)}), bf16[64,96,128]{2,1,0:T(8,128)(2,1)}, u32[]{:S(2)}, u32[]{:S(2)}) async-start(bf16[64,96,128]{2,1,0:T(8,128)(2,1)} %pad_maximum_fusion), calls=%async_computation.1 | async-start | bytes 3145728 | tf_op jit(solution)/shard_map/all_to_all | solution.py:208
  117.7 0.7 add.298
  118.5 0.7 concatenate.50
  119.3 1.0 copy.79
  121.4 0.6 reduce.13
  122.1 0.6 reduce.14
  122.7 0.7 add.260
  123.4 0.7 mul.200
  124.7 0.9 exponential_select_fusion
  125.7 1.5 mul.189
  127.1 2.9 %copy.90 = f32[128,4096]{1,0:T(8,128)} copy(f32[128,4096]{0,1:T(8,128)} %bitcast.205) | data formatting | bytes 4194304 | tf_op jit(solution)/shard_map/mul | solution.py:221
  130.3 1.3 fusion.64
  131.6 9.6 %fusion.5 = f32[8,8,64,128]{3,2,1,0:T(8,128)} fusion(f32[8,128,128]{2,1,0:T(8,128)S(1)} %fusion.64, f32[8,8,128]{2,1,0:T(8,128)S(1)} %bitcast.227, f32[128,8,8,64]{0,3,2,1:T(8,128)S(1)} %bitcast.199, pred[128,128]{1,0:T(8,128)(4,1)S(1)} %fusion.71, f32[128,8,8]{0,2,1:T(8,128)S(1)} %compare_select_fusion.4), kind=kOutput, calls=%fused_computation.19 | convolution fusion | flops 810024960 | bytes 4800512 | tf_op jit(solution)/shard_map/gktu,ugkp->tgkp/dot_general | solution.py:47
  141.2 2.9 %copy.91 = f32[128,4096]{1,0:T(8,128)} copy(f32[128,4096]{0,1:T(8,128)} %bitcast.201) | data formatting | bytes 4194304 | tf_op jit(solution)/shard_map/reshape | solution.py:52
  144.1 3.9 %gather_fusion.7 = s32[640]{0:T(1024)S(1)} fusion(s32[8192]{0:T(1024)S(1)} %bitcast.194, s32[1024]{0:T(1024)S(1)} %pad_clamp_fusion), kind=kCustom, calls=%fused_computation.7 | custom fusion | bytes 7680 | tf_op jit(solution)/shard_map/jit(_take)/gather | solution.py:233
  148.3 45.3 %all-to-all-done.1 = bf16[64,96,128]{2,1,0:T(8,128)(2,1)} async-done(((bf16[64,96,128]{2,1,0:T(8,128)(2,1)}), bf16[64,96,128]{2,1,0:T(8,128)(2,1)}, u32[]{:S(2)}, u32[]{:S(2)}) %all-to-all-start.1) | async-done | bytes 1572896 | tf_op jit(solution)/shard_map/all_to_all | solution.py:208
  193.6 1.2 slice.98
  194.9 0.9 copy.95
  195.7 1.3 slice.96
  197.1 1.9 multiply_reduce_fusion
  199.0 2.1 copy.89
  201.5 1.7 copy.111
  203.7 0.9 fusion.21
  204.8 0.9 copy-done.5
  205.7 1.3 fusion.11
  207.0 1.4 fusion.1
  208.4 1.7 multiply_reduce_fusion.2
  210.1 0.6 copy.98
  210.7 0.8 fusion.43
  211.7 1.3 fusion.12
  213.0 1.6 fusion.3
  214.6 1.6 multiply_reduce_fusion.1
  216.2 0.6 copy.100
  216.8 0.8 fusion.56
  217.6 1.7 collective-permute-start.1
  219.3 2.2 collective-permute-done
  221.5 6.0 %collective-permute-done.1 = bf16[1,64,4096]{2,1,0:T(8,128)(2,1)S(1)} collective-permute-done((bf16[1,64,4096]{2,1,0:T(8,128)(2,1)S(1)}, bf16[1,64,4096]{2,1,0:T(8,128)(2,1)S(1)}, u32[]{:S(2)}, u32[]{:S(2)}) %collective-permute-start.1) | collective-permute-done | bytes 524320 | tf_op jit(solution)/shard_map/ppermute | solution.py:27
  227.4 1.1 pad_maximum_fusion.1
  (104 shorter events, 6.3 us)
Async XLA Ops:
  9.8 0.5 copy-start.13
  11.1 24.6 %copy-start = (s32[1,8192]{1,0:T(1,128)S(1)}, s32[1,8192]{1,0:T(1,128)}, u32[]{:S(2)}) copy-start(s32[1,8192]{1,0:T(1,128)} %param.20) | copy-start | bytes 98308
  17.1 85.0 %all-to-all-start = ((bf16[64,80,128]{2,1,0:T(8,128)(2,1)}), bf16[64,80,128]{2,1,0:T(8,128)(2,1)S(1)}, u32[]{:S(2)}, u32[]{:S(2)}) async-start(bf16[64,80,128]{2,1,0:T(8,128)(2,1)} %get-tuple-element.8), calls=%async_computation | async-start | bytes 2621440 | tf_op jit(solution)/shard_map/all_to_all | solution.py:180
  38.4 2.1 copy-start.20
  38.4 2.1 copy-start.21
  40.3 66.0 %copy-start.18 = (s32[64]{0:T(128)S(1)}, s32[64]{0:T(128)}, u32[]{:S(2)}) copy-start(s32[64]{0:T(128)} %param.21) | copy-start | bytes 772
  109.3 9.9 %copy-start.8 = (bf16[1,128,512]{2,1,0:T(8,128)(2,1)S(1)}, bf16[1,128,512]{2,1,0:T(8,128)(2,1)}, u32[]{:S(2)}) copy-start(bf16[1,128,512]{2,1,0:T(8,128)(2,1)} %param.18) | copy-start | bytes 393220
  110.6 8.7 %copy-start.7 = (bf16[1,128,2048]{2,1,0:T(8,128)(2,1)S(1)}, bf16[1,128,2048]{2,1,0:T(8,128)(2,1)}, u32[]{:S(2)}) copy-start(bf16[1,128,2048]{2,1,0:T(8,128)(2,1)} %param.12) | copy-start | bytes 1572868
  110.6 9.7 %copy-start.1 = (bf16[1,128,4096]{2,1,0:T(8,128)(2,1)S(1)}, bf16[1,128,4096]{2,1,0:T(8,128)(2,1)}, u32[]{:S(2)}) copy-start(bf16[1,128,4096]{2,1,0:T(8,128)(2,1)} %param.11) | copy-start | bytes 3145732
  110.6 83.0 %all-to-all-start.1 = ((bf16[64,96,128]{2,1,0:T(8,128)(2,1)}), bf16[64,96,128]{2,1,0:T(8,128)(2,1)}, u32[]{:S(2)}, u32[]{:S(2)}) async-start(bf16[64,96,128]{2,1,0:T(8,128)(2,1)} %pad_maximum_fusion), calls=%async_computation.1 | async-start | bytes 3145728 | tf_op jit(solution)/shard_map/all_to_all | solution.py:208
  116.9 5.2 %copy-start.22 = (f32[1,64]{1,0:T(1,128)S(1)}, f32[1,64]{1,0:T(1,128)}, u32[]{:S(2)}) copy-start(f32[1,64]{1,0:T(1,128)} %param.16) | copy-start | bytes 772
  116.9 7.3 %copy-start.9 = (bf16[1,128,64]{2,1,0:T(8,128)(2,1)S(1)}, bf16[1,128,64]{2,1,0:T(8,128)(2,1)}, u32[]{:S(2)}) copy-start(bf16[1,128,64]{2,1,0:T(8,128)(2,1)} %copy.77) | copy-start | bytes 49156
  127.1 2.9 %copy-start.14 = (s32[1,128]{1,0:T(1,128)S(1)}, s32[1,128]{1,0:T(1,128)}, u32[]{:S(2)}) copy-start(s32[1,128]{1,0:T(1,128)} %copy-done.13) | copy-start | bytes 1540
  127.1 3.0 %copy-start.10 = (bf16[1,128,64]{1,2,0:T(8,128)(2,1)S(1)}, bf16[1,128,64]{1,2,0:T(8,128)(2,1)}, u32[]{:S(2)}) copy-start(bf16[1,128,64]{1,2,0:T(8,128)(2,1)} %param.13) | copy-start | bytes 49156
  127.1 3.0 %copy-start.17 = (f32[8,8]{1,0:T(8,128)S(1)}, f32[8,8]{1,0:T(8,128)}, u32[]{:S(2)}) copy-start(f32[8,8]{1,0:T(8,128)} %add.260) | copy-start | bytes 772
  141.2 2.9 %copy-start.19 = (s32[512,1]{0,1:T(1,128)S(1)}, s32[512,1]{0,1:T(1,128)}, u32[]{:S(2)}) copy-start(s32[512,1]{0,1:T(1,128)} %concatenate.50) | copy-start | bytes 6148
  144.1 4.0 %copy-start.12 = (s32[512]{0:T(512)S(1)}, s32[512]{0:T(512)}, u32[]{:S(2)}) copy-start(s32[512]{0:T(512)} %add.298) | copy-start | bytes 6148
  148.0 49.1 %copy-start.16 = (f32[8,8]{1,0:T(8,128)S(1)}, f32[8,8]{1,0:T(8,128)}, u32[]{:S(2)}) copy-start(f32[8,8]{1,0:T(8,128)} %mul.200) | copy-start | bytes 772
  193.6 3.4 %copy-start.4 = (f32[8,8,64,128]{3,2,1,0:T(8,128)S(1)}, f32[8,8,64,128]{3,2,1,0:T(8,128)}, u32[]{:S(2)}) copy-start(f32[8,8,64,128]{3,2,1,0:T(8,128)} %fusion.5) | copy-start | bytes 6291460
  193.6 3.4 %copy-start.6 = (bf16[1,128,2048]{1,2,0:T(8,128)(2,1)S(1)}, bf16[1,128,2048]{1,2,0:T(8,128)(2,1)}, u32[]{:S(2)}) copy-start(bf16[1,128,2048]{1,2,0:T(8,128)(2,1)} %copy.79) | copy-start | bytes 1572868
  201.3 1.9 copy-start.15
  201.5 1.7 copy-start.2
  201.5 2.2 copy-start.3
  204.6 1.0 copy-start.5
  208.4 2.3 %copy-start.11 = (f32[1,4096]{1,0:T(1,128)S(1)}, f32[1,4096]{1,0:T(1,128)}, u32[]{:S(2)}) copy-start(f32[1,4096]{1,0:T(1,128)} %param.19) | copy-start | bytes 49156
  211.6 9.8 %collective-permute-start = (bf16[1,64,4096]{2,1,0:T(8,128)(2,1)S(1)}, bf16[1,64,4096]{2,1,0:T(8,128)(2,1)S(1)}, u32[]{:S(2)}, u32[]{:S(2)}) collective-permute-start(bf16[1,64,4096]{2,1,0:T(8,128)(2,1)S(1)} %bitcast.218), channel_id=1, source_target_pairs={{0,64},{64,128},{128,192},{192,256},{256,320},{320,384},{384,448},... | collective-permute-start | bytes 1572872 | tf_op jit(solution)/shard_map/ppermute | solution.py:27
  217.6 9.8 %collective-permute-start.1 = (bf16[1,64,4096]{2,1,0:T(8,128)(2,1)S(1)}, bf16[1,64,4096]{2,1,0:T(8,128)(2,1)S(1)}, u32[]{:S(2)}, u32[]{:S(2)}) collective-permute-start(bf16[1,64,4096]{2,1,0:T(8,128)(2,1)S(1)} %fusion.56), channel_id=1, source_target_pairs={{0,64},{64,128},{128,192},{192,256},{256,320},{320,384},{384,448},... | collective-permute-start | bytes 1572872 | tf_op jit(solution)/shard_map/ppermute | solution.py:27
